TPU v7x, 32 devices: a whole 2x2x4 slice. The times are simulated.
32 devices in a mesh: grp: 8 (over y, x, core), sub: 4 (over z).
Axes of the slice: x: 2, y: 2, z: 4, core: 2. Of those that a mesh axis runs over, the one named last changes fastest.
Arguments:
- tokens: bfloat16 [128, 32, 256], P(('grp', 'sub')), may hold values from -64 to 64
- proj_weight: bfloat16 [256, 256], replicated, may hold values from -2 to 2
- match_grad: bfloat16 [4096, 1024], P(('grp', 'sub')), may hold values from -3072 to 3072
- edge_first: int32 [4096], P(('grp', 'sub')), may hold values from 0 to 15, as said below
- pair_second_image: int32 [4096], P(('grp', 'sub')), may hold values from 0 to 31, as said below
- send_pick: int32 [1024], P(('grp', 'sub')), may hold values from 0 to 3, as said below
Outputs:
- token_grad: bfloat16 [128, 32, 256], P(('grp', 'sub'))
Inputs may be any that keep to these rules, and one draw needn't show every extreme that they name: On each device the pairs (edge_first, pair_second_image) are distinct. `pair_second_image`: on each device every receive slot 0 to 31 is named by at least one pair. `send_pick`: for each device and each index p of grp, the 4 entries of its send slots p * 4 to p * 4 + 3 name different images.
All inputs are finite; a program needn't handle non-finite values.
Results may differ from a plain program's by a relative error of at most 0.017.
Values may be sent and summed in bfloat16 or wider, within the bound.
No kernel may reach another device: no remote copies, remote signals or barrier semaphores. Data moves between devices by JAX's collectives and lax.ppermute only.
A program may use at most 64 MiB of HBM per device.

v0:
```python
import jax
import jax.numpy as jnp
from jax import lax
from jax.sharding import PartitionSpec as P

EPSILON = 1e-05
SOFTMAX_COOLING = 0.1


def normalize(token_triple, proj_weight):
    image_count, length, feat_width = token_triple.shape
    feature = jnp.dot(
        token_triple.reshape(image_count * length, feat_width),
        proj_weight,
        preferred_element_type=jnp.float32,
    )
    inv_rms = lax.rsqrt(jnp.mean(feature * feature, axis=-1, keepdims=True) + EPSILON)
    normed = feature * inv_rms
    return (normed, inv_rms, normed.astype(jnp.bfloat16).reshape(image_count, length, feat_width))


def edge_terms(first_image_features, second_feats, match_block):
    score_scale = 1.0 / (first_image_features.shape[-1] * SOFTMAX_COOLING)
    scores = (
        jnp.einsum(
            "eid,ejd->eij", first_image_features, second_feats, preferred_element_type=jnp.float32
        )
        * score_scale
    )
    expo = jnp.exp(scores)
    rows = expo / jnp.sum(expo, axis=2, keepdims=True)
    cols = expo / jnp.sum(expo, axis=1, keepdims=True)
    incoming_gradient = match_block.astype(jnp.float32)
    d_rows = incoming_gradient * cols
    d_cols = incoming_gradient * rows
    d_scores = rows * (d_rows - jnp.sum(d_rows * rows, axis=2, keepdims=True)) + cols * (
        d_cols - jnp.sum(d_cols * cols, axis=1, keepdims=True)
    )
    d_scaled = (d_scores * score_scale).astype(jnp.bfloat16)
    grad_first = jnp.einsum(
        "eij,ejd->eid", d_scaled, second_feats, preferred_element_type=jnp.float32
    )
    grad_second = jnp.einsum(
        "eij,eid->ejd", d_scaled, first_image_features, preferred_element_type=jnp.float32
    )
    return (grad_first, grad_second)


def local(tokens, proj_weight, match_grad, edge_first, pair_second_image, send_pick):
    img_count, length, feat_width = tokens.shape
    normed, inv_rms, normed_b = normalize(tokens, proj_weight)
    raw_pool = lax.all_gather(tokens, "sub", axis=0, tiled=True)
    raw_received = lax.all_to_all(
        jnp.take(tokens, send_pick, axis=0), "grp", split_axis=0, concat_axis=0, tiled=True
    )
    pool = normalize(raw_pool, proj_weight)[2]
    received = normalize(raw_received, proj_weight)[2]
    pool_count = pool.shape[0]
    slot_count = received.shape[0]
    edge_count = edge_first.shape[0]
    grads = match_grad.reshape(edge_count, length, length)
    edge_block = 64

    def block_step(block_index, totals):
        pool_total, slot_total = totals
        block_start = block_index * edge_block
        first_images = lax.dynamic_slice_in_dim(edge_first, block_start, edge_block, 0)
        seconds = lax.dynamic_slice_in_dim(pair_second_image, block_start, edge_block, 0)
        block_grads = lax.dynamic_slice_in_dim(grads, block_start, edge_block, 0)
        grad_first, grad_second = edge_terms(
            jnp.take(pool, first_images, axis=0), jnp.take(received, seconds, axis=0), block_grads
        )
        pool_total = pool_total.at[first_images].add(grad_first)
        slot_total = slot_total.at[seconds].add(grad_second)
        return (pool_total, slot_total)

    start_totals = (
        jnp.zeros((pool_count, length, feat_width), jnp.float32),
        jnp.zeros((slot_count, length, feat_width), jnp.float32),
    )
    pool_total, slot_total = lax.fori_loop(0, edge_count // edge_block, block_step, start_totals)
    returned = lax.all_to_all(
        slot_total.astype(jnp.bfloat16), "grp", split_axis=0, concat_axis=0, tiled=True
    )
    owned = lax.psum_scatter(
        pool_total.astype(jnp.bfloat16), "sub", scatter_dimension=0, tiled=True
    ).astype(jnp.float32)
    pick_onehot = (jnp.arange(img_count, dtype=jnp.int32)[:, None] == send_pick[None, :]).astype(
        jnp.bfloat16
    )
    incoming_gradient = owned + jnp.einsum(
        "ir,rld->ild", pick_onehot, returned, preferred_element_type=jnp.float32
    )
    incoming_gradient = incoming_gradient.reshape(img_count * length, feat_width)
    feature_grad = (
        inv_rms
        * (
            incoming_gradient
            - normed * jnp.mean(incoming_gradient * normed, axis=-1, keepdims=True)
        )
    ).astype(jnp.bfloat16)
    token_grad = jnp.einsum(
        "nk,dk->nd", feature_grad, proj_weight, preferred_element_type=jnp.float32
    )
    return token_grad.astype(jnp.bfloat16).reshape(img_count, length, feat_width)


def solution(mesh):
    placed = (
        P(("grp", "sub"), None, None),
        P(),
        P(("grp", "sub"), None),
        P(("grp", "sub")),
        P(("grp", "sub")),
        P(("grp", "sub")),
    )
    return jax.shard_map(
        local, mesh=mesh, in_specs=placed, out_specs=P(("grp", "sub"), None, None), check_vma=False
    )
```

profile of v0, /device:TPU:0, one launch (start us, length us, event | category | flops | bytes accessed | tf_op | source)
XLA Modules:
  0.0 144.9 jit_solution(10182030258065522187)
XLA Ops:
  7.9 1.4 gather_fusion.2
  9.4 0.9 broadcast_select_fusion.6
  10.3 5.2 %all-to-all-start = ((bf16[32,32,256]{2,1,0:T(8,128)(2,1)}), bf16[32,32,256]{2,1,0:T(8,128)(2,1)S(1)}, u32[]{:S(2)}, u32[]{:S(2)}) async-start(bf16[32,32,256]{2,1,0:T(8,128)(2,1)} %broadcast_select_fusion.6), calls=%async_computation | async-start | bytes 1048576 | tf_op jit(solution)/shard_map/all_to_all | solution.py:53
  15.5 14.2 %all_gather.3 = bf16[16,32,256]{2,1,0:T(8,128)(2,1)S(1)} all-gather(bf16[4,32,256]{2,1,0:T(8,128)(2,1)S(1)} %copy-done.5), channel_id=1, replica_groups=mesh['grp'=8,'sub'=4] {'sub'}, dimensions={0}, use_global_device_ids=true | all-gather | bytes 327680 | tf_op jit(solution)/shard_map/all_gather | solution.py:52
  31.9 74.0 %while.15 = (s32[]{:T(128)}, f32[16,32,256]{2,1,0:T(8,128)S(1)}, f32[32,32,256]{2,1,0:T(8,128)S(1)}, s32[128]{0:T(128)S(1)}, bf16[16,32,256]{2,1,0:T(8,128)(2,1)...) while((s32[]{:T(128)}, f32[16,32,256]{2,1,0:T(8,128)S(1)}, ...), condition=%wide.region_10.11_spmd, body=%wide.region_3.10_spmd.sunk | while | flops 140456864 | bytes 40517248 | solution.py:81
  32.7 1.6 %gather_fusion = bf16[64,32,256]{2,1,0:T(8,128)(2,1)} fusion(bf16[16,32,256]{2,1,0:T(8,128)(2,1)S(1)} %get-tuple-element.284, s32[1024]{0:T(1024)S(1)} %pad_clamp_fusion.5), kind=kCustom, calls=%fused_computation.clone.1 | custom fusion | bytes 2097408 | tf_op jit(solution)/shard_map/while/body/eval_jaxpr/jit(_take)/gather | solution.py:71
  35.0 3.3 %fusion.59 = f32[64,32,32]{2,1,0:T(8,128)} fusion(bf16[64,32,256]{2,1,0:T(8,128)(2,1)} %gather_fusion, pred[64]{0:T(512)(128)(4,1)} %get-tuple-element.253, bf16[64,32,256]{2,1,0:T(8,128)(2,1)S(1)} %gather_fusion.1, pred[64]{0:T(512)(128)(4,1)S(1)} %get-tuple-element.255), kind=kOutput, calls=%fused_computation.9.clone.1 | convolution fusion | flops 34736160 | bytes 2359424 | tf_op jit(solution)/shard_map/while/body/eval_jaxpr/div | solution.py:31
  38.2 2.8 %fusion.58 = f32[64,32,32]{2,1,0:T(8,128)} fusion(bf16[64,32,256]{2,1,0:T(8,128)(2,1)} %gather_fusion, pred[64]{0:T(512)(128)(4,1)S(1)} %copy-done.8, bf16[64,32,256]{2,1,0:T(8,128)(2,1)S(1)} %gather_fusion.1, pred[64]{0:T(512)(128)(4,1)S(1)} %get-tuple-element.255), kind=kOutput, calls=%fused_computation.10.clone.1 | convolution fusion | flops 34736160 | bytes 2359424 | tf_op jit(solution)/shard_map/while/body/eval_jaxpr/div | solution.py:32
  42.0 2.5 %fusion.60 = f32[64,32,32]{2,1,0:T(8,128)S(1)} fusion(f32[64,32,32]{2,1,0:T(8,128)} %fusion.58, f32[64,32,32]{2,1,0:T(8,128)} %fusion.59, bf16[64,32,32]{2,1,0:T(8,128)(2,1)S(1)} %copy.34), kind=kOutput, calls=%fused_computation.16.clone.1 | output fusion | flops 460831 | bytes 917504 | tf_op jit(solution)/shard_map/while/body/eval_jaxpr/sub | solution.py:37
  44.5 5.0 %fusion.62 = f32[64,32,256]{2,1,0:T(8,128)} fusion(f32[64,32,32]{2,1,0:T(8,128)S(1)} %fusion.60, f32[64,32,32]{2,1,0:T(8,128)} %fusion.59, bf16[64,32,256]{2,1,0:T(8,128)(2,1)} %gather_fusion, pred[64]{0:T(512)(128)(4,1)S(1)} %copy-done.8, f32[64,32,32]{2,1,0:T(8,128)} %fusion.58, bf16[64,32,32]{2,1,0:T(8,128)(2,1)S(1)} %copy.34), kind=kOutput, calls=%fused_computation.28.clone.1 | convolution fusion | flops 34736160 | bytes 4063296 | tf_op jit(solution)/shard_map/while/body/eval_jaxpr/eij,eid->ejd/dot_general | solution.py:43
  49.5 7.0 %scatter_fusion.1 = f32[32,32,256]{2,1,0:T(8,128)S(1)} fusion(f32[32,32,256]{2,1,0:T(8,128)S(1)} %get-tuple-element.270, s32[64]{0:T(128)S(1)} %get-tuple-element.254, f32[64,32,256]{2,1,0:T(8,128)} %fusion.62), kind=kCustom, calls=%fused_computation.4.clone.1 | custom fusion | flops 524288 | bytes 6291712 | tf_op jit(solution)/shard_map/while/body/eval_jaxpr/scatter-add | solution.py:74
  56.6 5.3 %fusion.61 = f32[64,32,256]{2,1,0:T(8,128)} fusion(f32[64,32,32]{2,1,0:T(8,128)S(1)} %fusion.60, f32[64,32,32]{2,1,0:T(8,128)} %fusion.59, bf16[64,32,256]{2,1,0:T(8,128)(2,1)} %copy-done.1, pred[64]{0:T(512)(128)(4,1)S(1)} %get-tuple-element.255, f32[64,32,32]{2,1,0:T(8,128)} %fusion.58, bf16[64,32,32]{2,1,0:T(8,128)(2,1)S(1)} %copy.34), kind=kOutput, calls=%fused_computation.29.clone.1 | convolution fusion | flops 34736160 | bytes 4063296 | tf_op jit(solution)/shard_map/while/body/eval_jaxpr/eij,ejd->eid/dot_general | solution.py:40
  61.9 7.0 %scatter_fusion = f32[16,32,256]{2,1,0:T(8,128)S(1)} fusion(f32[16,32,256]{2,1,0:T(8,128)S(1)} %get-tuple-element.269, s32[64]{0:T(128)S(1)} %get-tuple-element.252, f32[64,32,256]{2,1,0:T(8,128)} %fusion.61), kind=kCustom, calls=%fused_computation.3.clone.1 | custom fusion | flops 524288 | bytes 6291712 | tf_op jit(solution)/shard_map/while/body/eval_jaxpr/scatter-add | solution.py:73
  69.7 1.6 %gather_fusion = bf16[64,32,256]{2,1,0:T(8,128)(2,1)} fusion(bf16[16,32,256]{2,1,0:T(8,128)(2,1)S(1)} %get-tuple-element.284, s32[1024]{0:T(1024)S(1)} %pad_clamp_fusion.5), kind=kCustom, calls=%fused_computation.clone.1 | custom fusion | bytes 2097408 | tf_op jit(solution)/shard_map/while/body/eval_jaxpr/jit(_take)/gather | solution.py:71
  71.9 3.2 %fusion.59 = f32[64,32,32]{2,1,0:T(8,128)} fusion(bf16[64,32,256]{2,1,0:T(8,128)(2,1)} %gather_fusion, pred[64]{0:T(512)(128)(4,1)} %get-tuple-element.253, bf16[64,32,256]{2,1,0:T(8,128)(2,1)S(1)} %gather_fusion.1, pred[64]{0:T(512)(128)(4,1)S(1)} %get-tuple-element.255), kind=kOutput, calls=%fused_computation.9.clone.1 | convolution fusion | flops 34736160 | bytes 2359424 | tf_op jit(solution)/shard_map/while/body/eval_jaxpr/div | solution.py:31
  75.2 2.8 %fusion.58 = f32[64,32,32]{2,1,0:T(8,128)} fusion(bf16[64,32,256]{2,1,0:T(8,128)(2,1)} %gather_fusion, pred[64]{0:T(512)(128)(4,1)S(1)} %copy-done.8, bf16[64,32,256]{2,1,0:T(8,128)(2,1)S(1)} %gather_fusion.1, pred[64]{0:T(512)(128)(4,1)S(1)} %get-tuple-element.255), kind=kOutput, calls=%fused_computation.10.clone.1 | convolution fusion | flops 34736160 | bytes 2359424 | tf_op jit(solution)/shard_map/while/body/eval_jaxpr/div | solution.py:32
  79.0 2.5 %fusion.60 = f32[64,32,32]{2,1,0:T(8,128)S(1)} fusion(f32[64,32,32]{2,1,0:T(8,128)} %fusion.58, f32[64,32,32]{2,1,0:T(8,128)} %fusion.59, bf16[64,32,32]{2,1,0:T(8,128)(2,1)S(1)} %copy.34), kind=kOutput, calls=%fused_computation.16.clone.1 | output fusion | flops 460831 | bytes 917504 | tf_op jit(solution)/shard_map/while/body/eval_jaxpr/sub | solution.py:37
  81.5 5.0 %fusion.62 = f32[64,32,256]{2,1,0:T(8,128)} fusion(f32[64,32,32]{2,1,0:T(8,128)S(1)} %fusion.60, f32[64,32,32]{2,1,0:T(8,128)} %fusion.59, bf16[64,32,256]{2,1,0:T(8,128)(2,1)} %gather_fusion, pred[64]{0:T(512)(128)(4,1)S(1)} %copy-done.8, f32[64,32,32]{2,1,0:T(8,128)} %fusion.58, bf16[64,32,32]{2,1,0:T(8,128)(2,1)S(1)} %copy.34), kind=kOutput, calls=%fused_computation.28.clone.1 | convolution fusion | flops 34736160 | bytes 4063296 | tf_op jit(solution)/shard_map/while/body/eval_jaxpr/eij,eid->ejd/dot_general | solution.py:43
  86.5 7.0 %scatter_fusion.1 = f32[32,32,256]{2,1,0:T(8,128)S(1)} fusion(f32[32,32,256]{2,1,0:T(8,128)S(1)} %get-tuple-element.270, s32[64]{0:T(128)S(1)} %get-tuple-element.254, f32[64,32,256]{2,1,0:T(8,128)} %fusion.62), kind=kCustom, calls=%fused_computation.4.clone.1 | custom fusion | flops 524288 | bytes 6291712 | tf_op jit(solution)/shard_map/while/body/eval_jaxpr/scatter-add | solution.py:74
  93.6 5.3 %fusion.61 = f32[64,32,256]{2,1,0:T(8,128)} fusion(f32[64,32,32]{2,1,0:T(8,128)S(1)} %fusion.60, f32[64,32,32]{2,1,0:T(8,128)} %fusion.59, bf16[64,32,256]{2,1,0:T(8,128)(2,1)} %copy-done.1, pred[64]{0:T(512)(128)(4,1)S(1)} %get-tuple-element.255, f32[64,32,32]{2,1,0:T(8,128)} %fusion.58, bf16[64,32,32]{2,1,0:T(8,128)(2,1)S(1)} %copy.34), kind=kOutput, calls=%fused_computation.29.clone.1 | convolution fusion | flops 34736160 | bytes 4063296 | tf_op jit(solution)/shard_map/while/body/eval_jaxpr/eij,ejd->eid/dot_general | solution.py:40
  98.9 7.0 %scatter_fusion = f32[16,32,256]{2,1,0:T(8,128)S(1)} fusion(f32[16,32,256]{2,1,0:T(8,128)S(1)} %get-tuple-element.269, s32[64]{0:T(128)S(1)} %get-tuple-element.252, f32[64,32,256]{2,1,0:T(8,128)} %fusion.61), kind=kCustom, calls=%fused_computation.3.clone.1 | custom fusion | flops 524288 | bytes 6291712 | tf_op jit(solution)/shard_map/while/body/eval_jaxpr/scatter-add | solution.py:73
  106.8 4.0 %all-to-all-start.1 = ((bf16[32,32,256]{2,1,0:T(8,128)(2,1)}), bf16[32,32,256]{2,1,0:T(8,128)(2,1)S(1)}, u32[]{:S(2)}, u32[]{:S(2)}) async-start(bf16[32,32,256]{2,1,0:T(8,128)(2,1)} %convert_element_type.40), calls=%async_computation.2 | async-start | bytes 1048576 | tf_op jit(solution)/shard_map/all_to_all | solution.py:82
  112.0 8.6 %all-to-all-done.1 = bf16[32,32,256]{2,1,0:T(8,128)(2,1)S(1)} async-done(((bf16[32,32,256]{2,1,0:T(8,128)(2,1)}), bf16[32,32,256]{2,1,0:T(8,128)(2,1)S(1)}, u32[]{:S(2)}, u32[]{:S(2)}) %all-to-all-start.1) | async-done | bytes 524320 | tf_op jit(solution)/shard_map/all_to_all | solution.py:82
  121.0 15.0 %reduce-scatter.2.cloned.1.call-done = bf16[4,32,256]{2,1,0:T(8,128)(2,1)} async-done(((bf16[16,32,256]{2,1,0:T(8,128)(2,1)}), bf16[4,32,256]{2,1,0:T(8,128)(2,1)}) %reduce-scatter.2.cloned.1.call-update) | async-done | bytes 65552 | tf_op jit(solution)/shard_map/reduce_scatter | solution.py:85
  (79 shorter events, 12.4 us)
Async XLA Ops:
  6.5 24.0 %copy-start = (bf16[256,256]{1,0:T(8,128)(2,1)S(1)}, bf16[256,256]{1,0:T(8,128)(2,1)}, u32[]{:S(2)}) copy-start(bf16[256,256]{1,0:T(8,128)(2,1)} %param.9) | copy-start | bytes 393220
  6.5 8.9 %copy-start.5 = (bf16[4,32,256]{2,1,0:T(8,128)(2,1)S(1)}, bf16[4,32,256]{2,1,0:T(8,128)(2,1)}, u32[]{:S(2)}) copy-start(bf16[4,32,256]{2,1,0:T(8,128)(2,1)} %param.8) | copy-start | bytes 196612
  6.5 23.2 %copy-start.7 = (bf16[128,1024]{1,0:T(8,128)(2,1)S(1)}, bf16[128,1024]{1,0:T(8,128)(2,1)}, u32[]{:S(2)}) copy-start(bf16[128,1024]{1,0:T(8,128)(2,1)} %param.10) | copy-start | bytes 786436
  10.3 20.8 %all-to-all-start = ((bf16[32,32,256]{2,1,0:T(8,128)(2,1)}), bf16[32,32,256]{2,1,0:T(8,128)(2,1)S(1)}, u32[]{:S(2)}, u32[]{:S(2)}) async-start(bf16[32,32,256]{2,1,0:T(8,128)(2,1)} %broadcast_select_fusion.6), calls=%async_computation | async-start | bytes 1048576 | tf_op jit(solution)/shard_map/all_to_all | solution.py:53
  31.1 0.8 copy-start.9
  31.1 0.8 copy-start.11
  32.0 3.0 %copy-start.2 = (bf16[32,32,256]{2,1,0:T(8,128)(2,1)}, bf16[32,32,256]{2,1,0:T(8,128)(2,1)S(1)}, u32[]{:S(2)}) copy-start(bf16[32,32,256]{2,1,0:T(8,128)(2,1)S(1)} %get-tuple-element.286) | copy-start | bytes 1572868 | tf_op jit(solution)/shard_map/while
  34.9 3.3 %copy-start.1 = (bf16[64,32,256]{2,1,0:T(8,128)(2,1)}, bf16[64,32,256]{2,1,0:T(8,128)(2,1)S(1)}, u32[]{:S(2)}) copy-start(bf16[64,32,256]{2,1,0:T(8,128)(2,1)S(1)} %gather_fusion.1) | copy-start | bytes 3145732 | tf_op jit(solution)/shard_map/while
  35.0 3.3 %copy-start.8 = (pred[64]{0:T(512)(128)(4,1)S(1)}, pred[64]{0:T(512)(128)(4,1)}, u32[]{:S(2)}) copy-start(pred[64]{0:T(512)(128)(4,1)} %get-tuple-element.253) | copy-start | bytes 196 | tf_op jit(solution)/shard_map/while
  38.2 2.9 %copy-start.4 = (bf16[128,32,32]{0,2,1:T(8,128)(2,1)S(1)}, bf16[128,32,32]{0,2,1:T(8,128)(2,1)}, u32[]{:S(2)}) copy-start(bf16[128,32,32]{0,2,1:T(8,128)(2,1)} %get-tuple-element.287) | copy-start | bytes 786436 | tf_op jit(solution)/shard_map/while
  61.9 7.0 %copy-start.3 = (bf16[32,32,256]{2,1,0:T(8,128)(2,1)S(1)}, bf16[32,32,256]{2,1,0:T(8,128)(2,1)}, u32[]{:S(2)}) copy-start(bf16[32,32,256]{2,1,0:T(8,128)(2,1)} %copy-done.2) | copy-start | bytes 1572868 | tf_op jit(solution)/shard_map/while
  61.9 7.0 %copy-start.10 = (s32[128]{0:T(128)S(1)}, s32[128]{0:T(128)}, u32[]{:S(2)}) copy-start(s32[128]{0:T(128)} %get-tuple-element.310) | copy-start | bytes 1540 | tf_op jit(solution)/shard_map/while
  61.9 7.1 %copy-start.12 = (s32[128]{0:T(128)S(1)}, s32[128]{0:T(128)}, u32[]{:S(2)}) copy-start(s32[128]{0:T(128)} %get-tuple-element.324) | copy-start | bytes 1540 | tf_op jit(solution)/shard_map/while
  68.9 3.0 %copy-start.2 = (bf16[32,32,256]{2,1,0:T(8,128)(2,1)}, bf16[32,32,256]{2,1,0:T(8,128)(2,1)S(1)}, u32[]{:S(2)}) copy-start(bf16[32,32,256]{2,1,0:T(8,128)(2,1)S(1)} %get-tuple-element.286) | copy-start | bytes 1572868 | tf_op jit(solution)/shard_map/while
  71.9 3.3 %copy-start.1 = (bf16[64,32,256]{2,1,0:T(8,128)(2,1)}, bf16[64,32,256]{2,1,0:T(8,128)(2,1)S(1)}, u32[]{:S(2)}) copy-start(bf16[64,32,256]{2,1,0:T(8,128)(2,1)S(1)} %gather_fusion.1) | copy-start | bytes 3145732 | tf_op jit(solution)/shard_map/while
  71.9 3.3 %copy-start.8 = (pred[64]{0:T(512)(128)(4,1)S(1)}, pred[64]{0:T(512)(128)(4,1)}, u32[]{:S(2)}) copy-start(pred[64]{0:T(512)(128)(4,1)} %get-tuple-element.253) | copy-start | bytes 196 | tf_op jit(solution)/shard_map/while
  75.2 2.9 %copy-start.4 = (bf16[128,32,32]{0,2,1:T(8,128)(2,1)S(1)}, bf16[128,32,32]{0,2,1:T(8,128)(2,1)}, u32[]{:S(2)}) copy-start(bf16[128,32,32]{0,2,1:T(8,128)(2,1)} %get-tuple-element.287) | copy-start | bytes 786436 | tf_op jit(solution)/shard_map/while
  98.9 7.0 %copy-start.3 = (bf16[32,32,256]{2,1,0:T(8,128)(2,1)S(1)}, bf16[32,32,256]{2,1,0:T(8,128)(2,1)}, u32[]{:S(2)}) copy-start(bf16[32,32,256]{2,1,0:T(8,128)(2,1)} %copy-done.2) | copy-start | bytes 1572868 | tf_op jit(solution)/shard_map/while
  98.9 7.0 %copy-start.10 = (s32[128]{0:T(128)S(1)}, s32[128]{0:T(128)}, u32[]{:S(2)}) copy-start(s32[128]{0:T(128)} %get-tuple-element.310) | copy-start | bytes 1540 | tf_op jit(solution)/shard_map/while
  98.9 7.1 %copy-start.12 = (s32[128]{0:T(128)S(1)}, s32[128]{0:T(128)}, u32[]{:S(2)}) copy-start(s32[128]{0:T(128)} %get-tuple-element.324) | copy-start | bytes 1540 | tf_op jit(solution)/shard_map/while
  105.9 5.8 %copy-start.6 = (bf16[4,32,256]{2,1,0:T(8,128)(2,1)S(1)}, bf16[4,32,256]{2,1,0:T(8,128)(2,1)}, u32[]{:S(2)}) copy-start(bf16[4,32,256]{2,1,0:T(8,128)(2,1)} %param.8) | copy-start | bytes 196612
  106.0 14.6 %copy-start.13 = (s32[32]{0:T(128)S(1)}, s32[32]{0:T(128)}, u32[]{:S(2)}) copy-start(s32[32]{0:T(128)} %param.13) | copy-start | bytes 388
  106.8 13.8 %all-to-all-start.1 = ((bf16[32,32,256]{2,1,0:T(8,128)(2,1)}), bf16[32,32,256]{2,1,0:T(8,128)(2,1)S(1)}, u32[]{:S(2)}, u32[]{:S(2)}) async-start(bf16[32,32,256]{2,1,0:T(8,128)(2,1)} %convert_element_type.40), calls=%async_computation.2 | async-start | bytes 1048576 | tf_op jit(solution)/shard_map/all_to_all | solution.py:82
  110.9 25.1 %reduce-scatter.2.cloned.1.call-start = ((), (), s32[]{:S(2)}) async-start(), calls=%async_computation.3 | async-start | bytes 327680 | tf_op jit(solution)/shard_map/reduce_scatter | solution.py:85
Sparse Core Ops, SparseCore 0:
  113.9 22.0 reduce-scatter.1
where the time goes:
time: 146 us; the launch traced here: 145 us
  other arithmetic  40 us (27%)
  matrix products  35 us (24%)
  waiting for transfers between devices  23.7 us (16%)
  blocking collectives  14.2 us (10%)
  between operations  13.6 us (9%)
  starting transfers between devices  9.28 us (6%)
  local copies, waits for them, and re-layouts  8.82 us (6%)
    reduce_scatter x1, waiting for transfers between devices, local(): lax.psum_scatter(pool_total.astype(jnp.bfloat16), 'sub', scatter_dimensio...  15 us
    all_gather x1, blocking collectives, local(): raw_pool = lax.all_gather(tokens, 'sub', axis=0, tiled=True)  14.2 us
    scatter-add x2, other arithmetic, block_step(): slot_total = slot_total.at[seconds].add(grad_second)  14.1 us
    scatter-add x2, other arithmetic, block_step(): pool_total = pool_total.at[first_images].add(grad_first)  14 us
    dot_general x2, matrix products, edge_terms(): jnp.einsum('eij,ejd->eid', d_scaled, second_feats, preferred_element_type...  10.6 us
    dot_general x2, matrix products, edge_terms(): jnp.einsum('eij,eid->ejd', d_scaled, first_image_features, preferred_elem...  10 us
    all_to_all x1, waiting for transfers between devices, local(): lax.all_to_all(slot_total.astype(jnp.bfloat16), 'grp', split_axis=0, conc...  8.62 us
    div x2, matrix products, edge_terms(): rows = expo / jnp.sum(expo, axis=2, keepdims=True)  6.5 us
  transfers between devices with their start and end apart: 3, of which 2 were waited for; matrix products, arithmetic and copies ran while one was open for 2% of the time, Pallas kernels for 0%

commit v1 on v0

v1 whole, which is shorter than its diff:
```python
import jax
import jax.numpy as jnp
from jax import lax
from jax.sharding import PartitionSpec as P

EPSILON = 1e-05
SOFTMAX_COOLING = 0.1
SUB_MODE = "perm"
GRP_MODE = "perm"
CHUNK_ELEMS = 1 << 19


def normalize(tokens, proj_weight):
    image_count, length, feat_width = tokens.shape
    feature = jnp.dot(
        tokens.reshape(image_count * length, feat_width),
        proj_weight,
        preferred_element_type=jnp.float32,
    )
    inv_rms = lax.rsqrt(jnp.mean(feature * feature, axis=-1, keepdims=True) + EPSILON)
    normed = feature * inv_rms
    return (normed, inv_rms, normed.astype(jnp.bfloat16).reshape(image_count, length, feat_width))


def shift(count, step):
    return [(i, (i + step) % count) for i in range(count)]


def dense_terms(pool_c, received, grads_c):
    score_scale = 1.0 / (pool_c.shape[-1] * SOFTMAX_COOLING)
    scores = (
        jnp.einsum("ird,jcd->ijrc", pool_c, received, preferred_element_type=jnp.float32)
        * score_scale
    )
    expo = jnp.exp(scores)
    rows = expo / jnp.sum(expo, axis=3, keepdims=True)
    cols = expo / jnp.sum(expo, axis=2, keepdims=True)
    d_rows = grads_c * cols
    d_cols = grads_c * rows
    d_scores = rows * (d_rows - jnp.sum(d_rows * rows, axis=3, keepdims=True)) + cols * (
        d_cols - jnp.sum(d_cols * cols, axis=2, keepdims=True)
    )
    d_scaled = (d_scores * score_scale).astype(jnp.bfloat16)
    pool_part = jnp.einsum("ijrc,jcd->ird", d_scaled, received, preferred_element_type=jnp.float32)
    slot_part = jnp.einsum("ijrc,ird->jcd", d_scaled, pool_c, preferred_element_type=jnp.float32)
    return pool_part, slot_part


def local(n_grp, n_sub, tokens, proj_weight, match_grad, edge_first, pair_second_image, send_pick):
    img_count, length, feat_width = tokens.shape
    recv = send_pick.shape[0]
    slots = recv // n_grp
    group_img = img_count * n_sub
    edge_count = edge_first.shape[0]
    grp_at = lax.axis_index("grp")
    sub_at = lax.axis_index("sub")

    normed, inv_rms, normed_b = normalize(tokens, proj_weight)

    if SUB_MODE == "perm":
        pool = jnp.concatenate(
            [normed_b] + [lax.ppermute(normed_b, "sub", shift(n_sub, k)) for k in range(1, n_sub)],
            axis=0,
        )
        first_at = ((sub_at - edge_first // img_count) % n_sub) * img_count + edge_first % img_count
    else:
        pool = lax.all_gather(normed_b, "sub", axis=0, tiled=True)
        first_at = edge_first

    picks = send_pick.reshape(n_grp, slots)
    flat_b = normed_b.reshape(img_count, length * feat_width)
    if GRP_MODE == "perm":
        order = picks[(grp_at + jnp.arange(n_grp, dtype=jnp.int32)) % n_grp].reshape(recv)
    else:
        order = send_pick
    pick_onehot = (order[:, None] == jnp.arange(img_count, dtype=jnp.int32)[None, :]).astype(
        jnp.bfloat16
    )
    outgoing = jnp.dot(pick_onehot, flat_b, preferred_element_type=jnp.float32).astype(jnp.bfloat16)
    outgoing = outgoing.reshape(recv, length, feat_width)
    if GRP_MODE == "perm":
        received = jnp.concatenate(
            [outgoing[:slots]]
            + [
                lax.ppermute(outgoing[k * slots : (k + 1) * slots], "grp", shift(n_grp, k))
                for k in range(1, n_grp)
            ],
            axis=0,
        )
        second_at = ((grp_at - pair_second_image // slots) % n_grp) * slots + pair_second_image % slots
    else:
        received = lax.all_to_all(outgoing, "grp", split_axis=0, concat_axis=0, tiled=True)
        second_at = pair_second_image

    pair_at = first_at * recv + second_at
    chunk = group_img
    while chunk > 1 and (chunk * recv * length * length > CHUNK_ELEMS or group_img % chunk):
        chunk -= 1
    n_chunks = group_img // chunk

    def one_chunk(chunk_index):
        base = chunk_index * (chunk * recv)
        scatter = (
            lax.broadcasted_iota(jnp.int32, (chunk * recv, edge_count), 0) + base == pair_at[None, :]
        ).astype(jnp.bfloat16)
        grads_c = jnp.dot(scatter, match_grad, preferred_element_type=jnp.float32).reshape(
            chunk, recv, length, length
        )
        pool_c = lax.dynamic_slice_in_dim(pool, chunk_index * chunk, chunk, 0)
        return dense_terms(pool_c, received, grads_c)

    if n_chunks == 1:
        pool_total, slot_total = one_chunk(0)
    else:

        def body(carry, chunk_index):
            pool_part, slot_part = one_chunk(chunk_index)
            return carry + slot_part, pool_part.astype(jnp.bfloat16)

        slot_total, pool_parts = lax.scan(
            body,
            jnp.zeros((recv, length, feat_width), jnp.float32),
            jnp.arange(n_chunks, dtype=jnp.int32),
        )
        pool_total = pool_parts.reshape(group_img, length, feat_width)
    pool_b = pool_total.astype(jnp.bfloat16)
    slot_b = slot_total.astype(jnp.bfloat16)

    if SUB_MODE == "perm":
        owned = pool_b[:img_count].astype(jnp.float32)
        for k in range(1, n_sub):
            owned = owned + lax.ppermute(
                pool_b[k * img_count : (k + 1) * img_count], "sub", shift(n_sub, -k)
            ).astype(jnp.float32)
    else:
        owned = lax.psum_scatter(pool_b, "sub", scatter_dimension=0, tiled=True).astype(jnp.float32)

    if GRP_MODE == "perm":
        returned = jnp.concatenate(
            [slot_b[:slots]]
            + [
                lax.ppermute(slot_b[k * slots : (k + 1) * slots], "grp", shift(n_grp, -k))
                for k in range(1, n_grp)
            ],
            axis=0,
        )
    else:
        returned = lax.all_to_all(slot_b, "grp", split_axis=0, concat_axis=0, tiled=True)
    incoming_gradient = owned.reshape(img_count, length * feat_width) + jnp.dot(
        pick_onehot.T, returned.reshape(recv, length * feat_width), preferred_element_type=jnp.float32
    )
    incoming_gradient = incoming_gradient.reshape(img_count * length, feat_width)
    feature_grad = (
        inv_rms
        * (
            incoming_gradient
            - normed * jnp.mean(incoming_gradient * normed, axis=-1, keepdims=True)
        )
    ).astype(jnp.bfloat16)
    token_grad = jnp.einsum(
        "nk,dk->nd", feature_grad, proj_weight, preferred_element_type=jnp.float32
    )
    return token_grad.astype(jnp.bfloat16).reshape(img_count, length, feat_width)


def solution(mesh):
    placed = (
        P(("grp", "sub"), None, None),
        P(),
        P(("grp", "sub"), None),
        P(("grp", "sub")),
        P(("grp", "sub")),
        P(("grp", "sub")),
    )
    n_grp = mesh.shape["grp"]
    n_sub = mesh.shape["sub"]

    def run(*args):
        return local(n_grp, n_sub, *args)

    return jax.shard_map(
        run, mesh=mesh, in_specs=placed, out_specs=P(("grp", "sub"), None, None), check_vma=False
    )
```

time: 146 us -> 126 us (0.86)
  other arithmetic: 40 us -> 13.7 us
  starting transfers between devices: 9.28 us -> 27.9 us
  matrix products: 35 us -> 53.4 us
  blocking collectives: 14.2 us -> 0 us
  between operations: 13.6 us -> 0.35 us
  waiting for transfers between devices: 23.7 us -> 11.5 us
  local copies, waits for them, and re-layouts: 8.82 us -> 16.8 us
    scatter-add x4 -> x0, other arithmetic: 28.1 us -> none  [the longest x2 14.1 us: block_step(): slot_total = slot_total.at[seconds].add(grad_second)]
    ppermute x0 -> x20, starting transfers between devices: none -> 27.9 us  [the longest x7 10.5 us: local(): lax.ppermute(outgoing[k * slots:(k + 1) * slots], 'grp', shift(n_grp, k))]
    dot_general x8 -> x6, matrix products: 22 us -> 43.1 us  [the longest x1 20.5 us: dense_terms(): jnp.einsum('ijrc,ird->jcd', d_scaled, pool_c, preferred_element_type=jnp....]
    reduce_scatter x1 -> x0, waiting for transfers between devices: 15 us -> none  [local(): lax.psum_scatter(pool_total.astype(jnp.bfloat16), 'sub', scatter_dimensio...]
    reshape x0 -> x4, local copies, waits for them, and re-layouts: none -> 14.6 us  [the longest x2 13.8 us: one_chunk(): jnp.dot(scatter, match_grad, preferred_element_type=jnp.float32)]
    all_gather x1 -> x0, blocking collectives: 14.2 us -> none  [local(): raw_pool = lax.all_gather(tokens, 'sub', axis=0, tiled=True)]
    ppermute x0 -> x20, waiting for transfers between devices: none -> 11.5 us  [the longest x7 7.44 us: local(): lax.ppermute(slot_b[k * slots:(k + 1) * slots], 'grp', shift(n_grp, -k))]
    all_to_all x2 -> x0, starting transfers between devices: 9.25 us -> none  [the longest x1 5.2 us: local(): lax.all_to_all(jnp.take(tokens, send_pick, axis=0), 'grp', split_axis=0,...]
  transfers between devices with their start and end apart: 3 -> 20, of which waited for: 2 -> 7; matrix products, arithmetic and copies ran while one was open for 2% -> 31% of each run, Pallas kernels for 0% -> 0%
where the time goes in v1:
time: 126 us; the launch traced here: 124 us
  matrix products  53.4 us (42%)
  starting transfers between devices  27.9 us (22%)
  local copies, waits for them, and re-layouts  16.8 us (13%)
  other arithmetic  13.7 us (11%)
  waiting for transfers between devices  11.5 us (9%)
    dot_general x1, matrix products, dense_terms(): jnp.einsum('ijrc,ird->jcd', d_scaled, pool_c, preferred_element_type=jnp....  20.5 us
    dot_general x1, matrix products, dense_terms(): jnp.einsum('ijrc,jcd->ird', d_scaled, received, preferred_element_type=jn...  20.3 us
    reshape x2, local copies, waits for them, and re-layouts, one_chunk(): jnp.dot(scatter, match_grad, preferred_element_type=jnp.float32)  13.8 us
    sub x1, other arithmetic, dense_terms(): d_rows - jnp.sum(d_rows * rows, axis=3, keepdims=True)  12.7 us
    ppermute x7, starting transfers between devices, local(): lax.ppermute(outgoing[k * slots:(k + 1) * slots], 'grp', shift(n_grp, k))  10.5 us
    ppermute x7, waiting for transfers between devices, local(): lax.ppermute(slot_b[k * slots:(k + 1) * slots], 'grp', shift(n_grp, -k))  7.44 us
    ppermute x7, starting transfers between devices, local(): lax.ppermute(slot_b[k * slots:(k + 1) * slots], 'grp', shift(n_grp, -k))  7.28 us
    ppermute x3, starting transfers between devices, local(): lax.ppermute(normed_b, 'sub', shift(n_sub, k))  6.14 us
  transfers between devices with their start and end apart: 20, of which 7 were waited for; matrix products, arithmetic and copies ran while one was open for 31% of the time, Pallas kernels for 0%

profile of v1, /device:TPU:0, one launch (start us, length us, event | category | flops | bytes accessed | tf_op | source)
XLA Modules:
  0.0 123.7 jit_solution(8542208228421318111)
XLA Ops:
  0.0 1.2 multiply_reduce_fusion.3
  1.4 5.1 %collective-permute-start.9 = (bf16[4,32,256]{2,1,0:T(8,128)(2,1)S(1)}, bf16[4,32,256]{2,1,0:T(8,128)(2,1)S(1)}, u32[]{:S(2)}, u32[]{:S(2)}) collective-permute-start(bf16[4,32,256]{2,1,0:T(8,128)(2,1)S(1)} %bitcast.100), channel_id=1, source_target_pairs={{0,3},{1,0},{2,1},{3,2},{4,7},{5,4},{6,5},{7,6},{8,11},{9,8},{10,9... | collective-permute-start | bytes 196616 | tf_op jit(solution)/shard_map/ppermute | solution.py:62
  9.6 1.5 %collective-permute-start.1 = (bf16[4,32,256]{2,1,0:T(8,128)(2,1)S(1)}, bf16[4,32,256]{2,1,0:T(8,128)(2,1)S(1)}, u32[]{:S(2)}, u32[]{:S(2)}) collective-permute-start(bf16[4,32,256]{2,1,0:T(8,128)(2,1)S(1)} %bitcast.118), channel_id=1, source_target_pairs={{0,8},{4,12},{8,16},{12,20},{16,24},{20,28},{24,0},{28,4},{1,9},{5... | collective-permute-start | bytes 196616 | tf_op jit(solution)/shard_map/ppermute | solution.py:85
  13.0 4.8 %reshape.103 = f32[16,32,32,32]{3,2,1,0:T(8,128)} reshape(f32[512,1024]{1,0:T(8,128)S(1)} %fusion.49) | data formatting | bytes 4194304 | tf_op jit(solution)/shard_map/reshape | solution.py:106
  17.8 9.0 %copy.9 = f32[16,32,32,32]{2,3,0,1:T(8,128)} copy(f32[16,32,32,32]{3,2,1,0:T(8,128)} %reshape.103) | data formatting | bytes 4194304 | tf_op jit(solution)/shard_map/reshape | solution.py:106
  26.8 2.4 %collective-permute-start.2 = (bf16[4,32,256]{2,1,0:T(8,128)(2,1)S(1)}, bf16[4,32,256]{2,1,0:T(8,128)(2,1)S(1)}, u32[]{:S(2)}, u32[]{:S(2)}) collective-permute-start(bf16[4,32,256]{2,1,0:T(8,128)(2,1)S(1)} %bitcast.121), channel_id=1, source_target_pairs={{0,12},{4,16},{8,20},{12,24},{16,28},{20,0},{24,4},{28,8},{1,13},{... | collective-permute-start | bytes 196616 | tf_op jit(solution)/shard_map/ppermute | solution.py:85
  29.8 1.3 %collective-permute-done.2 = bf16[4,32,256]{2,1,0:T(8,128)(2,1)S(1)} collective-permute-done((bf16[4,32,256]{2,1,0:T(8,128)(2,1)S(1)}, bf16[4,32,256]{2,1,0:T(8,128)(2,1)S(1)}, u32[]{:S(2)}, u32[]{:S(2)}) %collective-permute-start.2) | collective-permute-done | bytes 65568 | tf_op jit(solution)/shard_map/ppermute | solution.py:85
  31.1 1.7 %collective-permute-start.4 = (bf16[4,32,256]{2,1,0:T(8,128)(2,1)S(1)}, bf16[4,32,256]{2,1,0:T(8,128)(2,1)S(1)}, u32[]{:S(2)}, u32[]{:S(2)}) collective-permute-start(bf16[4,32,256]{2,1,0:T(8,128)(2,1)S(1)} %bitcast.117), channel_id=1, source_target_pairs={{0,20},{4,24},{8,28},{12,0},{16,4},{20,8},{24,12},{28,16},{1,21},{... | collective-permute-start | bytes 196616 | tf_op jit(solution)/shard_map/ppermute | solution.py:85
  33.6 1.4 %collective-permute-start.5 = (bf16[4,32,256]{2,1,0:T(8,128)(2,1)S(1)}, bf16[4,32,256]{2,1,0:T(8,128)(2,1)S(1)}, u32[]{:S(2)}, u32[]{:S(2)}) collective-permute-start(bf16[4,32,256]{2,1,0:T(8,128)(2,1)S(1)} %bitcast.116), channel_id=1, source_target_pairs={{0,24},{4,28},{8,0},{12,4},{16,8},{20,12},{24,16},{28,20},{1,25},{... | collective-permute-start | bytes 196616 | tf_op jit(solution)/shard_map/ppermute | solution.py:85
  35.2 2.8 %collective-permute-start.6 = (bf16[4,32,256]{2,1,0:T(8,128)(2,1)S(1)}, bf16[4,32,256]{2,1,0:T(8,128)(2,1)S(1)}, u32[]{:S(2)}, u32[]{:S(2)}) collective-permute-start(bf16[4,32,256]{2,1,0:T(8,128)(2,1)S(1)} %bitcast.115), channel_id=1, source_target_pairs={{0,28},{4,0},{8,4},{12,8},{16,12},{20,16},{24,20},{28,24},{1,29},{... | collective-permute-start | bytes 196616 | tf_op jit(solution)/shard_map/ppermute | solution.py:85
  38.0 1.9 %collective-permute-done.6 = bf16[4,32,256]{2,1,0:T(8,128)(2,1)S(1)} collective-permute-done((bf16[4,32,256]{2,1,0:T(8,128)(2,1)S(1)}, bf16[4,32,256]{2,1,0:T(8,128)(2,1)S(1)}, u32[]{:S(2)}, u32[]{:S(2)}) %collective-permute-start.6) | collective-permute-done | bytes 65568 | tf_op jit(solution)/shard_map/ppermute | solution.py:85
  39.9 4.5 %bitcast_divide_fusion.1 = f32[16,32,32,32]{2,3,0,1:T(8,128)} fusion(bf16[32,32,256]{2,1,0:T(8,128)(2,1)S(1)} %constant_dynamic-update-slice_fusion, bf16[4,32,256]{2,1,0:T(8,128)(2,1)S(1)} %collective-permute-done.9, bf16[4,32,256]{2,1,0:T(8,128)(2,1)S(1)} %collective-permute-done.8, bf16[4,32,256]{2,1,0:T(8,128)(2,1)S(1)} %collective-permute-done.7, ...), kind=kOutput, calls=%fused_computation.10 | convolution fusion | flops 270549024 | bytes 2883584 | tf_op jit(solution)/shard_map/div | solution.py:36
  44.4 4.9 %bitcast_divide_fusion = f32[16,32,32,32]{2,3,0,1:T(8,128)} fusion(bf16[32,32,256]{2,1,0:T(8,128)(2,1)S(1)} %constant_dynamic-update-slice_fusion, bf16[4,32,256]{2,1,0:T(8,128)(2,1)S(1)} %collective-permute-done.9, bf16[4,32,256]{2,1,0:T(8,128)(2,1)S(1)} %collective-permute-done.8, bf16[4,32,256]{2,1,0:T(8,128)(2,1)S(1)} %collective-permute-done.7, ...), kind=kOutput, calls=%fused_computation.8 | convolution fusion | flops 270549024 | bytes 2883584 | tf_op jit(solution)/shard_map/div | solution.py:37
  49.3 12.7 %fusion.1 = f32[16,32,32,32]{2,3,0,1:T(8,128)} fusion(f32[16,32,32,32]{2,3,0,1:T(8,128)} %bitcast_divide_fusion.1, f32[16,32,32,32]{2,3,0,1:T(8,128)} %copy.9, f32[16,32,32,32]{2,3,0,1:T(8,128)} %bitcast_divide_fusion), kind=kOutput, calls=%fused_computation.2 | output fusion | flops 1064991 | bytes 8388608 | tf_op jit(solution)/shard_map/sub | solution.py:40
  62.0 20.3 %fusion.37 = bf16[16,32,256]{2,1,0:T(8,128)(2,1)S(1)} fusion(f32[16,32,32,32]{2,3,0,1:T(8,128)} %bitcast_divide_fusion, f32[16,32,32,32]{2,3,0,1:T(8,128)} %bitcast_divide_fusion.1, f32[16,32,32,32]{2,3,0,1:T(8,128)} %fusion.1, f32[16,32,32,32]{2,3,0,1:T(8,128)} %copy.9, bf16[32,32,256]{2,1,0:T(8,128)(2,1)S(1)} %constant_dynamic-update-slice_fusion), kind=kOutput, calls=%fused_computation.29 | convolution fusion | flops 274350112 | bytes 9175040 | tf_op jit(solution)/shard_map/ijrc,jcd->ird/dot_general | solution.py:44
  82.3 2.9 %collective-permute-start.10 = (bf16[4,32,256]{2,1,0:T(8,128)(2,1)S(1)}, bf16[4,32,256]{2,1,0:T(8,128)(2,1)S(1)}, u32[]{:S(2)}, u32[]{:S(2)}) collective-permute-start(bf16[4,32,256]{2,1,0:T(8,128)(2,1)S(1)} %get-tuple-element.21), channel_id=1, source_target_pairs={{0,3},{1,0},{2,1},{3,2},{4,7},{5,4},{6,5},{7,6},{8,11},{9,8},{10,9... | collective-permute-start | bytes 196616 | tf_op jit(solution)/shard_map/ppermute | solution.py:132
  86.3 20.5 %fusion.31 = bf16[32,32,256]{2,1,0:T(8,128)(2,1)S(1)} fusion(f32[16,32,32,32]{2,3,0,1:T(8,128)} %bitcast_divide_fusion, f32[16,32,32,32]{2,3,0,1:T(8,128)} %bitcast_divide_fusion.1, f32[16,32,32,32]{2,3,0,1:T(8,128)} %fusion.1, f32[16,32,32,32]{2,3,0,1:T(8,128)} %copy.9, bf16[4,32,256]{2,1,0:T(8,128)(2,1)S(1)} %collective-permute-done.9, ...), kind=kOutput, calls=%fused_computation.27 | convolution fusion | flops 274874400 | bytes 9175040 | tf_op jit(solution)/shard_map/ijrc,ird->jcd/dot_general | solution.py:45
  107.0 2.2 %collective-permute-start.18 = (bf16[4,32,256]{2,1,0:T(8,128)(2,1)S(1)}, bf16[4,32,256]{2,1,0:T(8,128)(2,1)S(1)}, u32[]{:S(2)}, u32[]{:S(2)}) collective-permute-start(bf16[4,32,256]{2,1,0:T(8,128)(2,1)S(1)} %get-tuple-element.6), channel_id=1, source_target_pairs={{0,8},{4,12},{8,16},{12,20},{16,24},{20,28},{24,0},{28,4},{1,9},{5... | collective-permute-start | bytes 196616 | tf_op jit(solution)/shard_map/ppermute | solution.py:142
  110.2 1.2 %collective-permute-start.13 = (bf16[4,32,256]{2,1,0:T(8,128)(2,1)S(1)}, bf16[4,32,256]{2,1,0:T(8,128)(2,1)S(1)}, u32[]{:S(2)}, u32[]{:S(2)}) collective-permute-start(bf16[4,32,256]{2,1,0:T(8,128)(2,1)S(1)} %get-tuple-element.11), channel_id=1, source_target_pairs={{0,28},{4,0},{8,4},{12,8},{16,12},{20,16},{24,20},{28,24},{1,29},{... | collective-permute-start | bytes 196616 | tf_op jit(solution)/shard_map/ppermute | solution.py:142
  111.6 1.8 %collective-permute-done.13 = bf16[4,32,256]{2,1,0:T(8,128)(2,1)S(1)} collective-permute-done((bf16[4,32,256]{2,1,0:T(8,128)(2,1)S(1)}, bf16[4,32,256]{2,1,0:T(8,128)(2,1)S(1)}, u32[]{:S(2)}, u32[]{:S(2)}) %collective-permute-start.13) | collective-permute-done | bytes 65568 | tf_op jit(solution)/shard_map/ppermute | solution.py:142
  113.3 1.6 %collective-permute-start.14 = (bf16[4,32,256]{2,1,0:T(8,128)(2,1)S(1)}, bf16[4,32,256]{2,1,0:T(8,128)(2,1)S(1)}, u32[]{:S(2)}, u32[]{:S(2)}) collective-permute-start(bf16[4,32,256]{2,1,0:T(8,128)(2,1)S(1)} %get-tuple-element.10), channel_id=1, source_target_pairs={{0,24},{4,28},{8,0},{12,4},{16,8},{20,12},{24,16},{28,20},{1,25},{... | collective-permute-start | bytes 196616 | tf_op jit(solution)/shard_map/ppermute | solution.py:142
  114.9 2.7 %collective-permute-done.14 = bf16[4,32,256]{2,1,0:T(8,128)(2,1)S(1)} collective-permute-done((bf16[4,32,256]{2,1,0:T(8,128)(2,1)S(1)}, bf16[4,32,256]{2,1,0:T(8,128)(2,1)S(1)}, u32[]{:S(2)}, u32[]{:S(2)}) %collective-permute-start.14) | collective-permute-done | bytes 65568 | tf_op jit(solution)/shard_map/ppermute | solution.py:142
  117.6 1.2 collective-permute-start.15
  118.8 2.9 %collective-permute-done.15 = bf16[4,32,256]{2,1,0:T(8,128)(2,1)S(1)} collective-permute-done((bf16[4,32,256]{2,1,0:T(8,128)(2,1)S(1)}, bf16[4,32,256]{2,1,0:T(8,128)(2,1)S(1)}, u32[]{:S(2)}, u32[]{:S(2)}) %collective-permute-start.15) | collective-permute-done | bytes 65568 | tf_op jit(solution)/shard_map/ppermute | solution.py:142
  (75 shorter events, 10.7 us)
Async XLA Ops:
  0.0 11.8 %copy-start = (bf16[128,1024]{1,0:T(8,128)(2,1)S(1)}, bf16[128,1024]{1,0:T(8,128)(2,1)}, u32[]{:S(2)}) copy-start(bf16[128,1024]{1,0:T(8,128)(2,1)} %param.8) | copy-start | bytes 786436
  1.4 38.5 %collective-permute-start.9 = (bf16[4,32,256]{2,1,0:T(8,128)(2,1)S(1)}, bf16[4,32,256]{2,1,0:T(8,128)(2,1)S(1)}, u32[]{:S(2)}, u32[]{:S(2)}) collective-permute-start(bf16[4,32,256]{2,1,0:T(8,128)(2,1)S(1)} %bitcast.100), channel_id=1, source_target_pairs={{0,3},{1,0},{2,1},{3,2},{4,7},{5,4},{6,5},{7,6},{8,11},{9,8},{10,9... | collective-permute-start | bytes 196616 | tf_op jit(solution)/shard_map/ppermute | solution.py:62
  6.5 33.4 %collective-permute-start.8 = (bf16[4,32,256]{2,1,0:T(8,128)(2,1)S(1)}, bf16[4,32,256]{2,1,0:T(8,128)(2,1)S(1)}, u32[]{:S(2)}, u32[]{:S(2)}) collective-permute-start(bf16[4,32,256]{2,1,0:T(8,128)(2,1)S(1)} %bitcast.101), channel_id=1, source_target_pairs={{0,2},{1,3},{2,0},{3,1},{4,6},{5,7},{6,4},{7,5},{8,10},{9,11},{10,... | collective-permute-start | bytes 196616 | tf_op jit(solution)/shard_map/ppermute | solution.py:62
  6.5 33.4 %collective-permute-start.7 = (bf16[4,32,256]{2,1,0:T(8,128)(2,1)S(1)}, bf16[4,32,256]{2,1,0:T(8,128)(2,1)S(1)}, u32[]{:S(2)}, u32[]{:S(2)}) collective-permute-start(bf16[4,32,256]{2,1,0:T(8,128)(2,1)S(1)} %bitcast.102), channel_id=1, source_target_pairs={{0,1},{1,2},{2,3},{3,0},{4,5},{5,6},{6,7},{7,4},{8,9},{9,10},{10,1... | collective-permute-start | bytes 196616 | tf_op jit(solution)/shard_map/ppermute | solution.py:62
  9.5 17.3 %collective-permute-start = (bf16[4,32,256]{2,1,0:T(8,128)(2,1)S(1)}, bf16[4,32,256]{2,1,0:T(8,128)(2,1)S(1)}, u32[]{:S(2)}, u32[]{:S(2)}) collective-permute-start(bf16[4,32,256]{2,1,0:T(8,128)(2,1)S(1)} %bitcast.120), channel_id=1, source_target_pairs={{0,4},{4,8},{8,12},{12,16},{16,20},{20,24},{24,28},{28,0},{1,5},{5... | collective-permute-start | bytes 196616 | tf_op jit(solution)/shard_map/ppermute | solution.py:85
  9.6 19.7 %collective-permute-start.1 = (bf16[4,32,256]{2,1,0:T(8,128)(2,1)S(1)}, bf16[4,32,256]{2,1,0:T(8,128)(2,1)S(1)}, u32[]{:S(2)}, u32[]{:S(2)}) collective-permute-start(bf16[4,32,256]{2,1,0:T(8,128)(2,1)S(1)} %bitcast.118), channel_id=1, source_target_pairs={{0,8},{4,12},{8,16},{12,20},{16,24},{20,28},{24,0},{28,4},{1,9},{5... | collective-permute-start | bytes 196616 | tf_op jit(solution)/shard_map/ppermute | solution.py:85
  17.8 11.5 %copy-start.2 = (bf16[32,32,256]{2,1,0:T(8,128)(2,1)S(1)}, bf16[32,32,256]{2,1,0:T(8,128)(2,1)}, u32[]{:S(2)}) copy-start(bf16[32,32,256]{2,1,0:T(8,128)(2,1)} %bitcast_dynamic-update-slice_fusion) | copy-start | bytes 1572868
  26.8 4.3 %collective-permute-start.2 = (bf16[4,32,256]{2,1,0:T(8,128)(2,1)S(1)}, bf16[4,32,256]{2,1,0:T(8,128)(2,1)S(1)}, u32[]{:S(2)}, u32[]{:S(2)}) collective-permute-start(bf16[4,32,256]{2,1,0:T(8,128)(2,1)S(1)} %bitcast.121), channel_id=1, source_target_pairs={{0,12},{4,16},{8,20},{12,24},{16,28},{20,0},{24,4},{28,8},{1,13},{... | collective-permute-start | bytes 196616 | tf_op jit(solution)/shard_map/ppermute | solution.py:85
  29.3 4.4 %collective-permute-start.3 = (bf16[4,32,256]{2,1,0:T(8,128)(2,1)S(1)}, bf16[4,32,256]{2,1,0:T(8,128)(2,1)S(1)}, u32[]{:S(2)}, u32[]{:S(2)}) collective-permute-start(bf16[4,32,256]{2,1,0:T(8,128)(2,1)S(1)} %bitcast.119), channel_id=1, source_target_pairs={{0,16},{4,20},{8,24},{12,28},{16,0},{20,4},{24,8},{28,12},{1,17},{... | collective-permute-start | bytes 196616 | tf_op jit(solution)/shard_map/ppermute | solution.py:85
  31.1 4.0 %collective-permute-start.4 = (bf16[4,32,256]{2,1,0:T(8,128)(2,1)S(1)}, bf16[4,32,256]{2,1,0:T(8,128)(2,1)S(1)}, u32[]{:S(2)}, u32[]{:S(2)}) collective-permute-start(bf16[4,32,256]{2,1,0:T(8,128)(2,1)S(1)} %bitcast.117), channel_id=1, source_target_pairs={{0,20},{4,24},{8,28},{12,0},{16,4},{20,8},{24,12},{28,16},{1,21},{... | collective-permute-start | bytes 196616 | tf_op jit(solution)/shard_map/ppermute | solution.py:85
  33.6 4.4 %collective-permute-start.5 = (bf16[4,32,256]{2,1,0:T(8,128)(2,1)S(1)}, bf16[4,32,256]{2,1,0:T(8,128)(2,1)S(1)}, u32[]{:S(2)}, u32[]{:S(2)}) collective-permute-start(bf16[4,32,256]{2,1,0:T(8,128)(2,1)S(1)} %bitcast.116), channel_id=1, source_target_pairs={{0,24},{4,28},{8,0},{12,4},{16,8},{20,12},{24,16},{28,20},{1,25},{... | collective-permute-start | bytes 196616 | tf_op jit(solution)/shard_map/ppermute | solution.py:85
  35.2 4.7 %collective-permute-start.6 = (bf16[4,32,256]{2,1,0:T(8,128)(2,1)S(1)}, bf16[4,32,256]{2,1,0:T(8,128)(2,1)S(1)}, u32[]{:S(2)}, u32[]{:S(2)}) collective-permute-start(bf16[4,32,256]{2,1,0:T(8,128)(2,1)S(1)} %bitcast.115), channel_id=1, source_target_pairs={{0,28},{4,0},{8,4},{12,8},{16,12},{20,16},{24,20},{28,24},{1,29},{... | collective-permute-start | bytes 196616 | tf_op jit(solution)/shard_map/ppermute | solution.py:85
  82.3 26.8 %collective-permute-start.10 = (bf16[4,32,256]{2,1,0:T(8,128)(2,1)S(1)}, bf16[4,32,256]{2,1,0:T(8,128)(2,1)S(1)}, u32[]{:S(2)}, u32[]{:S(2)}) collective-permute-start(bf16[4,32,256]{2,1,0:T(8,128)(2,1)S(1)} %get-tuple-element.21), channel_id=1, source_target_pairs={{0,3},{1,0},{2,1},{3,2},{4,7},{5,4},{6,5},{7,6},{8,11},{9,8},{10,9... | collective-permute-start | bytes 196616 | tf_op jit(solution)/shard_map/ppermute | solution.py:132
  85.2 24.1 %collective-permute-start.12 = (bf16[4,32,256]{2,1,0:T(8,128)(2,1)S(1)}, bf16[4,32,256]{2,1,0:T(8,128)(2,1)S(1)}, u32[]{:S(2)}, u32[]{:S(2)}) collective-permute-start(bf16[4,32,256]{2,1,0:T(8,128)(2,1)S(1)} %get-tuple-element.22), channel_id=1, source_target_pairs={{0,1},{1,2},{2,3},{3,0},{4,5},{5,6},{6,7},{7,4},{8,9},{9,10},{10,1... | collective-permute-start | bytes 196616 | tf_op jit(solution)/shard_map/ppermute | solution.py:132
  85.2 37.6 %copy-start.1 = (bf16[256,256]{1,0:T(8,128)(2,1)S(1)}, bf16[256,256]{1,0:T(8,128)(2,1)}, u32[]{:S(2)}) copy-start(bf16[256,256]{1,0:T(8,128)(2,1)} %param.7) | copy-start | bytes 393220
  85.2 25.0 %collective-permute-start.11 = (bf16[4,32,256]{2,1,0:T(8,128)(2,1)S(1)}, bf16[4,32,256]{2,1,0:T(8,128)(2,1)S(1)}, u32[]{:S(2)}, u32[]{:S(2)}) collective-permute-start(bf16[4,32,256]{2,1,0:T(8,128)(2,1)S(1)} %get-tuple-element.23), channel_id=1, source_target_pairs={{0,2},{1,3},{2,0},{3,1},{4,6},{5,7},{6,4},{7,5},{8,10},{9,11},{10,... | collective-permute-start | bytes 196616 | tf_op jit(solution)/shard_map/ppermute | solution.py:132
  106.9 15.0 %collective-permute-start.19 = (bf16[4,32,256]{2,1,0:T(8,128)(2,1)S(1)}, bf16[4,32,256]{2,1,0:T(8,128)(2,1)S(1)}, u32[]{:S(2)}, u32[]{:S(2)}) collective-permute-start(bf16[4,32,256]{2,1,0:T(8,128)(2,1)S(1)} %get-tuple-element.5), channel_id=1, source_target_pairs={{0,4},{4,8},{8,12},{12,16},{16,20},{20,24},{24,28},{28,0},{1,5},{5... | collective-permute-start | bytes 196616 | tf_op jit(solution)/shard_map/ppermute | solution.py:142
  107.0 14.9 %collective-permute-start.18 = (bf16[4,32,256]{2,1,0:T(8,128)(2,1)S(1)}, bf16[4,32,256]{2,1,0:T(8,128)(2,1)S(1)}, u32[]{:S(2)}, u32[]{:S(2)}) collective-permute-start(bf16[4,32,256]{2,1,0:T(8,128)(2,1)S(1)} %get-tuple-element.6), channel_id=1, source_target_pairs={{0,8},{4,12},{8,16},{12,20},{16,24},{20,28},{24,0},{28,4},{1,9},{5... | collective-permute-start | bytes 196616 | tf_op jit(solution)/shard_map/ppermute | solution.py:142
  109.1 12.7 %collective-permute-start.17 = (bf16[4,32,256]{2,1,0:T(8,128)(2,1)S(1)}, bf16[4,32,256]{2,1,0:T(8,128)(2,1)S(1)}, u32[]{:S(2)}, u32[]{:S(2)}) collective-permute-start(bf16[4,32,256]{2,1,0:T(8,128)(2,1)S(1)} %get-tuple-element.7), channel_id=1, source_target_pairs={{0,12},{4,16},{8,20},{12,24},{16,28},{20,0},{24,4},{28,8},{1,13},{... | collective-permute-start | bytes 196616 | tf_op jit(solution)/shard_map/ppermute | solution.py:142
  109.3 12.5 %collective-permute-start.16 = (bf16[4,32,256]{2,1,0:T(8,128)(2,1)S(1)}, bf16[4,32,256]{2,1,0:T(8,128)(2,1)S(1)}, u32[]{:S(2)}, u32[]{:S(2)}) collective-permute-start(bf16[4,32,256]{2,1,0:T(8,128)(2,1)S(1)} %get-tuple-element.8), channel_id=1, source_target_pairs={{0,16},{4,20},{8,24},{12,28},{16,0},{20,4},{24,8},{28,12},{1,17},{... | collective-permute-start | bytes 196616 | tf_op jit(solution)/shard_map/ppermute | solution.py:142
  110.2 3.2 %collective-permute-start.13 = (bf16[4,32,256]{2,1,0:T(8,128)(2,1)S(1)}, bf16[4,32,256]{2,1,0:T(8,128)(2,1)S(1)}, u32[]{:S(2)}, u32[]{:S(2)}) collective-permute-start(bf16[4,32,256]{2,1,0:T(8,128)(2,1)S(1)} %get-tuple-element.11), channel_id=1, source_target_pairs={{0,28},{4,0},{8,4},{12,8},{16,12},{20,16},{24,20},{28,24},{1,29},{... | collective-permute-start | bytes 196616 | tf_op jit(solution)/shard_map/ppermute | solution.py:142
  113.3 4.3 %collective-permute-start.14 = (bf16[4,32,256]{2,1,0:T(8,128)(2,1)S(1)}, bf16[4,32,256]{2,1,0:T(8,128)(2,1)S(1)}, u32[]{:S(2)}, u32[]{:S(2)}) collective-permute-start(bf16[4,32,256]{2,1,0:T(8,128)(2,1)S(1)} %get-tuple-element.10), channel_id=1, source_target_pairs={{0,24},{4,28},{8,0},{12,4},{16,8},{20,12},{24,16},{28,20},{1,25},{... | collective-permute-start | bytes 196616 | tf_op jit(solution)/shard_map/ppermute | solution.py:142
  117.6 4.2 %collective-permute-start.15 = (bf16[4,32,256]{2,1,0:T(8,128)(2,1)S(1)}, bf16[4,32,256]{2,1,0:T(8,128)(2,1)S(1)}, u32[]{:S(2)}, u32[]{:S(2)}) collective-permute-start(bf16[4,32,256]{2,1,0:T(8,128)(2,1)S(1)} %get-tuple-element.9), channel_id=1, source_target_pairs={{0,20},{4,24},{8,28},{12,0},{16,4},{20,8},{24,12},{28,16},{1,21},{... | collective-permute-start | bytes 196616 | tf_op jit(solution)/shard_map/ppermute | solution.py:142

commit v2 on v1

--- a/solution.py
+++ b/solution.py
@@ -1,13 +1,16 @@
+import functools
+
 import jax
 import jax.numpy as jnp
 from jax import lax
+from jax.experimental import pallas as pl
+from jax.experimental.pallas import tpu as pltpu
 from jax.sharding import PartitionSpec as P
 
 EPSILON = 1e-05
 SOFTMAX_COOLING = 0.1
 SUB_MODE = "perm"
 GRP_MODE = "perm"
-CHUNK_ELEMS = 1 << 19
 
 
 def normalize(tokens, proj_weight):
@@ -26,24 +29,52 @@
     return [(i, (i + step) % count) for i in range(count)]
 
 
-def dense_terms(pool_c, received, grads_c):
-    score_scale = 1.0 / (pool_c.shape[-1] * SOFTMAX_COOLING)
-    scores = (
-        jnp.einsum("ird,jcd->ijrc", pool_c, received, preferred_element_type=jnp.float32)
-        * score_scale
-    )
-    expo = jnp.exp(scores)
-    rows = expo / jnp.sum(expo, axis=3, keepdims=True)
-    cols = expo / jnp.sum(expo, axis=2, keepdims=True)
-    d_rows = grads_c * cols
-    d_cols = grads_c * rows
-    d_scores = rows * (d_rows - jnp.sum(d_rows * rows, axis=3, keepdims=True)) + cols * (
-        d_cols - jnp.sum(d_cols * cols, axis=2, keepdims=True)
-    )
-    d_scaled = (d_scores * score_scale).astype(jnp.bfloat16)
-    pool_part = jnp.einsum("ijrc,jcd->ird", d_scaled, received, preferred_element_type=jnp.float32)
-    slot_part = jnp.einsum("ijrc,ird->jcd", d_scaled, pool_c, preferred_element_type=jnp.float32)
-    return pool_part, slot_part
+def lane_group_sum(x, group):
+    rows, width = x.shape
+    xt = x.T.reshape(width // group, group, rows)
+    total = jnp.sum(xt, axis=1, keepdims=True)
+    return jnp.broadcast_to(total, (width // group, group, rows)).reshape(width, rows).T
+
+
+def row_group_sum(x, group):
+    rows, width = x.shape
+    xr = x.reshape(rows // group, group, width)
+    total = jnp.sum(xr, axis=1, keepdims=True)
+    return jnp.broadcast_to(total, (rows // group, group, width)).reshape(rows, width)
+
+
+def softmax_bwd_kernel(group, score_scale, s_ref, g_ref, d_ref):
+    expo = jnp.exp(s_ref[...])
+    rows = expo / lane_group_sum(expo, group)
+    cols = expo / row_group_sum(expo, group)
+    grads = g_ref[...].astype(jnp.float32)
+    d_rows = grads * cols
+    d_cols = grads * rows
+    d_scores = rows * (d_rows - lane_group_sum(d_rows * rows, group)) + cols * (
+        d_cols - row_group_sum(d_cols * cols, group)
+    )
+    d_ref[...] = (d_scores * score_scale).astype(jnp.bfloat16)
+
+
+def softmax_bwd(scores, grads, group, score_scale):
+    total_rows, width = scores.shape
+    block = 128 if total_rows % 128 == 0 else total_rows
+    return pl.pallas_call(
+        functools.partial(softmax_bwd_kernel, group, score_scale),
+        out_shape=jax.ShapeDtypeStruct((total_rows, width), jnp.bfloat16),
+        grid=(total_rows // block,),
+        in_specs=[
+            pl.BlockSpec((block, width), lambda b: (b, 0)),
+            pl.BlockSpec((block, width), lambda b: (b, 0)),
+        ],
+        out_specs=pl.BlockSpec((block, width), lambda b: (b, 0)),
+        compiler_params=pltpu.CompilerParams(vmem_limit_bytes=48 * 1024 * 1024),
+        cost_estimate=pl.CostEstimate(
+            flops=30 * total_rows * width,
+            transcendentals=total_rows * width,
+            bytes_accessed=8 * total_rows * width,
+        ),
+    )(scores, grads)
 
 
 def local(n_grp, n_sub, tokens, proj_weight, match_grad, edge_first, pair_second_image, send_pick):
@@ -93,36 +124,26 @@
         second_at = pair_second_image
 
     pair_at = first_at * recv + second_at
-    chunk = group_img
-    while chunk > 1 and (chunk * recv * length * length > CHUNK_ELEMS or group_img % chunk):
-        chunk -= 1
-    n_chunks = group_img // chunk
-
-    def one_chunk(chunk_index):
-        base = chunk_index * (chunk * recv)
-        scatter = (
-            lax.broadcasted_iota(jnp.int32, (chunk * recv, edge_count), 0) + base == pair_at[None, :]
-        ).astype(jnp.bfloat16)
-        grads_c = jnp.dot(scatter, match_grad, preferred_element_type=jnp.float32).reshape(
-            chunk, recv, length, length
-        )
-        pool_c = lax.dynamic_slice_in_dim(pool, chunk_index * chunk, chunk, 0)
-        return dense_terms(pool_c, received, grads_c)
-
-    if n_chunks == 1:
-        pool_total, slot_total = one_chunk(0)
-    else:
-
-        def body(carry, chunk_index):
-            pool_part, slot_part = one_chunk(chunk_index)
-            return carry + slot_part, pool_part.astype(jnp.bfloat16)
-
-        slot_total, pool_parts = lax.scan(
-            body,
-            jnp.zeros((recv, length, feat_width), jnp.float32),
-            jnp.arange(n_chunks, dtype=jnp.int32),
-        )
-        pool_total = pool_parts.reshape(group_img, length, feat_width)
+    scatter = (
+        lax.broadcasted_iota(jnp.int32, (group_img * recv, edge_count), 0) == pair_at[None, :]
+    ).astype(jnp.bfloat16)
+    grads = jnp.dot(scatter, match_grad, preferred_element_type=jnp.float32).astype(jnp.bfloat16)
+    grads = grads.reshape(group_img, recv, length, length).transpose(0, 2, 1, 3)
+    grads = grads.reshape(group_img * length, recv * length)
+    pool2 = pool.reshape(group_img * length, feat_width)
+    recv2 = received.reshape(recv * length, feat_width)
+    score_scale = 1.0 / (feat_width * SOFTMAX_COOLING)
+    scores = (
+        lax.dot_general(pool2, recv2, (((1,), (1,)), ((), ())), preferred_element_type=jnp.float32)
+        * score_scale
+    )
+    d_scaled = softmax_bwd(scores, grads, length, score_scale)
+    pool_total = jnp.dot(d_scaled, recv2, preferred_element_type=jnp.float32).reshape(
+        group_img, length, feat_width
+    )
+    slot_total = lax.dot_general(
+        d_scaled, pool2, (((0,), (0,)), ((), ())), preferred_element_type=jnp.float32
+    ).reshape(recv, length, feat_width)
     pool_b = pool_total.astype(jnp.bfloat16)
     slot_b = slot_total.astype(jnp.bfloat16)
 

time: 126 us -> 70.6 us (0.56); the launches traced: 124 us -> 70.3 us
  matrix products: 53.4 us -> 4.49 us
  other arithmetic: 13.7 us -> 1.33 us
  waiting for transfers between devices: 11.5 us -> 15.9 us
  local copies, waits for them, and re-layouts: 16.8 us -> 19.9 us
  Pallas kernels: 0 us -> 2.6 us
  starting transfers between devices: 27.9 us -> 25.6 us
    dot_general x3 -> x4, matrix products: 41.3 us -> 1.76 us  [the longest x1 0.47 us: local(): lax.dot_general(pool2, recv2, (((1,), (1,)), ((), ())), preferred_element...]
    sub x1 -> x0, other arithmetic: 12.7 us -> none  [dense_terms(): d_rows - jnp.sum(d_rows * rows, axis=3, keepdims=True)]
    div x2 -> x0, matrix products: 9.4 us -> none  [the longest x1 4.94 us: dense_terms(): cols = expo / jnp.sum(expo, axis=2, keepdims=True)]
    ppermute x3, waiting for transfers between devices: 0.01 us -> 3.06 us  [local(): lax.ppermute(pool_b[k * img_count:(k + 1) * img_count], 'sub', shift(n_su...]
    reshape x2 -> x3, local copies, waits for them, and re-layouts: 13.8 us -> 16.4 us  [the longest x2 10.3 us: local(): grads = grads.reshape(group_img, recv, length, length).transpose(0, 2, 1, 3)]
    pallas_call x0 -> x1, Pallas kernels: none -> 2.6 us  [softmax_bwd(): pl.pallas_call(functools.partial(softmax_bwd_kernel, group, score_scale),...]
    ppermute x7, starting transfers between devices: 7.28 us -> 4.92 us  [local(): lax.ppermute(slot_b[k * slots:(k + 1) * slots], 'grp', shift(n_grp, -k))]
    ppermute x7, waiting for transfers between devices: 7.44 us -> 8.8 us  [local(): lax.ppermute(slot_b[k * slots:(k + 1) * slots], 'grp', shift(n_grp, -k))]
  transfers between devices with their start and end apart: 20 -> 20, of which waited for: 7 -> 9; matrix products, arithmetic and copies ran while one was open for 31% -> 30% of each run, Pallas kernels for 0% -> 0%
where the time goes in v2:
time: 70.6 us; the launch traced here: 70.3 us
  starting transfers between devices  25.6 us (36%)
  local copies, waits for them, and re-layouts  19.9 us (28%)
  waiting for transfers between devices  15.9 us (23%)
  matrix products  4.49 us (6%)
  Pallas kernels  2.6 us (4%)
  other arithmetic  1.33 us (2%)
    ppermute x7, starting transfers between devices, local(): lax.ppermute(outgoing[k * slots:(k + 1) * slots], 'grp', shift(n_grp, k))  10.6 us
    reshape x2, local copies, waits for them, and re-layouts, local(): grads = grads.reshape(group_img, recv, length, length).transpose(0, 2, 1, 3)  10.3 us
    ppermute x7, waiting for transfers between devices, local(): lax.ppermute(slot_b[k * slots:(k + 1) * slots], 'grp', shift(n_grp, -k))  8.8 us
    reshape x1, local copies, waits for them, and re-layouts, local(): grads = grads.reshape(group_img * length, recv * length)  6.16 us
    ppermute x3, starting transfers between devices, local(): lax.ppermute(normed_b, 'sub', shift(n_sub, k))  6.15 us
    ppermute x7, starting transfers between devices, local(): lax.ppermute(slot_b[k * slots:(k + 1) * slots], 'grp', shift(n_grp, -k))  4.92 us
    ppermute x7, waiting for transfers between devices, local(): lax.ppermute(outgoing[k * slots:(k + 1) * slots], 'grp', shift(n_grp, k))  4.08 us
    ppermute x3, starting transfers between devices, local(): lax.ppermute(pool_b[k * img_count:(k + 1) * img_count], 'sub', shift(n_su...  3.94 us
  transfers between devices with their start and end apart: 20, of which 9 were waited for; matrix products, arithmetic and copies ran while one was open for 30% of the time, Pallas kernels for 0%

profile of v2, /device:TPU:0, one launch (start us, length us, event | category | flops | bytes accessed | tf_op | source)
XLA Modules:
  0.0 70.3 jit_solution(6647536748081876641)
XLA Ops:
  0.0 1.2 %multiply_reduce_fusion.1 = (f32[128]{0:T(128)S(1)}, f32[128,256]{1,0:T(8,128)S(1)}) fusion(bf16[128,256]{1,0:T(8,128)(2,1)} %bitcast.90, bf16[256,256]{1,0:T(8,128)(2,1)} %param.7), kind=kOutput, calls=%fused_computation.14 | convolution fusion | flops 16842624 | bytes 328192 | tf_op jit(solution)/shard_map/dot_general | solution.py:18
  1.4 5.1 %collective-permute-start.2 = (bf16[4,32,256]{2,1,0:T(8,128)(2,1)S(1)}, bf16[4,32,256]{2,1,0:T(8,128)(2,1)S(1)}, u32[]{:S(2)}, u32[]{:S(2)}) collective-permute-start(bf16[4,32,256]{2,1,0:T(8,128)(2,1)S(1)} %bitcast.77), channel_id=1, source_target_pairs={{0,3},{1,0},{2,1},{3,2},{4,7},{5,4},{6,5},{7,6},{8,11},{9,8},{10,9... | collective-permute-start | bytes 196616 | tf_op jit(solution)/shard_map/ppermute | solution.py:93
  6.5 1.0 %collective-permute-start = (bf16[4,32,256]{2,1,0:T(8,128)(2,1)S(1)}, bf16[4,32,256]{2,1,0:T(8,128)(2,1)S(1)}, u32[]{:S(2)}, u32[]{:S(2)}) collective-permute-start(bf16[4,32,256]{2,1,0:T(8,128)(2,1)S(1)} %bitcast.79), channel_id=1, source_target_pairs={{0,1},{1,2},{2,3},{3,0},{4,5},{5,6},{6,7},{7,4},{8,9},{9,10},{10,1... | collective-permute-start | bytes 196616 | tf_op jit(solution)/shard_map/ppermute | solution.py:93
  9.6 1.5 %collective-permute-start.4 = (bf16[4,32,256]{2,1,0:T(8,128)(2,1)S(1)}, bf16[4,32,256]{2,1,0:T(8,128)(2,1)S(1)}, u32[]{:S(2)}, u32[]{:S(2)}) collective-permute-start(bf16[4,32,256]{2,1,0:T(8,128)(2,1)S(1)} %bitcast.94), channel_id=1, source_target_pairs={{0,8},{4,12},{8,16},{12,20},{16,24},{20,28},{24,0},{28,4},{1,9},{5... | collective-permute-start | bytes 196616 | tf_op jit(solution)/shard_map/ppermute | solution.py:116
  11.7 4.3 %reshape.114 = bf16[16,32,32,32]{3,2,1,0:T(8,128)(2,1)} reshape(bf16[512,1024]{1,0:T(8,128)(2,1)S(1)} %convolution_convert_fusion.1) | data formatting | bytes 2097152 | tf_op jit(solution)/shard_map/reshape | solution.py:131
  16.1 6.0 %copy.30 = bf16[16,32,32,32]{3,1,2,0:T(8,128)(2,1)} copy(bf16[16,32,32,32]{3,2,1,0:T(8,128)(2,1)} %reshape.114) | data formatting | bytes 2097152 | tf_op jit(solution)/shard_map/reshape | solution.py:131
  22.0 6.2 %reshape.115.g_ref = bf16[512,1024]{1,0:T(8,128)(2,1)S(1)} reshape(bf16[16,32,32,32]{3,2,1,0:T(8,128)(2,1)} %bitcast.69) | data formatting | bytes 2097152 | tf_op jit(solution)/shard_map/reshape | solution.py:132
  28.2 2.5 %collective-permute-start.5 = (bf16[4,32,256]{2,1,0:T(8,128)(2,1)S(1)}, bf16[4,32,256]{2,1,0:T(8,128)(2,1)S(1)}, u32[]{:S(2)}, u32[]{:S(2)}) collective-permute-start(bf16[4,32,256]{2,1,0:T(8,128)(2,1)S(1)} %bitcast.97), channel_id=1, source_target_pairs={{0,12},{4,16},{8,20},{12,24},{16,28},{20,0},{24,4},{28,8},{1,13},{... | collective-permute-start | bytes 196616 | tf_op jit(solution)/shard_map/ppermute | solution.py:116
  31.2 1.3 %collective-permute-done.5 = bf16[4,32,256]{2,1,0:T(8,128)(2,1)S(1)} collective-permute-done((bf16[4,32,256]{2,1,0:T(8,128)(2,1)S(1)}, bf16[4,32,256]{2,1,0:T(8,128)(2,1)S(1)}, u32[]{:S(2)}, u32[]{:S(2)}) %collective-permute-start.5) | collective-permute-done | bytes 65568 | tf_op jit(solution)/shard_map/ppermute | solution.py:116
  32.5 1.7 %collective-permute-start.7 = (bf16[4,32,256]{2,1,0:T(8,128)(2,1)S(1)}, bf16[4,32,256]{2,1,0:T(8,128)(2,1)S(1)}, u32[]{:S(2)}, u32[]{:S(2)}) collective-permute-start(bf16[4,32,256]{2,1,0:T(8,128)(2,1)S(1)} %bitcast.93), channel_id=1, source_target_pairs={{0,20},{4,24},{8,28},{12,0},{16,4},{20,8},{24,12},{28,16},{1,21},{... | collective-permute-start | bytes 196616 | tf_op jit(solution)/shard_map/ppermute | solution.py:116
  35.0 1.4 %collective-permute-start.8 = (bf16[4,32,256]{2,1,0:T(8,128)(2,1)S(1)}, bf16[4,32,256]{2,1,0:T(8,128)(2,1)S(1)}, u32[]{:S(2)}, u32[]{:S(2)}) collective-permute-start(bf16[4,32,256]{2,1,0:T(8,128)(2,1)S(1)} %bitcast.92), channel_id=1, source_target_pairs={{0,24},{4,28},{8,0},{12,4},{16,8},{20,12},{24,16},{28,20},{1,25},{... | collective-permute-start | bytes 196616 | tf_op jit(solution)/shard_map/ppermute | solution.py:116
  36.6 2.8 %collective-permute-start.9 = (bf16[4,32,256]{2,1,0:T(8,128)(2,1)S(1)}, bf16[4,32,256]{2,1,0:T(8,128)(2,1)S(1)}, u32[]{:S(2)}, u32[]{:S(2)}) collective-permute-start(bf16[4,32,256]{2,1,0:T(8,128)(2,1)S(1)} %bitcast.91), channel_id=1, source_target_pairs={{0,28},{4,0},{8,4},{12,8},{16,12},{20,16},{24,20},{28,24},{1,29},{... | collective-permute-start | bytes 196616 | tf_op jit(solution)/shard_map/ppermute | solution.py:116
  39.4 1.9 %collective-permute-done.9 = bf16[4,32,256]{2,1,0:T(8,128)(2,1)S(1)} collective-permute-done((bf16[4,32,256]{2,1,0:T(8,128)(2,1)S(1)}, bf16[4,32,256]{2,1,0:T(8,128)(2,1)S(1)}, u32[]{:S(2)}, u32[]{:S(2)}) %collective-permute-start.9) | collective-permute-done | bytes 65568 | tf_op jit(solution)/shard_map/ppermute | solution.py:116
  41.8 2.6 %shard_map.64 = bf16[512,1024]{1,0:T(8,128)(2,1)S(1)} custom-call(f32[512,1024]{1,0:T(8,128)S(1)} %convolution_multiply_fusion.s_ref, bf16[512,1024]{1,0:T(8,128)(2,1)S(1)} %reshape.115.g_ref), custom_call_target="tpu_custom_call" | custom-call | flops 15728640 | bytes 4194304 | tf_op jit(solution)/shard_map/pallas_call | solution.py:62
  45.6 2.8 %collective-permute-start.10 = (bf16[4,32,256]{2,1,0:T(8,128)(2,1)}, bf16[4,32,256]{2,1,0:T(8,128)(2,1)}, u32[]{:S(2)}, u32[]{:S(2)}) collective-permute-start(bf16[4,32,256]{2,1,0:T(8,128)(2,1)} %get-tuple-element.21), channel_id=1, source_target_pairs={{0,3},{1,0},{2,1},{3,2},{4,7},{5,4},{6,5},{7,6},{8,11},{9,8},{10,9... | collective-permute-start | bytes 196616 | tf_op jit(solution)/shard_map/ppermute | solution.py:153
  48.4 1.1 %collective-permute-start.11 = (bf16[4,32,256]{2,1,0:T(8,128)(2,1)}, bf16[4,32,256]{2,1,0:T(8,128)(2,1)}, u32[]{:S(2)}, u32[]{:S(2)}) collective-permute-start(bf16[4,32,256]{2,1,0:T(8,128)(2,1)} %get-tuple-element.23), channel_id=1, source_target_pairs={{0,2},{1,3},{2,0},{3,1},{4,6},{5,7},{6,4},{7,5},{8,10},{9,11},{10,... | collective-permute-start | bytes 196616 | tf_op jit(solution)/shard_map/ppermute | solution.py:153
  50.6 2.2 %collective-permute-start.18 = (bf16[4,32,256]{2,1,0:T(8,128)(2,1)S(1)}, bf16[4,32,256]{2,1,0:T(8,128)(2,1)S(1)}, u32[]{:S(2)}, u32[]{:S(2)}) collective-permute-start(bf16[4,32,256]{2,1,0:T(8,128)(2,1)S(1)} %get-tuple-element.6), channel_id=1, source_target_pairs={{0,8},{4,12},{8,16},{12,20},{16,24},{20,28},{24,0},{28,4},{1,9},{5... | collective-permute-start | bytes 196616 | tf_op jit(solution)/shard_map/ppermute | solution.py:163
  52.9 2.4 %collective-permute-done.12 = bf16[4,32,256]{2,1,0:T(8,128)(2,1)} collective-permute-done((bf16[4,32,256]{2,1,0:T(8,128)(2,1)}, bf16[4,32,256]{2,1,0:T(8,128)(2,1)}, u32[]{:S(2)}, u32[]{:S(2)}) %collective-permute-start.12) | collective-permute-done | bytes 65568 | tf_op jit(solution)/shard_map/ppermute | solution.py:153
  56.6 1.3 %collective-permute-start.13 = (bf16[4,32,256]{2,1,0:T(8,128)(2,1)S(1)}, bf16[4,32,256]{2,1,0:T(8,128)(2,1)S(1)}, u32[]{:S(2)}, u32[]{:S(2)}) collective-permute-start(bf16[4,32,256]{2,1,0:T(8,128)(2,1)S(1)} %get-tuple-element.11), channel_id=1, source_target_pairs={{0,28},{4,0},{8,4},{12,8},{16,12},{20,16},{24,20},{28,24},{1,29},{... | collective-permute-start | bytes 196616 | tf_op jit(solution)/shard_map/ppermute | solution.py:163
  57.8 0.9 %add_bitcast_fusion = f32[1,4,32,256]{3,2,1,0:T(8,128)S(1)} fusion(bf16[4,32,256]{2,1,0:T(8,128)(2,1)} %collective-permute-done.12, bf16[4,32,256]{2,1,0:T(8,128)(2,1)} %collective-permute-done.11, bf16[4,32,256]{2,1,0:T(8,128)(2,1)} %collective-permute-done.10, bf16[16,32,256]{2,1,0:T(8,128)(2,1)S(1)} %convolution_convert_fusion.3), kind=kLoop, calls=%fused_computation.12 | loop fusion | flops 229376 | bytes 393216
  58.8 0.9 %collective-permute-done.13 = bf16[4,32,256]{2,1,0:T(8,128)(2,1)S(1)} collective-permute-done((bf16[4,32,256]{2,1,0:T(8,128)(2,1)S(1)}, bf16[4,32,256]{2,1,0:T(8,128)(2,1)S(1)}, u32[]{:S(2)}, u32[]{:S(2)}) %collective-permute-start.13) | collective-permute-done | bytes 65568 | tf_op jit(solution)/shard_map/ppermute | solution.py:163
  60.0 4.7 %collective-permute-done.14 = bf16[4,32,256]{2,1,0:T(8,128)(2,1)S(1)} collective-permute-done((bf16[4,32,256]{2,1,0:T(8,128)(2,1)S(1)}, bf16[4,32,256]{2,1,0:T(8,128)(2,1)S(1)}, u32[]{:S(2)}, u32[]{:S(2)}) %collective-permute-start.14) | collective-permute-done | bytes 65568 | tf_op jit(solution)/shard_map/ppermute | solution.py:163
  65.2 3.2 %collective-permute-done.15 = bf16[4,32,256]{2,1,0:T(8,128)(2,1)S(1)} collective-permute-done((bf16[4,32,256]{2,1,0:T(8,128)(2,1)S(1)}, bf16[4,32,256]{2,1,0:T(8,128)(2,1)S(1)}, u32[]{:S(2)}, u32[]{:S(2)}) %collective-permute-start.15) | collective-permute-done | bytes 65568 | tf_op jit(solution)/shard_map/ppermute | solution.py:163
  69.4 0.9 %convolution_convert_fusion.4 = bf16[128,256]{1,0:T(8,128)(2,1)} fusion(bf16[256,256]{1,0:T(8,128)(2,1)S(1)} %copy-done.1, f32[128,256]{1,0:T(8,128)S(1)} %reshape.118, f32[128,256]{1,0:T(8,128)S(1)} %get-tuple-element.25, f32[128]{0:T(128)S(1)} %broadcast_multiply_fusion, f32[128]{0:T(128)S(1)} %add_rsqrt_fusion), kind=kOutput, calls=%fused_computation.7 | convolution fusion | flops 16973824 | bytes 459776 | tf_op jit(solution)/shard_map/nk,dk->nd/dot_general | solution.py:181
  (79 shorter events, 10.0 us)
Async XLA Ops:
  0.0 11.2 %copy-start = (bf16[128,1024]{1,0:T(8,128)(2,1)S(1)}, bf16[128,1024]{1,0:T(8,128)(2,1)}, u32[]{:S(2)}) copy-start(bf16[128,1024]{1,0:T(8,128)(2,1)} %param.8) | copy-start | bytes 786436
  0.0 11.1 %copy-start.2 = (s32[128]{0:T(128)S(1)}, s32[128]{0:T(128)}, u32[]{:S(2)}) copy-start(s32[128]{0:T(128)} %param.10) | copy-start | bytes 1540
  0.0 11.1 %copy-start.3 = (s32[128]{0:T(128)S(1)}, s32[128]{0:T(128)}, u32[]{:S(2)}) copy-start(s32[128]{0:T(128)} %param.9) | copy-start | bytes 1540
  1.4 39.9 %collective-permute-start.2 = (bf16[4,32,256]{2,1,0:T(8,128)(2,1)S(1)}, bf16[4,32,256]{2,1,0:T(8,128)(2,1)S(1)}, u32[]{:S(2)}, u32[]{:S(2)}) collective-permute-start(bf16[4,32,256]{2,1,0:T(8,128)(2,1)S(1)} %bitcast.77), channel_id=1, source_target_pairs={{0,3},{1,0},{2,1},{3,2},{4,7},{5,4},{6,5},{7,6},{8,11},{9,8},{10,9... | collective-permute-start | bytes 196616 | tf_op jit(solution)/shard_map/ppermute | solution.py:93
  6.5 34.8 %collective-permute-start.1 = (bf16[4,32,256]{2,1,0:T(8,128)(2,1)S(1)}, bf16[4,32,256]{2,1,0:T(8,128)(2,1)S(1)}, u32[]{:S(2)}, u32[]{:S(2)}) collective-permute-start(bf16[4,32,256]{2,1,0:T(8,128)(2,1)S(1)} %bitcast.78), channel_id=1, source_target_pairs={{0,2},{1,3},{2,0},{3,1},{4,6},{5,7},{6,4},{7,5},{8,10},{9,11},{10,... | collective-permute-start | bytes 196616 | tf_op jit(solution)/shard_map/ppermute | solution.py:93
  6.5 34.8 %collective-permute-start = (bf16[4,32,256]{2,1,0:T(8,128)(2,1)S(1)}, bf16[4,32,256]{2,1,0:T(8,128)(2,1)S(1)}, u32[]{:S(2)}, u32[]{:S(2)}) collective-permute-start(bf16[4,32,256]{2,1,0:T(8,128)(2,1)S(1)} %bitcast.79), channel_id=1, source_target_pairs={{0,1},{1,2},{2,3},{3,0},{4,5},{5,6},{6,7},{7,4},{8,9},{9,10},{10,1... | collective-permute-start | bytes 196616 | tf_op jit(solution)/shard_map/ppermute | solution.py:93
  9.5 18.7 %collective-permute-start.3 = (bf16[4,32,256]{2,1,0:T(8,128)(2,1)S(1)}, bf16[4,32,256]{2,1,0:T(8,128)(2,1)S(1)}, u32[]{:S(2)}, u32[]{:S(2)}) collective-permute-start(bf16[4,32,256]{2,1,0:T(8,128)(2,1)S(1)} %bitcast.96), channel_id=1, source_target_pairs={{0,4},{4,8},{8,12},{12,16},{16,20},{20,24},{24,28},{28,0},{1,5},{5... | collective-permute-start | bytes 196616 | tf_op jit(solution)/shard_map/ppermute | solution.py:116
  9.6 21.1 %collective-permute-start.4 = (bf16[4,32,256]{2,1,0:T(8,128)(2,1)S(1)}, bf16[4,32,256]{2,1,0:T(8,128)(2,1)S(1)}, u32[]{:S(2)}, u32[]{:S(2)}) collective-permute-start(bf16[4,32,256]{2,1,0:T(8,128)(2,1)S(1)} %bitcast.94), channel_id=1, source_target_pairs={{0,8},{4,12},{8,16},{12,20},{16,24},{20,28},{24,0},{28,4},{1,9},{5... | collective-permute-start | bytes 196616 | tf_op jit(solution)/shard_map/ppermute | solution.py:116
  28.2 4.4 %collective-permute-start.5 = (bf16[4,32,256]{2,1,0:T(8,128)(2,1)S(1)}, bf16[4,32,256]{2,1,0:T(8,128)(2,1)S(1)}, u32[]{:S(2)}, u32[]{:S(2)}) collective-permute-start(bf16[4,32,256]{2,1,0:T(8,128)(2,1)S(1)} %bitcast.97), channel_id=1, source_target_pairs={{0,12},{4,16},{8,20},{12,24},{16,28},{20,0},{24,4},{28,8},{1,13},{... | collective-permute-start | bytes 196616 | tf_op jit(solution)/shard_map/ppermute | solution.py:116
  30.7 4.4 %collective-permute-start.6 = (bf16[4,32,256]{2,1,0:T(8,128)(2,1)S(1)}, bf16[4,32,256]{2,1,0:T(8,128)(2,1)S(1)}, u32[]{:S(2)}, u32[]{:S(2)}) collective-permute-start(bf16[4,32,256]{2,1,0:T(8,128)(2,1)S(1)} %bitcast.95), channel_id=1, source_target_pairs={{0,16},{4,20},{8,24},{12,28},{16,0},{20,4},{24,8},{28,12},{1,17},{... | collective-permute-start | bytes 196616 | tf_op jit(solution)/shard_map/ppermute | solution.py:116
  32.5 4.0 %collective-permute-start.7 = (bf16[4,32,256]{2,1,0:T(8,128)(2,1)S(1)}, bf16[4,32,256]{2,1,0:T(8,128)(2,1)S(1)}, u32[]{:S(2)}, u32[]{:S(2)}) collective-permute-start(bf16[4,32,256]{2,1,0:T(8,128)(2,1)S(1)} %bitcast.93), channel_id=1, source_target_pairs={{0,20},{4,24},{8,28},{12,0},{16,4},{20,8},{24,12},{28,16},{1,21},{... | collective-permute-start | bytes 196616 | tf_op jit(solution)/shard_map/ppermute | solution.py:116
  35.0 4.4 %collective-permute-start.8 = (bf16[4,32,256]{2,1,0:T(8,128)(2,1)S(1)}, bf16[4,32,256]{2,1,0:T(8,128)(2,1)S(1)}, u32[]{:S(2)}, u32[]{:S(2)}) collective-permute-start(bf16[4,32,256]{2,1,0:T(8,128)(2,1)S(1)} %bitcast.92), channel_id=1, source_target_pairs={{0,24},{4,28},{8,0},{12,4},{16,8},{20,12},{24,16},{28,20},{1,25},{... | collective-permute-start | bytes 196616 | tf_op jit(solution)/shard_map/ppermute | solution.py:116
  36.6 4.7 %collective-permute-start.9 = (bf16[4,32,256]{2,1,0:T(8,128)(2,1)S(1)}, bf16[4,32,256]{2,1,0:T(8,128)(2,1)S(1)}, u32[]{:S(2)}, u32[]{:S(2)}) collective-permute-start(bf16[4,32,256]{2,1,0:T(8,128)(2,1)S(1)} %bitcast.91), channel_id=1, source_target_pairs={{0,28},{4,0},{8,4},{12,8},{16,12},{20,16},{24,20},{28,24},{1,29},{... | collective-permute-start | bytes 196616 | tf_op jit(solution)/shard_map/ppermute | solution.py:116
  45.6 7.2 %collective-permute-start.10 = (bf16[4,32,256]{2,1,0:T(8,128)(2,1)}, bf16[4,32,256]{2,1,0:T(8,128)(2,1)}, u32[]{:S(2)}, u32[]{:S(2)}) collective-permute-start(bf16[4,32,256]{2,1,0:T(8,128)(2,1)} %get-tuple-element.21), channel_id=1, source_target_pairs={{0,3},{1,0},{2,1},{3,2},{4,7},{5,4},{6,5},{7,6},{8,11},{9,8},{10,9... | collective-permute-start | bytes 196616 | tf_op jit(solution)/shard_map/ppermute | solution.py:153
  48.4 6.9 %collective-permute-start.12 = (bf16[4,32,256]{2,1,0:T(8,128)(2,1)}, bf16[4,32,256]{2,1,0:T(8,128)(2,1)}, u32[]{:S(2)}, u32[]{:S(2)}) collective-permute-start(bf16[4,32,256]{2,1,0:T(8,128)(2,1)} %get-tuple-element.22), channel_id=1, source_target_pairs={{0,1},{1,2},{2,3},{3,0},{4,5},{5,6},{6,7},{7,4},{8,9},{9,10},{10,1... | collective-permute-start | bytes 196616 | tf_op jit(solution)/shard_map/ppermute | solution.py:153
  48.4 8.2 %collective-permute-start.11 = (bf16[4,32,256]{2,1,0:T(8,128)(2,1)}, bf16[4,32,256]{2,1,0:T(8,128)(2,1)}, u32[]{:S(2)}, u32[]{:S(2)}) collective-permute-start(bf16[4,32,256]{2,1,0:T(8,128)(2,1)} %get-tuple-element.23), channel_id=1, source_target_pairs={{0,2},{1,3},{2,0},{3,1},{4,6},{5,7},{6,4},{7,5},{8,10},{9,11},{10,... | collective-permute-start | bytes 196616 | tf_op jit(solution)/shard_map/ppermute | solution.py:153
  50.5 17.9 %collective-permute-start.19 = (bf16[4,32,256]{2,1,0:T(8,128)(2,1)S(1)}, bf16[4,32,256]{2,1,0:T(8,128)(2,1)S(1)}, u32[]{:S(2)}, u32[]{:S(2)}) collective-permute-start(bf16[4,32,256]{2,1,0:T(8,128)(2,1)S(1)} %get-tuple-element.5), channel_id=1, source_target_pairs={{0,4},{4,8},{8,12},{12,16},{16,20},{20,24},{24,28},{28,0},{1,5},{5... | collective-permute-start | bytes 196616 | tf_op jit(solution)/shard_map/ppermute | solution.py:163
  50.6 17.8 %collective-permute-start.18 = (bf16[4,32,256]{2,1,0:T(8,128)(2,1)S(1)}, bf16[4,32,256]{2,1,0:T(8,128)(2,1)S(1)}, u32[]{:S(2)}, u32[]{:S(2)}) collective-permute-start(bf16[4,32,256]{2,1,0:T(8,128)(2,1)S(1)} %get-tuple-element.6), channel_id=1, source_target_pairs={{0,8},{4,12},{8,16},{12,20},{16,24},{20,28},{24,0},{28,4},{1,9},{5... | collective-permute-start | bytes 196616 | tf_op jit(solution)/shard_map/ppermute | solution.py:163
  52.8 15.6 %collective-permute-start.17 = (bf16[4,32,256]{2,1,0:T(8,128)(2,1)S(1)}, bf16[4,32,256]{2,1,0:T(8,128)(2,1)S(1)}, u32[]{:S(2)}, u32[]{:S(2)}) collective-permute-start(bf16[4,32,256]{2,1,0:T(8,128)(2,1)S(1)} %get-tuple-element.7), channel_id=1, source_target_pairs={{0,12},{4,16},{8,20},{12,24},{16,28},{20,0},{24,4},{28,8},{1,13},{... | collective-permute-start | bytes 196616 | tf_op jit(solution)/shard_map/ppermute | solution.py:163
  55.3 13.1 %collective-permute-start.16 = (bf16[4,32,256]{2,1,0:T(8,128)(2,1)S(1)}, bf16[4,32,256]{2,1,0:T(8,128)(2,1)S(1)}, u32[]{:S(2)}, u32[]{:S(2)}) collective-permute-start(bf16[4,32,256]{2,1,0:T(8,128)(2,1)S(1)} %get-tuple-element.8), channel_id=1, source_target_pairs={{0,16},{4,20},{8,24},{12,28},{16,0},{20,4},{24,8},{28,12},{1,17},{... | collective-permute-start | bytes 196616 | tf_op jit(solution)/shard_map/ppermute | solution.py:163
  56.6 12.9 %copy-start.1 = (bf16[256,256]{1,0:T(8,128)(2,1)S(1)}, bf16[256,256]{1,0:T(8,128)(2,1)}, u32[]{:S(2)}) copy-start(bf16[256,256]{1,0:T(8,128)(2,1)} %param.7) | copy-start | bytes 393220
  56.6 3.2 %collective-permute-start.13 = (bf16[4,32,256]{2,1,0:T(8,128)(2,1)S(1)}, bf16[4,32,256]{2,1,0:T(8,128)(2,1)S(1)}, u32[]{:S(2)}, u32[]{:S(2)}) collective-permute-start(bf16[4,32,256]{2,1,0:T(8,128)(2,1)S(1)} %get-tuple-element.11), channel_id=1, source_target_pairs={{0,28},{4,0},{8,4},{12,8},{16,12},{20,16},{24,20},{28,24},{1,29},{... | collective-permute-start | bytes 196616 | tf_op jit(solution)/shard_map/ppermute | solution.py:163
  59.7 5.0 %collective-permute-start.14 = (bf16[4,32,256]{2,1,0:T(8,128)(2,1)S(1)}, bf16[4,32,256]{2,1,0:T(8,128)(2,1)S(1)}, u32[]{:S(2)}, u32[]{:S(2)}) collective-permute-start(bf16[4,32,256]{2,1,0:T(8,128)(2,1)S(1)} %get-tuple-element.10), channel_id=1, source_target_pairs={{0,24},{4,28},{8,0},{12,4},{16,8},{20,12},{24,16},{28,20},{1,25},{... | collective-permute-start | bytes 196616 | tf_op jit(solution)/shard_map/ppermute | solution.py:163
  64.7 3.7 %collective-permute-start.15 = (bf16[4,32,256]{2,1,0:T(8,128)(2,1)S(1)}, bf16[4,32,256]{2,1,0:T(8,128)(2,1)S(1)}, u32[]{:S(2)}, u32[]{:S(2)}) collective-permute-start(bf16[4,32,256]{2,1,0:T(8,128)(2,1)S(1)} %get-tuple-element.9), channel_id=1, source_target_pairs={{0,20},{4,24},{8,28},{12,0},{16,4},{20,8},{24,12},{28,16},{1,21},{... | collective-permute-start | bytes 196616 | tf_op jit(solution)/shard_map/ppermute | solution.py:163

commit v3 on v2

--- a/solution.py
+++ b/solution.py
@@ -43,11 +43,24 @@
     return jnp.broadcast_to(total, (rows // group, group, width)).reshape(rows, width)
 
 
-def softmax_bwd_kernel(group, score_scale, s_ref, g_ref, d_ref):
+def softmax_bwd_kernel(group, score_scale, recv, edge_at_ref, s_ref, m_ref, d_ref, g_scr):
+    block = pl.program_id(0)
+    firsts = s_ref.shape[0] // group
+
+    def place(first, carry):
+        row = pl.multiple_of(first * group, group)
+        base = (block * firsts + first) * recv
+        for second in range(recv):
+            g_scr[pl.ds(row, group), second * group : (second + 1) * group] = m_ref[
+                edge_at_ref[base + second]
+            ].astype(jnp.float32)
+        return carry
+
+    lax.fori_loop(0, firsts, place, 0)
     expo = jnp.exp(s_ref[...])
     rows = expo / lane_group_sum(expo, group)
     cols = expo / row_group_sum(expo, group)
-    grads = g_ref[...].astype(jnp.float32)
+    grads = g_scr[...]
     d_rows = grads * cols
     d_cols = grads * rows
     d_scores = rows * (d_rows - lane_group_sum(d_rows * rows, group)) + cols * (
@@ -56,25 +69,30 @@
     d_ref[...] = (d_scores * score_scale).astype(jnp.bfloat16)
 
 
-def softmax_bwd(scores, grads, group, score_scale):
+def softmax_bwd(scores, edge_at, blocks, group, score_scale):
     total_rows, width = scores.shape
+    recv = width // group
     block = 128 if total_rows % 128 == 0 else total_rows
     return pl.pallas_call(
-        functools.partial(softmax_bwd_kernel, group, score_scale),
+        functools.partial(softmax_bwd_kernel, group, score_scale, recv),
         out_shape=jax.ShapeDtypeStruct((total_rows, width), jnp.bfloat16),
-        grid=(total_rows // block,),
-        in_specs=[
-            pl.BlockSpec((block, width), lambda b: (b, 0)),
-            pl.BlockSpec((block, width), lambda b: (b, 0)),
-        ],
-        out_specs=pl.BlockSpec((block, width), lambda b: (b, 0)),
+        grid_spec=pltpu.PrefetchScalarGridSpec(
+            num_scalar_prefetch=1,
+            grid=(total_rows // block,),
+            in_specs=[
+                pl.BlockSpec((block, width), lambda b, e: (b, 0)),
+                pl.BlockSpec(blocks.shape, lambda b, e: (0, 0, 0)),
+            ],
+            out_specs=pl.BlockSpec((block, width), lambda b, e: (b, 0)),
+            scratch_shapes=[pltpu.VMEM((block, width), jnp.float32)],
+        ),
         compiler_params=pltpu.CompilerParams(vmem_limit_bytes=48 * 1024 * 1024),
         cost_estimate=pl.CostEstimate(
             flops=30 * total_rows * width,
             transcendentals=total_rows * width,
-            bytes_accessed=8 * total_rows * width,
+            bytes_accessed=6 * total_rows * width,
         ),
-    )(scores, grads)
+    )(edge_at, scores, blocks)
 
 
 def local(n_grp, n_sub, tokens, proj_weight, match_grad, edge_first, pair_second_image, send_pick):
@@ -124,12 +142,19 @@
         second_at = pair_second_image
 
     pair_at = first_at * recv + second_at
-    scatter = (
-        lax.broadcasted_iota(jnp.int32, (group_img * recv, edge_count), 0) == pair_at[None, :]
-    ).astype(jnp.bfloat16)
-    grads = jnp.dot(scatter, match_grad, preferred_element_type=jnp.float32).astype(jnp.bfloat16)
-    grads = grads.reshape(group_img, recv, length, length).transpose(0, 2, 1, 3)
-    grads = grads.reshape(group_img * length, recv * length)
+    edge_ids = jnp.arange(edge_count, dtype=jnp.int32)
+    edge_at = jnp.min(
+        jnp.where(
+            lax.broadcasted_iota(jnp.int32, (group_img * recv, edge_count), 0) == pair_at[None, :],
+            edge_ids[None, :],
+            edge_count,
+        ),
+        axis=1,
+    )
+    blocks = jnp.concatenate(
+        [match_grad.reshape(edge_count, length, length), jnp.zeros((1, length, length), match_grad.dtype)],
+        axis=0,
+    )
     pool2 = pool.reshape(group_img * length, feat_width)
     recv2 = received.reshape(recv * length, feat_width)
     score_scale = 1.0 / (feat_width * SOFTMAX_COOLING)
@@ -137,7 +162,7 @@
         lax.dot_general(pool2, recv2, (((1,), (1,)), ((), ())), preferred_element_type=jnp.float32)
         * score_scale
     )
-    d_scaled = softmax_bwd(scores, grads, length, score_scale)
+    d_scaled = softmax_bwd(scores, edge_at, blocks, length, score_scale)
     pool_total = jnp.dot(d_scaled, recv2, preferred_element_type=jnp.float32).reshape(
         group_img, length, feat_width
     )

time: 70.6 us -> 57.6 us (0.82)
  local copies, waits for them, and re-layouts: 19.9 us -> 5.56 us
  Pallas kernels: 2.6 us -> 5.09 us
  waiting for transfers between devices: 15.9 us -> 16.8 us
  other arithmetic: 1.33 us -> 0.58 us
    reshape x3 -> x1, local copies, waits for them, and re-layouts: 16.4 us -> 1.45 us  [local(): match_grad.reshape(edge_count, length, length)]
    pallas_call x1, Pallas kernels: 2.6 us -> 5.09 us  [softmax_bwd(): pl.pallas_call(functools.partial(softmax_bwd_kernel, group, score_scale,...]
    ppermute x7, starting transfers between devices: 10.6 us -> 8.57 us  [local(): lax.ppermute(outgoing[k * slots:(k + 1) * slots], 'grp', shift(n_grp, k))]
    ppermute x7, starting transfers between devices: 4.92 us -> 6.3 us  [local(): lax.ppermute(slot_b[k * slots:(k + 1) * slots], 'grp', shift(n_grp, -k))]
    ppermute x7, waiting for transfers between devices: 4.08 us -> 5.4 us  [local(): lax.ppermute(outgoing[k * slots:(k + 1) * slots], 'grp', shift(n_grp, k))]
    ppermute x3, waiting for transfers between devices: 3.06 us -> 1.96 us  [local(): lax.ppermute(pool_b[k * img_count:(k + 1) * img_count], 'sub', shift(n_su...]
    unnamed x30 -> x31, local copies, waits for them, and re-layouts: 0.55 us -> 1.62 us
    unnamed x1, other arithmetic: 0.94 us -> 0.03 us
  transfers between devices with their start and end apart: 20 -> 20, of which waited for: 9 -> 11; matrix products, arithmetic and copies ran while one was open for 30% -> 9% of each run, Pallas kernels for 0% -> 0%
where the time goes in v3:
time: 57.6 us; the launch traced here: 57.4 us
  starting transfers between devices  25 us (43%)
  waiting for transfers between devices  16.8 us (29%)
  local copies, waits for them, and re-layouts  5.56 us (10%)
  Pallas kernels  5.09 us (9%)
  matrix products  3.94 us (7%)
  other arithmetic  0.58 us (1%)
    ppermute x7, waiting for transfers between devices, local(): lax.ppermute(slot_b[k * slots:(k + 1) * slots], 'grp', shift(n_grp, -k))  9.47 us
    ppermute x7, starting transfers between devices, local(): lax.ppermute(outgoing[k * slots:(k + 1) * slots], 'grp', shift(n_grp, k))  8.57 us
    ppermute x7, starting transfers between devices, local(): lax.ppermute(slot_b[k * slots:(k + 1) * slots], 'grp', shift(n_grp, -k))  6.3 us
    ppermute x3, starting transfers between devices, local(): lax.ppermute(normed_b, 'sub', shift(n_sub, k))  6.14 us
    ppermute x7, waiting for transfers between devices, local(): lax.ppermute(outgoing[k * slots:(k + 1) * slots], 'grp', shift(n_grp, k))  5.4 us
    pallas_call x1, Pallas kernels, softmax_bwd(): pl.pallas_call(functools.partial(softmax_bwd_kernel, group, score_scale,...  5.09 us
    ppermute x3, starting transfers between devices, local(): lax.ppermute(pool_b[k * img_count:(k + 1) * img_count], 'sub', shift(n_su...  3.99 us
    ppermute x3, waiting for transfers between devices, local(): lax.ppermute(pool_b[k * img_count:(k + 1) * img_count], 'sub', shift(n_su...  1.96 us
  transfers between devices with their start and end apart: 20, of which 11 were waited for; matrix products, arithmetic and copies ran while one was open for 9% of the time, Pallas kernels for 0%

profile of v3, /device:TPU:0, one launch (start us, length us, event | category | flops | bytes accessed | tf_op | source)
XLA Modules:
  0.0 57.4 jit_solution(12939095089221600809)
XLA Ops:
  0.0 0.9 %copy-done = bf16[256,256]{1,0:T(8,128)(2,1)S(1)} copy-done((bf16[256,256]{1,0:T(8,128)(2,1)S(1)}, bf16[256,256]{1,0:T(8,128)(2,1)}, u32[]{:S(2)}) %copy-start) | copy-done | bytes 131096
  0.9 1.1 %multiply_reduce_fusion.1 = (f32[128]{0:T(128)S(1)}, f32[128,256]{1,0:T(8,128)S(1)}) fusion(bf16[128,256]{1,0:T(8,128)(2,1)} %bitcast.85, bf16[256,256]{1,0:T(8,128)(2,1)S(1)} %copy-done), kind=kOutput, calls=%fused_computation.12 | convolution fusion | flops 16842624 | bytes 328192 | tf_op jit(solution)/shard_map/dot_general | solution.py:18
  2.1 5.1 %collective-permute-start.2 = (bf16[4,32,256]{2,1,0:T(8,128)(2,1)S(1)}, bf16[4,32,256]{2,1,0:T(8,128)(2,1)S(1)}, u32[]{:S(2)}, u32[]{:S(2)}) collective-permute-start(bf16[4,32,256]{2,1,0:T(8,128)(2,1)S(1)} %bitcast.72), channel_id=1, source_target_pairs={{0,3},{1,0},{2,1},{3,2},{4,7},{5,4},{6,5},{7,6},{8,11},{9,8},{10,9... | collective-permute-start | bytes 196616 | tf_op jit(solution)/shard_map/ppermute | solution.py:111
  7.3 1.0 %collective-permute-start = (bf16[4,32,256]{2,1,0:T(8,128)(2,1)S(1)}, bf16[4,32,256]{2,1,0:T(8,128)(2,1)S(1)}, u32[]{:S(2)}, u32[]{:S(2)}) collective-permute-start(bf16[4,32,256]{2,1,0:T(8,128)(2,1)S(1)} %bitcast.74), channel_id=1, source_target_pairs={{0,1},{1,2},{2,3},{3,0},{4,5},{5,6},{6,7},{7,4},{8,9},{9,10},{10,1... | collective-permute-start | bytes 196616 | tf_op jit(solution)/shard_map/ppermute | solution.py:111
  10.3 1.5 %collective-permute-start.4 = (bf16[4,32,256]{2,1,0:T(8,128)(2,1)S(1)}, bf16[4,32,256]{2,1,0:T(8,128)(2,1)S(1)}, u32[]{:S(2)}, u32[]{:S(2)}) collective-permute-start(bf16[4,32,256]{2,1,0:T(8,128)(2,1)S(1)} %bitcast.90), channel_id=1, source_target_pairs={{0,8},{4,12},{8,16},{12,20},{16,24},{20,28},{24,0},{28,4},{1,9},{5... | collective-permute-start | bytes 196616 | tf_op jit(solution)/shard_map/ppermute | solution.py:134
  12.2 1.4 %copy.12 = bf16[128,32,32]{2,1,0:T(8,128)(2,1)S(1)} copy(bf16[128,32,32]{0,2,1:T(8,128)(2,1)S(1)} %bitcast.68) | data formatting | bytes 524288 | tf_op jit(solution)/shard_map/reshape | solution.py:155
  14.9 1.6 %collective-permute-start.5 = (bf16[4,32,256]{2,1,0:T(8,128)(2,1)S(1)}, bf16[4,32,256]{2,1,0:T(8,128)(2,1)S(1)}, u32[]{:S(2)}, u32[]{:S(2)}) collective-permute-start(bf16[4,32,256]{2,1,0:T(8,128)(2,1)S(1)} %bitcast.92), channel_id=1, source_target_pairs={{0,12},{4,16},{8,20},{12,24},{16,28},{20,0},{24,4},{28,8},{1,13},{... | collective-permute-start | bytes 196616 | tf_op jit(solution)/shard_map/ppermute | solution.py:134
  17.3 1.4 %collective-permute-done.5 = bf16[4,32,256]{2,1,0:T(8,128)(2,1)S(1)} collective-permute-done((bf16[4,32,256]{2,1,0:T(8,128)(2,1)S(1)}, bf16[4,32,256]{2,1,0:T(8,128)(2,1)S(1)}, u32[]{:S(2)}, u32[]{:S(2)}) %collective-permute-start.5) | collective-permute-done | bytes 65568 | tf_op jit(solution)/shard_map/ppermute | solution.py:134
  18.6 1.6 %collective-permute-start.7 = (bf16[4,32,256]{2,1,0:T(8,128)(2,1)S(1)}, bf16[4,32,256]{2,1,0:T(8,128)(2,1)S(1)}, u32[]{:S(2)}, u32[]{:S(2)}) collective-permute-start(bf16[4,32,256]{2,1,0:T(8,128)(2,1)S(1)} %bitcast.88), channel_id=1, source_target_pairs={{0,20},{4,24},{8,28},{12,0},{16,4},{20,8},{24,12},{28,16},{1,21},{... | collective-permute-start | bytes 196616 | tf_op jit(solution)/shard_map/ppermute | solution.py:134
  20.3 1.1 %collective-permute-done.6 = bf16[4,32,256]{2,1,0:T(8,128)(2,1)S(1)} collective-permute-done((bf16[4,32,256]{2,1,0:T(8,128)(2,1)S(1)}, bf16[4,32,256]{2,1,0:T(8,128)(2,1)S(1)}, u32[]{:S(2)}, u32[]{:S(2)}) %collective-permute-start.6) | collective-permute-done | bytes 65568 | tf_op jit(solution)/shard_map/ppermute | solution.py:134
  21.4 1.0 %collective-permute-start.8 = (bf16[4,32,256]{2,1,0:T(8,128)(2,1)S(1)}, bf16[4,32,256]{2,1,0:T(8,128)(2,1)S(1)}, u32[]{:S(2)}, u32[]{:S(2)}) collective-permute-start(bf16[4,32,256]{2,1,0:T(8,128)(2,1)S(1)} %bitcast.87), channel_id=1, source_target_pairs={{0,24},{4,28},{8,0},{12,4},{16,8},{20,12},{24,16},{28,20},{1,25},{... | collective-permute-start | bytes 196616 | tf_op jit(solution)/shard_map/ppermute | solution.py:134
  22.5 2.1 %collective-permute-start.9 = (bf16[4,32,256]{2,1,0:T(8,128)(2,1)S(1)}, bf16[4,32,256]{2,1,0:T(8,128)(2,1)S(1)}, u32[]{:S(2)}, u32[]{:S(2)}) collective-permute-start(bf16[4,32,256]{2,1,0:T(8,128)(2,1)S(1)} %bitcast.86), channel_id=1, source_target_pairs={{0,28},{4,0},{8,4},{12,8},{16,12},{20,16},{24,20},{28,24},{1,29},{... | collective-permute-start | bytes 196616 | tf_op jit(solution)/shard_map/ppermute | solution.py:134
  24.6 1.0 %collective-permute-done.8 = bf16[4,32,256]{2,1,0:T(8,128)(2,1)S(1)} collective-permute-done((bf16[4,32,256]{2,1,0:T(8,128)(2,1)S(1)}, bf16[4,32,256]{2,1,0:T(8,128)(2,1)S(1)}, u32[]{:S(2)}, u32[]{:S(2)}) %collective-permute-start.8) | collective-permute-done | bytes 65568 | tf_op jit(solution)/shard_map/ppermute | solution.py:134
  27.0 5.1 %shard_map.64 = bf16[512,1024]{1,0:T(8,128)(2,1)S(1)} custom-call(s32[512]{0:T(512)S(1)} %select_reduce_fusion.edge_at_ref, f32[512,1024]{1,0:T(8,128)S(1)} %convolution_multiply_fusion.s_ref, bf16[129,32,32]{2,1,0:T(8,128)(2,1)S(1)} %concatenate.14.m_ref), custom_call_target="tpu_custom_call" | custom-call | flops 15728640 | bytes 3145728 | tf_op jit(solution)/shard_map/pallas_call | solution.py:76
  32.6 2.9 %collective-permute-start.10 = (bf16[4,32,256]{2,1,0:T(8,128)(2,1)S(1)}, bf16[4,32,256]{2,1,0:T(8,128)(2,1)S(1)}, u32[]{:S(2)}, u32[]{:S(2)}) collective-permute-start(bf16[4,32,256]{2,1,0:T(8,128)(2,1)S(1)} %get-tuple-element.21), channel_id=1, source_target_pairs={{0,3},{1,0},{2,1},{3,2},{4,7},{5,4},{6,5},{7,6},{8,11},{9,8},{10,9... | collective-permute-start | bytes 196616 | tf_op jit(solution)/shard_map/ppermute | solution.py:178
  35.5 1.1 %collective-permute-start.11 = (bf16[4,32,256]{2,1,0:T(8,128)(2,1)S(1)}, bf16[4,32,256]{2,1,0:T(8,128)(2,1)S(1)}, u32[]{:S(2)}, u32[]{:S(2)}) collective-permute-start(bf16[4,32,256]{2,1,0:T(8,128)(2,1)S(1)} %get-tuple-element.23), channel_id=1, source_target_pairs={{0,2},{1,3},{2,0},{3,1},{4,6},{5,7},{6,4},{7,5},{8,10},{9,11},{10,... | collective-permute-start | bytes 196616 | tf_op jit(solution)/shard_map/ppermute | solution.py:178
  38.2 2.4 %collective-permute-start.18 = (bf16[4,32,256]{2,1,0:T(8,128)(2,1)S(1)}, bf16[4,32,256]{2,1,0:T(8,128)(2,1)S(1)}, u32[]{:S(2)}, u32[]{:S(2)}) collective-permute-start(bf16[4,32,256]{2,1,0:T(8,128)(2,1)S(1)} %get-tuple-element.6), channel_id=1, source_target_pairs={{0,8},{4,12},{8,16},{12,20},{16,24},{20,28},{24,0},{28,4},{1,9},{5... | collective-permute-start | bytes 196616 | tf_op jit(solution)/shard_map/ppermute | solution.py:188
  40.7 1.6 %collective-permute-done.12 = bf16[4,32,256]{2,1,0:T(8,128)(2,1)S(1)} collective-permute-done((bf16[4,32,256]{2,1,0:T(8,128)(2,1)S(1)}, bf16[4,32,256]{2,1,0:T(8,128)(2,1)S(1)}, u32[]{:S(2)}, u32[]{:S(2)}) %collective-permute-start.12) | collective-permute-done | bytes 65568 | tf_op jit(solution)/shard_map/ppermute | solution.py:178
  42.3 1.3 %collective-permute-start.16 = (bf16[4,32,256]{2,1,0:T(8,128)(2,1)S(1)}, bf16[4,32,256]{2,1,0:T(8,128)(2,1)S(1)}, u32[]{:S(2)}, u32[]{:S(2)}) collective-permute-start(bf16[4,32,256]{2,1,0:T(8,128)(2,1)S(1)} %get-tuple-element.8), channel_id=1, source_target_pairs={{0,16},{4,20},{8,24},{12,28},{16,0},{20,4},{24,8},{28,12},{1,17},{... | collective-permute-start | bytes 196616 | tf_op jit(solution)/shard_map/ppermute | solution.py:188
  44.8 1.8 %collective-permute-done.13 = bf16[4,32,256]{2,1,0:T(8,128)(2,1)S(1)} collective-permute-done((bf16[4,32,256]{2,1,0:T(8,128)(2,1)S(1)}, bf16[4,32,256]{2,1,0:T(8,128)(2,1)S(1)}, u32[]{:S(2)}, u32[]{:S(2)}) %collective-permute-start.13) | collective-permute-done | bytes 65568 | tf_op jit(solution)/shard_map/ppermute | solution.py:188
  46.7 4.2 %collective-permute-done.14 = bf16[4,32,256]{2,1,0:T(8,128)(2,1)S(1)} collective-permute-done((bf16[4,32,256]{2,1,0:T(8,128)(2,1)S(1)}, bf16[4,32,256]{2,1,0:T(8,128)(2,1)S(1)}, u32[]{:S(2)}, u32[]{:S(2)}) %collective-permute-start.14) | collective-permute-done | bytes 65568 | tf_op jit(solution)/shard_map/ppermute | solution.py:188
  51.0 1.1 %collective-permute-start.15 = (bf16[4,32,256]{2,1,0:T(8,128)(2,1)S(1)}, bf16[4,32,256]{2,1,0:T(8,128)(2,1)S(1)}, u32[]{:S(2)}, u32[]{:S(2)}) collective-permute-start(bf16[4,32,256]{2,1,0:T(8,128)(2,1)S(1)} %get-tuple-element.9), channel_id=1, source_target_pairs={{0,20},{4,24},{8,28},{12,0},{16,4},{20,8},{24,12},{28,16},{1,21},{... | collective-permute-start | bytes 196616 | tf_op jit(solution)/shard_map/ppermute | solution.py:188
  52.0 3.4 %collective-permute-done.15 = bf16[4,32,256]{2,1,0:T(8,128)(2,1)S(1)} collective-permute-done((bf16[4,32,256]{2,1,0:T(8,128)(2,1)S(1)}, bf16[4,32,256]{2,1,0:T(8,128)(2,1)S(1)}, u32[]{:S(2)}, u32[]{:S(2)}) %collective-permute-start.15) | collective-permute-done | bytes 65568 | tf_op jit(solution)/shard_map/ppermute | solution.py:188
  56.5 0.9 %convolution_convert_fusion.3 = bf16[128,256]{1,0:T(8,128)(2,1)} fusion(bf16[256,256]{1,0:T(8,128)(2,1)S(1)} %copy-done, f32[128,256]{1,0:T(8,128)S(1)} %reshape.114, f32[128,256]{1,0:T(8,128)S(1)} %get-tuple-element.25, f32[128]{0:T(128)S(1)} %broadcast_multiply_fusion, f32[128]{0:T(128)S(1)} %add_rsqrt_fusion), kind=kOutput, calls=%fused_computation.5 | convolution fusion | flops 16973824 | bytes 459776 | tf_op jit(solution)/shard_map/nk,dk->nd/dot_general | solution.py:206
  (79 shorter events, 10.3 us)
Async XLA Ops:
  0.0 0.9 %copy-start = (bf16[256,256]{1,0:T(8,128)(2,1)S(1)}, bf16[256,256]{1,0:T(8,128)(2,1)}, u32[]{:S(2)}) copy-start(bf16[256,256]{1,0:T(8,128)(2,1)} %param.7) | copy-start | bytes 393220
  0.0 11.9 %copy-start.1 = (bf16[128,1024]{1,0:T(8,128)(2,1)S(1)}, bf16[128,1024]{1,0:T(8,128)(2,1)}, u32[]{:S(2)}) copy-start(bf16[128,1024]{1,0:T(8,128)(2,1)} %param.8) | copy-start | bytes 786436
  2.1 24.4 %collective-permute-start.2 = (bf16[4,32,256]{2,1,0:T(8,128)(2,1)S(1)}, bf16[4,32,256]{2,1,0:T(8,128)(2,1)S(1)}, u32[]{:S(2)}, u32[]{:S(2)}) collective-permute-start(bf16[4,32,256]{2,1,0:T(8,128)(2,1)S(1)} %bitcast.72), channel_id=1, source_target_pairs={{0,3},{1,0},{2,1},{3,2},{4,7},{5,4},{6,5},{7,6},{8,11},{9,8},{10,9... | collective-permute-start | bytes 196616 | tf_op jit(solution)/shard_map/ppermute | solution.py:111
  7.2 19.2 %collective-permute-start.1 = (bf16[4,32,256]{2,1,0:T(8,128)(2,1)S(1)}, bf16[4,32,256]{2,1,0:T(8,128)(2,1)S(1)}, u32[]{:S(2)}, u32[]{:S(2)}) collective-permute-start(bf16[4,32,256]{2,1,0:T(8,128)(2,1)S(1)} %bitcast.73), channel_id=1, source_target_pairs={{0,2},{1,3},{2,0},{3,1},{4,6},{5,7},{6,4},{7,5},{8,10},{9,11},{10,... | collective-permute-start | bytes 196616 | tf_op jit(solution)/shard_map/ppermute | solution.py:111
  7.3 19.3 %collective-permute-start = (bf16[4,32,256]{2,1,0:T(8,128)(2,1)S(1)}, bf16[4,32,256]{2,1,0:T(8,128)(2,1)S(1)}, u32[]{:S(2)}, u32[]{:S(2)}) collective-permute-start(bf16[4,32,256]{2,1,0:T(8,128)(2,1)S(1)} %bitcast.74), channel_id=1, source_target_pairs={{0,1},{1,2},{2,3},{3,0},{4,5},{5,6},{6,7},{7,4},{8,9},{9,10},{10,1... | collective-permute-start | bytes 196616 | tf_op jit(solution)/shard_map/ppermute | solution.py:111
  10.3 4.7 %collective-permute-start.3 = (bf16[4,32,256]{2,1,0:T(8,128)(2,1)S(1)}, bf16[4,32,256]{2,1,0:T(8,128)(2,1)S(1)}, u32[]{:S(2)}, u32[]{:S(2)}) collective-permute-start(bf16[4,32,256]{2,1,0:T(8,128)(2,1)S(1)} %bitcast.91), channel_id=1, source_target_pairs={{0,4},{4,8},{8,12},{12,16},{16,20},{20,24},{24,28},{28,0},{1,5},{5... | collective-permute-start | bytes 196616 | tf_op jit(solution)/shard_map/ppermute | solution.py:134
  10.3 6.2 %collective-permute-start.4 = (bf16[4,32,256]{2,1,0:T(8,128)(2,1)S(1)}, bf16[4,32,256]{2,1,0:T(8,128)(2,1)S(1)}, u32[]{:S(2)}, u32[]{:S(2)}) collective-permute-start(bf16[4,32,256]{2,1,0:T(8,128)(2,1)S(1)} %bitcast.90), channel_id=1, source_target_pairs={{0,8},{4,12},{8,16},{12,20},{16,24},{20,28},{24,0},{28,4},{1,9},{5... | collective-permute-start | bytes 196616 | tf_op jit(solution)/shard_map/ppermute | solution.py:134
  12.1 1.8 %copy-start.2 = (s32[128]{0:T(128)S(1)}, s32[128]{0:T(128)}, u32[]{:S(2)}) copy-start(s32[128]{0:T(128)} %param.10) | copy-start | bytes 1540
  12.1 1.8 %copy-start.3 = (s32[128]{0:T(128)S(1)}, s32[128]{0:T(128)}, u32[]{:S(2)}) copy-start(s32[128]{0:T(128)} %param.9) | copy-start | bytes 1540
  14.9 3.7 %collective-permute-start.5 = (bf16[4,32,256]{2,1,0:T(8,128)(2,1)S(1)}, bf16[4,32,256]{2,1,0:T(8,128)(2,1)S(1)}, u32[]{:S(2)}, u32[]{:S(2)}) collective-permute-start(bf16[4,32,256]{2,1,0:T(8,128)(2,1)S(1)} %bitcast.92), channel_id=1, source_target_pairs={{0,12},{4,16},{8,20},{12,24},{16,28},{20,0},{24,4},{28,8},{1,13},{... | collective-permute-start | bytes 196616 | tf_op jit(solution)/shard_map/ppermute | solution.py:134
  16.6 4.8 %collective-permute-start.6 = (bf16[4,32,256]{2,1,0:T(8,128)(2,1)S(1)}, bf16[4,32,256]{2,1,0:T(8,128)(2,1)S(1)}, u32[]{:S(2)}, u32[]{:S(2)}) collective-permute-start(bf16[4,32,256]{2,1,0:T(8,128)(2,1)S(1)} %bitcast.89), channel_id=1, source_target_pairs={{0,16},{4,20},{8,24},{12,28},{16,0},{20,4},{24,8},{28,12},{1,17},{... | collective-permute-start | bytes 196616 | tf_op jit(solution)/shard_map/ppermute | solution.py:134
  18.6 3.8 %collective-permute-start.7 = (bf16[4,32,256]{2,1,0:T(8,128)(2,1)S(1)}, bf16[4,32,256]{2,1,0:T(8,128)(2,1)S(1)}, u32[]{:S(2)}, u32[]{:S(2)}) collective-permute-start(bf16[4,32,256]{2,1,0:T(8,128)(2,1)S(1)} %bitcast.88), channel_id=1, source_target_pairs={{0,20},{4,24},{8,28},{12,0},{16,4},{20,8},{24,12},{28,16},{1,21},{... | collective-permute-start | bytes 196616 | tf_op jit(solution)/shard_map/ppermute | solution.py:134
  21.4 4.3 %collective-permute-start.8 = (bf16[4,32,256]{2,1,0:T(8,128)(2,1)S(1)}, bf16[4,32,256]{2,1,0:T(8,128)(2,1)S(1)}, u32[]{:S(2)}, u32[]{:S(2)}) collective-permute-start(bf16[4,32,256]{2,1,0:T(8,128)(2,1)S(1)} %bitcast.87), channel_id=1, source_target_pairs={{0,24},{4,28},{8,0},{12,4},{16,8},{20,12},{24,16},{28,20},{1,25},{... | collective-permute-start | bytes 196616 | tf_op jit(solution)/shard_map/ppermute | solution.py:134
  22.5 4.0 %collective-permute-start.9 = (bf16[4,32,256]{2,1,0:T(8,128)(2,1)S(1)}, bf16[4,32,256]{2,1,0:T(8,128)(2,1)S(1)}, u32[]{:S(2)}, u32[]{:S(2)}) collective-permute-start(bf16[4,32,256]{2,1,0:T(8,128)(2,1)S(1)} %bitcast.86), channel_id=1, source_target_pairs={{0,28},{4,0},{8,4},{12,8},{16,12},{20,16},{24,20},{28,24},{1,29},{... | collective-permute-start | bytes 196616 | tf_op jit(solution)/shard_map/ppermute | solution.py:134
  32.6 7.9 %collective-permute-start.10 = (bf16[4,32,256]{2,1,0:T(8,128)(2,1)S(1)}, bf16[4,32,256]{2,1,0:T(8,128)(2,1)S(1)}, u32[]{:S(2)}, u32[]{:S(2)}) collective-permute-start(bf16[4,32,256]{2,1,0:T(8,128)(2,1)S(1)} %get-tuple-element.21), channel_id=1, source_target_pairs={{0,3},{1,0},{2,1},{3,2},{4,7},{5,4},{6,5},{7,6},{8,11},{9,8},{10,9... | collective-permute-start | bytes 196616 | tf_op jit(solution)/shard_map/ppermute | solution.py:178
  35.5 6.9 %collective-permute-start.12 = (bf16[4,32,256]{2,1,0:T(8,128)(2,1)S(1)}, bf16[4,32,256]{2,1,0:T(8,128)(2,1)S(1)}, u32[]{:S(2)}, u32[]{:S(2)}) collective-permute-start(bf16[4,32,256]{2,1,0:T(8,128)(2,1)S(1)} %get-tuple-element.22), channel_id=1, source_target_pairs={{0,1},{1,2},{2,3},{3,0},{4,5},{5,6},{6,7},{7,4},{8,9},{9,10},{10,1... | collective-permute-start | bytes 196616 | tf_op jit(solution)/shard_map/ppermute | solution.py:178
  35.5 8.5 %collective-permute-start.11 = (bf16[4,32,256]{2,1,0:T(8,128)(2,1)S(1)}, bf16[4,32,256]{2,1,0:T(8,128)(2,1)S(1)}, u32[]{:S(2)}, u32[]{:S(2)}) collective-permute-start(bf16[4,32,256]{2,1,0:T(8,128)(2,1)S(1)} %get-tuple-element.23), channel_id=1, source_target_pairs={{0,2},{1,3},{2,0},{3,1},{4,6},{5,7},{6,4},{7,5},{8,10},{9,11},{10,... | collective-permute-start | bytes 196616 | tf_op jit(solution)/shard_map/ppermute | solution.py:178
  37.6 18.0 %collective-permute-start.19 = (bf16[4,32,256]{2,1,0:T(8,128)(2,1)S(1)}, bf16[4,32,256]{2,1,0:T(8,128)(2,1)S(1)}, u32[]{:S(2)}, u32[]{:S(2)}) collective-permute-start(bf16[4,32,256]{2,1,0:T(8,128)(2,1)S(1)} %get-tuple-element.5), channel_id=1, source_target_pairs={{0,4},{4,8},{8,12},{12,16},{16,20},{20,24},{24,28},{28,0},{1,5},{5... | collective-permute-start | bytes 196616 | tf_op jit(solution)/shard_map/ppermute | solution.py:188
  38.2 17.4 %collective-permute-start.18 = (bf16[4,32,256]{2,1,0:T(8,128)(2,1)S(1)}, bf16[4,32,256]{2,1,0:T(8,128)(2,1)S(1)}, u32[]{:S(2)}, u32[]{:S(2)}) collective-permute-start(bf16[4,32,256]{2,1,0:T(8,128)(2,1)S(1)} %get-tuple-element.6), channel_id=1, source_target_pairs={{0,8},{4,12},{8,16},{12,20},{16,24},{20,28},{24,0},{28,4},{1,9},{5... | collective-permute-start | bytes 196616 | tf_op jit(solution)/shard_map/ppermute | solution.py:188
  40.5 15.0 %collective-permute-start.17 = (bf16[4,32,256]{2,1,0:T(8,128)(2,1)S(1)}, bf16[4,32,256]{2,1,0:T(8,128)(2,1)S(1)}, u32[]{:S(2)}, u32[]{:S(2)}) collective-permute-start(bf16[4,32,256]{2,1,0:T(8,128)(2,1)S(1)} %get-tuple-element.7), channel_id=1, source_target_pairs={{0,12},{4,16},{8,20},{12,24},{16,28},{20,0},{24,4},{28,8},{1,13},{... | collective-permute-start | bytes 196616 | tf_op jit(solution)/shard_map/ppermute | solution.py:188
  42.3 13.2 %collective-permute-start.16 = (bf16[4,32,256]{2,1,0:T(8,128)(2,1)S(1)}, bf16[4,32,256]{2,1,0:T(8,128)(2,1)S(1)}, u32[]{:S(2)}, u32[]{:S(2)}) collective-permute-start(bf16[4,32,256]{2,1,0:T(8,128)(2,1)S(1)} %get-tuple-element.8), channel_id=1, source_target_pairs={{0,16},{4,20},{8,24},{12,28},{16,0},{20,4},{24,8},{28,12},{1,17},{... | collective-permute-start | bytes 196616 | tf_op jit(solution)/shard_map/ppermute | solution.py:188
  43.9 2.7 %collective-permute-start.13 = (bf16[4,32,256]{2,1,0:T(8,128)(2,1)S(1)}, bf16[4,32,256]{2,1,0:T(8,128)(2,1)S(1)}, u32[]{:S(2)}, u32[]{:S(2)}) collective-permute-start(bf16[4,32,256]{2,1,0:T(8,128)(2,1)S(1)} %get-tuple-element.11), channel_id=1, source_target_pairs={{0,28},{4,0},{8,4},{12,8},{16,12},{20,16},{24,20},{28,24},{1,29},{... | collective-permute-start | bytes 196616 | tf_op jit(solution)/shard_map/ppermute | solution.py:188
  46.6 4.4 %collective-permute-start.14 = (bf16[4,32,256]{2,1,0:T(8,128)(2,1)S(1)}, bf16[4,32,256]{2,1,0:T(8,128)(2,1)S(1)}, u32[]{:S(2)}, u32[]{:S(2)}) collective-permute-start(bf16[4,32,256]{2,1,0:T(8,128)(2,1)S(1)} %get-tuple-element.10), channel_id=1, source_target_pairs={{0,24},{4,28},{8,0},{12,4},{16,8},{20,12},{24,16},{28,20},{1,25},{... | collective-permute-start | bytes 196616 | tf_op jit(solution)/shard_map/ppermute | solution.py:188
  51.0 4.5 %collective-permute-start.15 = (bf16[4,32,256]{2,1,0:T(8,128)(2,1)S(1)}, bf16[4,32,256]{2,1,0:T(8,128)(2,1)S(1)}, u32[]{:S(2)}, u32[]{:S(2)}) collective-permute-start(bf16[4,32,256]{2,1,0:T(8,128)(2,1)S(1)} %get-tuple-element.9), channel_id=1, source_target_pairs={{0,20},{4,24},{8,28},{12,0},{16,4},{20,8},{24,12},{28,16},{1,21},{... | collective-permute-start | bytes 196616 | tf_op jit(solution)/shard_map/ppermute | solution.py:188

commit v4 on v3

--- a/solution.py
+++ b/solution.py
@@ -10,7 +10,7 @@
 EPSILON = 1e-05
 SOFTMAX_COOLING = 0.1
 SUB_MODE = "perm"
-GRP_MODE = "perm"
+GRP_MODE = "a2a"
 
 
 def normalize(tokens, proj_weight):
@@ -112,8 +112,13 @@
             axis=0,
         )
         first_at = ((sub_at - edge_first // img_count) % n_sub) * img_count + edge_first % img_count
-    else:
+    elif SUB_MODE == "gather":
         pool = lax.all_gather(normed_b, "sub", axis=0, tiled=True)
+        first_at = edge_first
+    else:
+        pool = lax.all_to_all(
+            jnp.concatenate([normed_b] * n_sub, axis=0), "sub", split_axis=0, concat_axis=0, tiled=True
+        )
         first_at = edge_first
 
     picks = send_pick.reshape(n_grp, slots)
@@ -178,6 +183,9 @@
             owned = owned + lax.ppermute(
                 pool_b[k * img_count : (k + 1) * img_count], "sub", shift(n_sub, -k)
             ).astype(jnp.float32)
+    elif SUB_MODE == "a2a":
+        back = lax.all_to_all(pool_b, "sub", split_axis=0, concat_axis=0, tiled=True).astype(jnp.float32)
+        owned = jnp.sum(back.reshape(n_sub, img_count, length, feat_width), axis=0)
     else:
         owned = lax.psum_scatter(pool_b, "sub", scatter_dimension=0, tiled=True).astype(jnp.float32)
 

time: 57.6 us -> 48.2 us (0.84)
  starting transfers between devices: 25 us -> 17.4 us
  waiting for transfers between devices: 16.8 us -> 14.4 us
  matrix products: 3.94 us -> 5.4 us
  local copies, waits for them, and re-layouts: 5.56 us -> 4.73 us
    ppermute x14 -> x0, waiting for transfers between devices: 14.9 us -> none  [the longest x7 9.47 us: local(): lax.ppermute(slot_b[k * slots:(k + 1) * slots], 'grp', shift(n_grp, -k))]
    ppermute x14 -> x0, starting transfers between devices: 14.9 us -> none  [the longest x7 8.57 us: local(): lax.ppermute(outgoing[k * slots:(k + 1) * slots], 'grp', shift(n_grp, k))]
    all_to_all x0 -> x2, waiting for transfers between devices: none -> 7.57 us  [the longest x1 7.56 us: local(): lax.all_to_all(outgoing, 'grp', split_axis=0, concat_axis=0, tiled=True)]
    all_to_all x0 -> x2, starting transfers between devices: none -> 7.22 us  [the longest x1 3.73 us: local(): lax.all_to_all(outgoing, 'grp', split_axis=0, concat_axis=0, tiled=True)]
    ppermute x3, waiting for transfers between devices: 1.96 us -> 6.84 us  [local(): lax.ppermute(pool_b[k * img_count:(k + 1) * img_count], 'sub', shift(n_su...]
    dot_general x1, matrix products: 0.43 us -> 1.24 us  [local(): lax.dot_general(d_scaled, pool2, (((0,), (0,)), ((), ())), preferred_elem...]
    unnamed x31 -> x14, local copies, waits for them, and re-layouts: 1.62 us -> 2.4 us
    reshape x1 -> x0, local copies, waits for them, and re-layouts: 0.73 us -> none  [local(): picks = send_pick.reshape(n_grp, slots)]
  transfers between devices with their start and end apart: 20 -> 8, of which waited for: 11 -> 4; matrix products, arithmetic and copies ran while one was open for 9% -> 10% of each run, Pallas kernels for 0% -> 0%
where the time goes in v4:
time: 48.2 us; the launch traced here: 47.8 us
  starting transfers between devices  17.4 us (36%)
  waiting for transfers between devices  14.4 us (30%)
  matrix products  5.4 us (11%)
  Pallas kernels  5.09 us (11%)
  local copies, waits for them, and re-layouts  4.73 us (10%)
  other arithmetic  0.57 us (1%)
    all_to_all x1, waiting for transfers between devices, local(): lax.all_to_all(outgoing, 'grp', split_axis=0, concat_axis=0, tiled=True)  7.56 us
    ppermute x3, waiting for transfers between devices, local(): lax.ppermute(pool_b[k * img_count:(k + 1) * img_count], 'sub', shift(n_su...  6.84 us
    ppermute x3, starting transfers between devices, local(): lax.ppermute(normed_b, 'sub', shift(n_sub, k))  6.14 us
    pallas_call x1, Pallas kernels, softmax_bwd(): pl.pallas_call(functools.partial(softmax_bwd_kernel, group, score_scale,...  5.09 us
    ppermute x3, starting transfers between devices, local(): lax.ppermute(pool_b[k * img_count:(k + 1) * img_count], 'sub', shift(n_su...  4 us
    all_to_all x1, starting transfers between devices, local(): lax.all_to_all(outgoing, 'grp', split_axis=0, concat_axis=0, tiled=True)  3.73 us
    all_to_all x1, starting transfers between devices, local(): lax.all_to_all(slot_b, 'grp', split_axis=0, concat_axis=0, tiled=True)  3.49 us
    unnamed x14, local copies, waits for them, and re-layouts  2.4 us
  transfers between devices with their start and end apart: 8, of which 4 were waited for; matrix products, arithmetic and copies ran while one was open for 10% of the time, Pallas kernels for 0%

profile of v4, /device:TPU:0, one launch (start us, length us, event | category | flops | bytes accessed | tf_op | source)
XLA Modules:
  0.0 47.8 jit_solution(12749586040716890088)
XLA Ops:
  0.0 0.9 %copy-done = bf16[256,256]{1,0:T(8,128)(2,1)S(1)} copy-done((bf16[256,256]{1,0:T(8,128)(2,1)S(1)}, bf16[256,256]{1,0:T(8,128)(2,1)}, u32[]{:S(2)}) %copy-start) | copy-done | bytes 131096
  0.9 1.1 %multiply_reduce_fusion.1 = (f32[128]{0:T(128)S(1)}, f32[128,256]{1,0:T(8,128)S(1)}) fusion(bf16[128,256]{1,0:T(8,128)(2,1)} %bitcast.47, bf16[256,256]{1,0:T(8,128)(2,1)S(1)} %copy-done), kind=kOutput, calls=%fused_computation.11 | convolution fusion | flops 16842624 | bytes 328192 | tf_op jit(solution)/shard_map/dot_general | solution.py:18
  2.1 5.1 %collective-permute-start.2 = (bf16[4,32,256]{2,1,0:T(8,128)(2,1)S(1)}, bf16[4,32,256]{2,1,0:T(8,128)(2,1)S(1)}, u32[]{:S(2)}, u32[]{:S(2)}) collective-permute-start(bf16[4,32,256]{2,1,0:T(8,128)(2,1)S(1)} %bitcast.42), channel_id=1, source_target_pairs={{0,3},{1,0},{2,1},{3,2},{4,7},{5,4},{6,5},{7,6},{8,11},{9,8},{10,9... | collective-permute-start | bytes 196616 | tf_op jit(solution)/shard_map/ppermute | solution.py:111
  7.3 1.0 %collective-permute-start = (bf16[4,32,256]{2,1,0:T(8,128)(2,1)S(1)}, bf16[4,32,256]{2,1,0:T(8,128)(2,1)S(1)}, u32[]{:S(2)}, u32[]{:S(2)}) collective-permute-start(bf16[4,32,256]{2,1,0:T(8,128)(2,1)S(1)} %bitcast.44), channel_id=1, source_target_pairs={{0,1},{1,2},{2,3},{3,0},{4,5},{5,6},{6,7},{7,4},{8,9},{9,10},{10,1... | collective-permute-start | bytes 196616 | tf_op jit(solution)/shard_map/ppermute | solution.py:111
  8.3 1.0 %convolution_convert_fusion = bf16[32,8192]{1,0:T(8,128)(2,1)S(1)} fusion(bf16[4,8192]{1,0:T(4,128)(2,1)S(1)} %reshape_reshape.3, s32[32]{0:T(128)} %param.11), kind=kOutput, calls=%fused_computation | convolution fusion | flops 2359424 | bytes 589952 | tf_op jit(solution)/shard_map/dot_general | solution.py:133
  9.3 0.9 %copy.14 = bf16[4,8,32,256]{3,2,1,0:T(8,128)(2,1)} copy(bf16[4,8,32,256]{3,1,2,0:T(8,128)(2,1)S(1)} %bitcast.37) | data formatting | bytes 1048576
  10.2 3.7 %all-to-all-start = ((bf16[32,32,256]{2,1,0:T(8,128)(2,1)}), bf16[32,32,256]{2,1,0:T(8,128)(2,1)S(1)}, u32[]{:S(2)}, u32[]{:S(2)}) async-start(bf16[32,32,256]{2,1,0:T(8,128)(2,1)} %bitcast.14), calls=%async_computation | async-start | bytes 1048576 | tf_op jit(solution)/shard_map/all_to_all | solution.py:146
  14.2 1.4 %copy.12 = bf16[128,32,32]{2,1,0:T(8,128)(2,1)S(1)} copy(bf16[128,32,32]{0,2,1:T(8,128)(2,1)S(1)} %bitcast.41) | data formatting | bytes 524288 | tf_op jit(solution)/shard_map/reshape | solution.py:160
  15.6 0.2 concatenate.7.m_ref
  16.1 7.6 %all-to-all-done = bf16[32,32,256]{2,1,0:T(8,128)(2,1)S(1)} async-done(((bf16[32,32,256]{2,1,0:T(8,128)(2,1)}), bf16[32,32,256]{2,1,0:T(8,128)(2,1)S(1)}, u32[]{:S(2)}, u32[]{:S(2)}) %all-to-all-start) | async-done | bytes 524320 | tf_op jit(solution)/shard_map/all_to_all | solution.py:146
  23.7 0.5 convolution_multiply_fusion.s_ref
  24.1 5.1 %shard_map.64 = bf16[512,1024]{1,0:T(8,128)(2,1)S(1)} custom-call(s32[512]{0:T(512)S(1)} %select_reduce_fusion.edge_at_ref, f32[512,1024]{1,0:T(8,128)S(1)} %convolution_multiply_fusion.s_ref, bf16[129,32,32]{2,1,0:T(8,128)(2,1)S(1)} %concatenate.7.m_ref), custom_call_target="tpu_custom_call" | custom-call | flops 15728640 | bytes 3145728 | tf_op jit(solution)/shard_map/pallas_call | solution.py:76
  29.2 0.5 %copy.13 = bf16[1024,512]{1,0:T(8,128)(2,1)S(1)} copy(bf16[1024,512]{0,1:T(8,128)(2,1)S(1)} %bitcast.31) | data formatting | bytes 2097152 | tf_op jit(solution)/shard_map/dot_general | solution.py:174
  29.8 1.2 %convolution_convert_fusion.1 = bf16[32,32,256]{2,1,0:T(8,128)(2,1)} fusion(bf16[32,32,512]{2,1,0:T(8,128)(2,1)S(1)} %bitcast.33, bf16[512,256,1]{1,0,2:T(8,128)(2,1)S(1)} %bitcast.35), kind=kOutput, calls=%fused_computation.2 | convolution fusion | flops 268697600 | bytes 1835008 | tf_op jit(solution)/shard_map/dot_general | solution.py:174
  31.0 3.5 %all-to-all-start.1 = ((bf16[32,32,256]{2,1,0:T(8,128)(2,1)}), bf16[32,32,256]{2,1,0:T(8,128)(2,1)S(1)}, u32[]{:S(2)}, u32[]{:S(2)}) async-start(bf16[32,32,256]{2,1,0:T(8,128)(2,1)} %convolution_convert_fusion.1), calls=%async_computation.1 | async-start | bytes 1048576 | tf_op jit(solution)/shard_map/all_to_all | solution.py:202
  34.5 0.4 convolution_convert_fusion.2
  35.0 2.9 %collective-permute-start.3 = (bf16[4,32,256]{2,1,0:T(8,128)(2,1)S(1)}, bf16[4,32,256]{2,1,0:T(8,128)(2,1)S(1)}, u32[]{:S(2)}, u32[]{:S(2)}) collective-permute-start(bf16[4,32,256]{2,1,0:T(8,128)(2,1)S(1)} %get-tuple-element.5), channel_id=1, source_target_pairs={{0,3},{1,0},{2,1},{3,2},{4,7},{5,4},{6,5},{7,6},{8,11},{9,8},{10,9... | collective-permute-start | bytes 196616 | tf_op jit(solution)/shard_map/ppermute | solution.py:183
  37.9 1.1 %collective-permute-start.4 = (bf16[4,32,256]{2,1,0:T(8,128)(2,1)S(1)}, bf16[4,32,256]{2,1,0:T(8,128)(2,1)S(1)}, u32[]{:S(2)}, u32[]{:S(2)}) collective-permute-start(bf16[4,32,256]{2,1,0:T(8,128)(2,1)S(1)} %get-tuple-element.7), channel_id=1, source_target_pairs={{0,2},{1,3},{2,0},{3,1},{4,6},{5,7},{6,4},{7,5},{8,10},{9,11},{10,... | collective-permute-start | bytes 196616 | tf_op jit(solution)/shard_map/ppermute | solution.py:183
  39.0 1.4 %collective-permute-done.3 = bf16[4,32,256]{2,1,0:T(8,128)(2,1)S(1)} collective-permute-done((bf16[4,32,256]{2,1,0:T(8,128)(2,1)S(1)}, bf16[4,32,256]{2,1,0:T(8,128)(2,1)S(1)}, u32[]{:S(2)}, u32[]{:S(2)}) %collective-permute-start.3) | collective-permute-done | bytes 65568 | tf_op jit(solution)/shard_map/ppermute | solution.py:183
  40.4 4.2 %collective-permute-done.5 = bf16[4,32,256]{2,1,0:T(8,128)(2,1)S(1)} collective-permute-done((bf16[4,32,256]{2,1,0:T(8,128)(2,1)S(1)}, bf16[4,32,256]{2,1,0:T(8,128)(2,1)S(1)}, u32[]{:S(2)}, u32[]{:S(2)}) %collective-permute-start.5) | collective-permute-done | bytes 65568 | tf_op jit(solution)/shard_map/ppermute | solution.py:183
  44.6 1.3 %collective-permute-done.4 = bf16[4,32,256]{2,1,0:T(8,128)(2,1)S(1)} collective-permute-done((bf16[4,32,256]{2,1,0:T(8,128)(2,1)S(1)}, bf16[4,32,256]{2,1,0:T(8,128)(2,1)S(1)}, u32[]{:S(2)}, u32[]{:S(2)}) %collective-permute-start.4) | collective-permute-done | bytes 65568 | tf_op jit(solution)/shard_map/ppermute | solution.py:183
  46.0 0.3 copy.16
  46.3 0.3 fusion.2
  47.0 0.9 %convolution_convert_fusion.3 = bf16[128,256]{1,0:T(8,128)(2,1)} fusion(bf16[256,256]{1,0:T(8,128)(2,1)S(1)} %copy-done, f32[128,256]{1,0:T(8,128)S(1)} %reshape.56, f32[128,256]{1,0:T(8,128)S(1)} %get-tuple-element.9, f32[128]{0:T(128)S(1)} %broadcast_multiply_fusion, f32[128]{0:T(128)S(1)} %add_rsqrt_fusion), kind=kOutput, calls=%fused_computation.4 | convolution fusion | flops 16973824 | bytes 459776 | tf_op jit(solution)/shard_map/nk,dk->nd/dot_general | solution.py:214
  (29 shorter events, 1.0 us)
Async XLA Ops:
  0.0 0.9 %copy-start = (bf16[256,256]{1,0:T(8,128)(2,1)S(1)}, bf16[256,256]{1,0:T(8,128)(2,1)}, u32[]{:S(2)}) copy-start(bf16[256,256]{1,0:T(8,128)(2,1)} %param.7) | copy-start | bytes 393220
  0.0 14.0 %copy-start.1 = (bf16[128,1024]{1,0:T(8,128)(2,1)S(1)}, bf16[128,1024]{1,0:T(8,128)(2,1)}, u32[]{:S(2)}) copy-start(bf16[128,1024]{1,0:T(8,128)(2,1)} %param.8) | copy-start | bytes 786436
  2.1 13.9 %collective-permute-start.2 = (bf16[4,32,256]{2,1,0:T(8,128)(2,1)S(1)}, bf16[4,32,256]{2,1,0:T(8,128)(2,1)S(1)}, u32[]{:S(2)}, u32[]{:S(2)}) collective-permute-start(bf16[4,32,256]{2,1,0:T(8,128)(2,1)S(1)} %bitcast.42), channel_id=1, source_target_pairs={{0,3},{1,0},{2,1},{3,2},{4,7},{5,4},{6,5},{7,6},{8,11},{9,8},{10,9... | collective-permute-start | bytes 196616 | tf_op jit(solution)/shard_map/ppermute | solution.py:111
  7.2 8.8 %collective-permute-start.1 = (bf16[4,32,256]{2,1,0:T(8,128)(2,1)S(1)}, bf16[4,32,256]{2,1,0:T(8,128)(2,1)S(1)}, u32[]{:S(2)}, u32[]{:S(2)}) collective-permute-start(bf16[4,32,256]{2,1,0:T(8,128)(2,1)S(1)} %bitcast.43), channel_id=1, source_target_pairs={{0,2},{1,3},{2,0},{3,1},{4,6},{5,7},{6,4},{7,5},{8,10},{9,11},{10,... | collective-permute-start | bytes 196616 | tf_op jit(solution)/shard_map/ppermute | solution.py:111
  7.3 8.8 %collective-permute-start = (bf16[4,32,256]{2,1,0:T(8,128)(2,1)S(1)}, bf16[4,32,256]{2,1,0:T(8,128)(2,1)S(1)}, u32[]{:S(2)}, u32[]{:S(2)}) collective-permute-start(bf16[4,32,256]{2,1,0:T(8,128)(2,1)S(1)} %bitcast.44), channel_id=1, source_target_pairs={{0,1},{1,2},{2,3},{3,0},{4,5},{5,6},{6,7},{7,4},{8,9},{9,10},{10,1... | collective-permute-start | bytes 196616 | tf_op jit(solution)/shard_map/ppermute | solution.py:111
  10.2 13.4 %all-to-all-start = ((bf16[32,32,256]{2,1,0:T(8,128)(2,1)}), bf16[32,32,256]{2,1,0:T(8,128)(2,1)S(1)}, u32[]{:S(2)}, u32[]{:S(2)}) async-start(bf16[32,32,256]{2,1,0:T(8,128)(2,1)} %bitcast.14), calls=%async_computation | async-start | bytes 1048576 | tf_op jit(solution)/shard_map/all_to_all | solution.py:146
  13.9 1.9 %copy-start.3 = (s32[128]{0:T(128)S(1)}, s32[128]{0:T(128)}, u32[]{:S(2)}) copy-start(s32[128]{0:T(128)} %param.10) | copy-start | bytes 1540
  14.0 1.9 %copy-start.4 = (s32[128]{0:T(128)S(1)}, s32[128]{0:T(128)}, u32[]{:S(2)}) copy-start(s32[128]{0:T(128)} %param.9) | copy-start | bytes 1540
  31.0 15.0 %all-to-all-start.1 = ((bf16[32,32,256]{2,1,0:T(8,128)(2,1)}), bf16[32,32,256]{2,1,0:T(8,128)(2,1)S(1)}, u32[]{:S(2)}, u32[]{:S(2)}) async-start(bf16[32,32,256]{2,1,0:T(8,128)(2,1)} %convolution_convert_fusion.1), calls=%async_computation.1 | async-start | bytes 1048576 | tf_op jit(solution)/shard_map/all_to_all | solution.py:202
  34.5 11.8 %copy-start.2 = (s32[32]{0:T(128)S(1)}, s32[32]{0:T(128)}, u32[]{:S(2)}) copy-start(s32[32]{0:T(128)} %param.11) | copy-start | bytes 388
  35.0 5.4 %collective-permute-start.3 = (bf16[4,32,256]{2,1,0:T(8,128)(2,1)S(1)}, bf16[4,32,256]{2,1,0:T(8,128)(2,1)S(1)}, u32[]{:S(2)}, u32[]{:S(2)}) collective-permute-start(bf16[4,32,256]{2,1,0:T(8,128)(2,1)S(1)} %get-tuple-element.5), channel_id=1, source_target_pairs={{0,3},{1,0},{2,1},{3,2},{4,7},{5,4},{6,5},{7,6},{8,11},{9,8},{10,9... | collective-permute-start | bytes 196616 | tf_op jit(solution)/shard_map/ppermute | solution.py:183
  37.9 6.7 %collective-permute-start.5 = (bf16[4,32,256]{2,1,0:T(8,128)(2,1)S(1)}, bf16[4,32,256]{2,1,0:T(8,128)(2,1)S(1)}, u32[]{:S(2)}, u32[]{:S(2)}) collective-permute-start(bf16[4,32,256]{2,1,0:T(8,128)(2,1)S(1)} %get-tuple-element.6), channel_id=1, source_target_pairs={{0,1},{1,2},{2,3},{3,0},{4,5},{5,6},{6,7},{7,4},{8,9},{9,10},{10,1... | collective-permute-start | bytes 196616 | tf_op jit(solution)/shard_map/ppermute | solution.py:183
  37.9 8.0 %collective-permute-start.4 = (bf16[4,32,256]{2,1,0:T(8,128)(2,1)S(1)}, bf16[4,32,256]{2,1,0:T(8,128)(2,1)S(1)}, u32[]{:S(2)}, u32[]{:S(2)}) collective-permute-start(bf16[4,32,256]{2,1,0:T(8,128)(2,1)S(1)} %get-tuple-element.7), channel_id=1, source_target_pairs={{0,2},{1,3},{2,0},{3,1},{4,6},{5,7},{6,4},{7,5},{8,10},{9,11},{10,... | collective-permute-start | bytes 196616 | tf_op jit(solution)/shard_map/ppermute | solution.py:183

commit v5 on v4

--- a/solution.py
+++ b/solution.py
@@ -108,7 +108,11 @@
 
     if SUB_MODE == "perm":
         pool = jnp.concatenate(
-            [normed_b] + [lax.ppermute(normed_b, "sub", shift(n_sub, k)) for k in range(1, n_sub)],
+            [normed_b]
+            + [
+                normalize(lax.ppermute(tokens, "sub", shift(n_sub, k)), proj_weight)[2]
+                for k in range(1, n_sub)
+            ],
             axis=0,
         )
         first_at = ((sub_at - edge_first // img_count) % n_sub) * img_count + edge_first % img_count
@@ -122,16 +126,13 @@
         first_at = edge_first
 
     picks = send_pick.reshape(n_grp, slots)
-    flat_b = normed_b.reshape(img_count, length * feat_width)
     if GRP_MODE == "perm":
         order = picks[(grp_at + jnp.arange(n_grp, dtype=jnp.int32)) % n_grp].reshape(recv)
     else:
         order = send_pick
-    pick_onehot = (order[:, None] == jnp.arange(img_count, dtype=jnp.int32)[None, :]).astype(
-        jnp.bfloat16
-    )
-    outgoing = jnp.dot(pick_onehot, flat_b, preferred_element_type=jnp.float32).astype(jnp.bfloat16)
-    outgoing = outgoing.reshape(recv, length, feat_width)
+    outgoing = jnp.broadcast_to(tokens[img_count - 1], (recv, length, feat_width))
+    for image in range(img_count - 2, -1, -1):
+        outgoing = jnp.where(order[:, None, None] == image, tokens[image], outgoing)
     if GRP_MODE == "perm":
         received = jnp.concatenate(
             [outgoing[:slots]]
@@ -143,7 +144,9 @@
         )
         second_at = ((grp_at - pair_second_image // slots) % n_grp) * slots + pair_second_image % slots
     else:
-        received = lax.all_to_all(outgoing, "grp", split_axis=0, concat_axis=0, tiled=True)
+        received = normalize(
+            lax.all_to_all(outgoing, "grp", split_axis=0, concat_axis=0, tiled=True), proj_weight
+        )[2]
         second_at = pair_second_image
 
     pair_at = first_at * recv + second_at
@@ -200,8 +203,9 @@
         )
     else:
         returned = lax.all_to_all(slot_b, "grp", split_axis=0, concat_axis=0, tiled=True)
-    incoming_gradient = owned.reshape(img_count, length * feat_width) + jnp.dot(
-        pick_onehot.T, returned.reshape(recv, length * feat_width), preferred_element_type=jnp.float32
+    slot_images = order[:, None, None, None] == jnp.arange(img_count, dtype=jnp.int32)[None, :, None, None]
+    incoming_gradient = owned + jnp.sum(
+        jnp.where(slot_images, returned.astype(jnp.float32)[:, None], 0.0), axis=0
     )
     incoming_gradient = incoming_gradient.reshape(img_count * length, feat_width)
     feature_grad = (

time: 48.2 us -> 45.8 us (0.950)
  waiting for transfers between devices: 14.4 us -> 10.6 us
  other arithmetic: 0.57 us -> 4.33 us
  local copies, waits for them, and re-layouts: 4.73 us -> 3.22 us
  starting transfers between devices: 17.4 us -> 16.6 us
    ppermute x3, waiting for transfers between devices: 6.84 us -> 0.01 us  [local(): lax.ppermute(pool_b[k * img_count:(k + 1) * img_count], 'sub', shift(n_su...]
    all_to_all x1, waiting for transfers between devices: 0.01 us -> 6.69 us  [local(): lax.all_to_all(slot_b, 'grp', split_axis=0, concat_axis=0, tiled=True)]
    all_to_all x1, waiting for transfers between devices: 7.56 us -> 3.88 us  [local(): lax.all_to_all(outgoing, 'grp', split_axis=0, concat_axis=0, tiled=True)]
    unnamed x14 -> x19, local copies, waits for them, and re-layouts: 2.4 us -> 0.21 us
    eq x0 -> x2, other arithmetic: none -> 1.98 us  [the longest x1 1.32 us: local(): order[:, None, None, None]]
    ppermute x3, starting transfers between devices: 4 us -> 2.4 us  [local(): lax.ppermute(pool_b[k * img_count:(k + 1) * img_count], 'sub', shift(n_su...]
    dot_general x2 -> x0, matrix products: 1.3 us -> none  [the longest x1 0.99 us: local(): jnp.dot(pick_onehot, flat_b, preferred_element_type=jnp.float32)]
    dot_general x1 -> x5, matrix products: 1.09 us -> 2.22 us  [normalize(): jnp.dot(tokens.reshape(image_count * length, feat_width), proj_weight, pr...]
  transfers between devices with their start and end apart: 8 -> 8, of which waited for: 4 -> 2; matrix products, arithmetic and copies ran while one was open for 10% -> 20% of each run, Pallas kernels for 0% -> 0%
where the time goes in v5:
time: 45.8 us; the launch traced here: 45.4 us
  starting transfers between devices  16.6 us (36%)
  waiting for transfers between devices  10.6 us (23%)
  matrix products  5.2 us (11%)
  Pallas kernels  5.09 us (11%)
  other arithmetic  4.33 us (9%)
  local copies, waits for them, and re-layouts  3.22 us (7%)
    ppermute x3, starting transfers between devices, local(): lax.ppermute(tokens, 'sub', shift(n_sub, k))  6.99 us
    all_to_all x1, waiting for transfers between devices, local(): lax.all_to_all(slot_b, 'grp', split_axis=0, concat_axis=0, tiled=True)  6.69 us
    pallas_call x1, Pallas kernels, softmax_bwd(): pl.pallas_call(functools.partial(softmax_bwd_kernel, group, score_scale,...  5.09 us
    all_to_all x1, waiting for transfers between devices, local(): lax.all_to_all(outgoing, 'grp', split_axis=0, concat_axis=0, tiled=True)  3.88 us
    all_to_all x1, starting transfers between devices, local(): lax.all_to_all(outgoing, 'grp', split_axis=0, concat_axis=0, tiled=True)  3.72 us
    all_to_all x1, starting transfers between devices, local(): lax.all_to_all(slot_b, 'grp', split_axis=0, concat_axis=0, tiled=True)  3.49 us
    ppermute x3, starting transfers between devices, local(): lax.ppermute(pool_b[k * img_count:(k + 1) * img_count], 'sub', shift(n_su...  2.4 us
    dot_general x5, matrix products, normalize(): jnp.dot(tokens.reshape(image_count * length, feat_width), proj_weight, pr...  2.22 us
  transfers between devices with their start and end apart: 8, of which 2 were waited for; matrix products, arithmetic and copies ran while one was open for 20% of the time, Pallas kernels for 0%

profile of v5, /device:TPU:0, one launch (start us, length us, event | category | flops | bytes accessed | tf_op | source)
XLA Modules:
  0.0 45.4 jit_solution(2120953755012351867)
XLA Ops:
  0.0 3.1 %collective-permute-start = (bf16[4,32,256]{2,1,0:T(8,128)(2,1)}, bf16[4,32,256]{2,1,0:T(8,128)(2,1)S(1)}, u32[]{:S(2)}, u32[]{:S(2)}) collective-permute-start(bf16[4,32,256]{2,1,0:T(8,128)(2,1)} %param.6), channel_id=1, source_target_pairs={{0,1},{1,2},{2,3},{3,0},{4,5},{5,6},{6,7},{7,4},{8,9},{9,10},{10,1... | collective-permute-start | bytes 196616 | tf_op jit(solution)/shard_map/ppermute | solution.py:113
  3.1 2.6 %collective-permute-start.1 = (bf16[4,32,256]{2,1,0:T(8,128)(2,1)}, bf16[4,32,256]{2,1,0:T(8,128)(2,1)S(1)}, u32[]{:S(2)}, u32[]{:S(2)}) collective-permute-start(bf16[4,32,256]{2,1,0:T(8,128)(2,1)} %param.6), channel_id=1, source_target_pairs={{0,2},{1,3},{2,0},{3,1},{4,6},{5,7},{6,4},{7,5},{8,10},{9,11},{10,... | collective-permute-start | bytes 196616 | tf_op jit(solution)/shard_map/ppermute | solution.py:113
  5.6 1.3 %collective-permute-start.2 = (bf16[4,32,256]{2,1,0:T(8,128)(2,1)}, bf16[4,32,256]{2,1,0:T(8,128)(2,1)S(1)}, u32[]{:S(2)}, u32[]{:S(2)}) collective-permute-start(bf16[4,32,256]{2,1,0:T(8,128)(2,1)} %param.6), channel_id=1, source_target_pairs={{0,3},{1,0},{2,1},{3,2},{4,7},{5,4},{6,5},{7,6},{8,11},{9,8},{10,9... | collective-permute-start | bytes 196616 | tf_op jit(solution)/shard_map/ppermute | solution.py:113
  7.0 0.8 %slice_bitcast_fusion.3 = (bf16[32,256]{1,0:T(8,128)(2,1)S(1)}, bf16[32,256]{1,0:T(8,128)(2,1)S(1)}, bf16[32,256]{1,0:T(8,128)(2,1)S(1)}, bf16[32,256]{1,0:T(8,128)(2,1)S(1)}) fusion(bf16[4,32,256]{2,1,0:T(8,128)(2,1)} %param.6), kind=kLoop, calls=%fused_computation.32 | loop fusion | bytes 131072 | tf_op jit(solution)/shard_map/squeeze | solution.py:135
  7.8 0.7 %broadcast_compare_fusion.2 = (pred[32]{0:T(512)(128)(4,1)S(1)}, pred[32]{0:T(512)(128)(4,1)S(1)}, pred[32]{0:T(512)(128)(4,1)S(1)}) fusion(s32[32]{0:T(128)} %param.11), kind=kLoop, calls=%fused_computation.52 | loop fusion | flops 96 | bytes 224 | tf_op jit(solution)/shard_map/eq | solution.py:135
  8.5 1.0 %select_select_fusion = bf16[32,32,256]{2,1,0:T(8,128)(2,1)} fusion(pred[32]{0:T(512)(128)(4,1)S(1)} %get-tuple-element.15, pred[32]{0:T(512)(128)(4,1)S(1)} %get-tuple-element.14, pred[32]{0:T(512)(128)(4,1)S(1)} %get-tuple-element.13, bf16[32,256]{1,0:T(8,128)(2,1)S(1)} %get-tuple-element.11, bf16[32,256]{1,0:T(8,128)(2,1)S(1)} %get-tuple-element.12, ...), kind=kLoop, calls=%fused_computation.7 | loop fusion | flops 786432 | bytes 589920 | tf_op jit(solution)/shard_map/jit(_where)/select_n | solution.py:135
  9.4 3.7 %all-to-all-start = ((bf16[32,32,256]{2,1,0:T(8,128)(2,1)}), bf16[32,32,256]{2,1,0:T(8,128)(2,1)S(1)}, u32[]{:S(2)}, u32[]{:S(2)}) async-start(bf16[32,32,256]{2,1,0:T(8,128)(2,1)} %select_select_fusion), calls=%async_computation | async-start | bytes 1048576 | tf_op jit(solution)/shard_map/all_to_all | solution.py:148
  13.1 1.3 %iota_compare_fusion.1 = pred[32,4]{1,0:T(8,128)(4,1)} fusion(s32[32]{0:T(128)} %param.11), kind=kLoop, calls=%fused_computation.28 | loop fusion | flops 128 | bytes 256 | tf_op jit(solution)/shard_map/eq | solution.py:206
  14.5 1.1 %multiply_reduce_fusion.4 = (f32[128]{0:T(128)S(1)}, f32[128,256]{1,0:T(8,128)S(1)}) fusion(bf16[128,256]{1,0:T(8,128)(2,1)} %bitcast.60, bf16[256,256]{1,0:T(8,128)(2,1)S(1)} %copy-done), kind=kOutput, calls=%fused_computation.26 | convolution fusion | flops 16842624 | bytes 328192 | tf_op jit(solution)/shard_map/dot_general | solution.py:18
  15.8 1.4 %copy.12 = bf16[128,32,32]{2,1,0:T(8,128)(2,1)S(1)} copy(bf16[128,32,32]{0,2,1:T(8,128)(2,1)S(1)} %bitcast.59) | data formatting | bytes 524288 | tf_op jit(solution)/shard_map/reshape | solution.py:163
  18.4 0.3 multiply_reduce_fusion.1
  19.0 3.9 %all-to-all-done = bf16[32,32,256]{2,1,0:T(8,128)(2,1)S(1)} async-done(((bf16[32,32,256]{2,1,0:T(8,128)(2,1)}), bf16[32,32,256]{2,1,0:T(8,128)(2,1)S(1)}, u32[]{:S(2)}, u32[]{:S(2)}) %all-to-all-start) | async-done | bytes 524320 | tf_op jit(solution)/shard_map/all_to_all | solution.py:148
  22.9 0.4 multiply_reduce_fusion
  23.2 0.4 convolution_multiply_fusion.s_ref
  23.7 5.1 %shard_map.64 = bf16[512,1024]{1,0:T(8,128)(2,1)S(1)} custom-call(s32[512]{0:T(512)S(1)} %select_reduce_fusion.1.edge_at_ref, f32[512,1024]{1,0:T(8,128)S(1)} %convolution_multiply_fusion.s_ref, bf16[129,32,32]{2,1,0:T(8,128)(2,1)S(1)} %concatenate.7.m_ref), custom_call_target="tpu_custom_call" | custom-call | flops 15728640 | bytes 3145728 | tf_op jit(solution)/shard_map/pallas_call | solution.py:76
  28.8 0.5 %copy.13 = bf16[1024,512]{1,0:T(8,128)(2,1)S(1)} copy(bf16[1024,512]{0,1:T(8,128)(2,1)S(1)} %bitcast.54) | data formatting | bytes 2097152 | tf_op jit(solution)/shard_map/dot_general | solution.py:177
  29.3 1.2 %convolution_convert_fusion = bf16[32,32,256]{2,1,0:T(8,128)(2,1)} fusion(bf16[32,32,512]{2,1,0:T(8,128)(2,1)S(1)} %bitcast.55, bf16[512,256,1]{1,0,2:T(8,128)(2,1)S(1)} %bitcast.57), kind=kOutput, calls=%fused_computation.2 | convolution fusion | flops 268697600 | bytes 1835008 | tf_op jit(solution)/shard_map/dot_general | solution.py:177
  30.6 3.5 %all-to-all-start.1 = ((bf16[32,32,256]{2,1,0:T(8,128)(2,1)}), bf16[32,32,256]{2,1,0:T(8,128)(2,1)S(1)}, u32[]{:S(2)}, u32[]{:S(2)}) async-start(bf16[32,32,256]{2,1,0:T(8,128)(2,1)} %convolution_convert_fusion), calls=%async_computation.1 | async-start | bytes 1048576 | tf_op jit(solution)/shard_map/all_to_all | solution.py:205
  34.1 0.5 %convolution_convert_fusion.1 = bf16[512,256]{1,0:T(8,128)(2,1)S(1)} fusion(bf16[512,1024]{1,0:T(8,128)(2,1)S(1)} %shard_map.64, f32[1024,256]{0,1:T(8,128)S(1)} %get-tuple-element.25, f32[1024]{0:T(1024)S(1)} %add_rsqrt_fusion), kind=kOutput, calls=%fused_computation.3 | convolution fusion | flops 269090816 | bytes 2363392 | tf_op jit(solution)/shard_map/dot_general | solution.py:174
  34.6 0.5 %collective-permute-start.3 = (bf16[4,32,256]{2,1,0:T(8,128)(2,1)S(1)}, bf16[4,32,256]{2,1,0:T(8,128)(2,1)S(1)}, u32[]{:S(2)}, u32[]{:S(2)}) collective-permute-start(bf16[4,32,256]{2,1,0:T(8,128)(2,1)S(1)} %bitcast.71), channel_id=1, source_target_pairs={{0,3},{1,0},{2,1},{3,2},{4,7},{5,4},{6,5},{7,6},{8,11},{9,8},{10,9... | collective-permute-start | bytes 196616 | tf_op jit(solution)/shard_map/ppermute | solution.py:186
  35.1 1.7 %collective-permute-start.4 = (bf16[4,32,256]{2,1,0:T(8,128)(2,1)S(1)}, bf16[4,32,256]{2,1,0:T(8,128)(2,1)S(1)}, u32[]{:S(2)}, u32[]{:S(2)}) collective-permute-start(bf16[4,32,256]{2,1,0:T(8,128)(2,1)S(1)} %bitcast.70), channel_id=1, source_target_pairs={{0,2},{1,3},{2,0},{3,1},{4,6},{5,7},{6,4},{7,5},{8,10},{9,11},{10,... | collective-permute-start | bytes 196616 | tf_op jit(solution)/shard_map/ppermute | solution.py:186
  37.0 6.7 %all-to-all-done.1 = bf16[32,32,256]{2,1,0:T(8,128)(2,1)S(1)} async-done(((bf16[32,32,256]{2,1,0:T(8,128)(2,1)}), bf16[32,32,256]{2,1,0:T(8,128)(2,1)S(1)}, u32[]{:S(2)}, u32[]{:S(2)}) %all-to-all-start.1) | async-done | bytes 524320 | tf_op jit(solution)/shard_map/all_to_all | solution.py:205
  43.8 0.4 select_reduce_fusion
  44.6 0.8 %convolution_convert_fusion.2 = bf16[128,256]{1,0:T(8,128)(2,1)} fusion(bf16[128,256]{1,0:T(8,128)(2,1)S(1)} %fusion.5, bf16[256,256]{1,0:T(8,128)(2,1)S(1)} %copy-done), kind=kOutput, calls=%fused_computation.4 | convolution fusion | flops 16809984 | bytes 262144 | tf_op jit(solution)/shard_map/nk,dk->nd/dot_general | solution.py:218
  (47 shorter events, 2.2 us)
Async XLA Ops:
  0.0 14.5 %copy-start = (bf16[256,256]{1,0:T(8,128)(2,1)S(1)}, bf16[256,256]{1,0:T(8,128)(2,1)}, u32[]{:S(2)}) copy-start(bf16[256,256]{1,0:T(8,128)(2,1)} %param.7) | copy-start | bytes 393220
  0.0 15.6 %copy-start.3 = (bf16[128,1024]{1,0:T(8,128)(2,1)S(1)}, bf16[128,1024]{1,0:T(8,128)(2,1)}, u32[]{:S(2)}) copy-start(bf16[128,1024]{1,0:T(8,128)(2,1)} %param.8) | copy-start | bytes 786436
  0.0 17.8 %collective-permute-start = (bf16[4,32,256]{2,1,0:T(8,128)(2,1)}, bf16[4,32,256]{2,1,0:T(8,128)(2,1)S(1)}, u32[]{:S(2)}, u32[]{:S(2)}) collective-permute-start(bf16[4,32,256]{2,1,0:T(8,128)(2,1)} %param.6), channel_id=1, source_target_pairs={{0,1},{1,2},{2,3},{3,0},{4,5},{5,6},{6,7},{7,4},{8,9},{9,10},{10,1... | collective-permute-start | bytes 196616 | tf_op jit(solution)/shard_map/ppermute | solution.py:113
  3.1 15.0 %collective-permute-start.1 = (bf16[4,32,256]{2,1,0:T(8,128)(2,1)}, bf16[4,32,256]{2,1,0:T(8,128)(2,1)S(1)}, u32[]{:S(2)}, u32[]{:S(2)}) collective-permute-start(bf16[4,32,256]{2,1,0:T(8,128)(2,1)} %param.6), channel_id=1, source_target_pairs={{0,2},{1,3},{2,0},{3,1},{4,6},{5,7},{6,4},{7,5},{8,10},{9,11},{10,... | collective-permute-start | bytes 196616 | tf_op jit(solution)/shard_map/ppermute | solution.py:113
  5.6 12.7 %collective-permute-start.2 = (bf16[4,32,256]{2,1,0:T(8,128)(2,1)}, bf16[4,32,256]{2,1,0:T(8,128)(2,1)S(1)}, u32[]{:S(2)}, u32[]{:S(2)}) collective-permute-start(bf16[4,32,256]{2,1,0:T(8,128)(2,1)} %param.6), channel_id=1, source_target_pairs={{0,3},{1,0},{2,1},{3,2},{4,7},{5,4},{6,5},{7,6},{8,11},{9,8},{10,9... | collective-permute-start | bytes 196616 | tf_op jit(solution)/shard_map/ppermute | solution.py:113
  9.4 13.4 %all-to-all-start = ((bf16[32,32,256]{2,1,0:T(8,128)(2,1)}), bf16[32,32,256]{2,1,0:T(8,128)(2,1)S(1)}, u32[]{:S(2)}, u32[]{:S(2)}) async-start(bf16[32,32,256]{2,1,0:T(8,128)(2,1)} %select_select_fusion), calls=%async_computation | async-start | bytes 1048576 | tf_op jit(solution)/shard_map/all_to_all | solution.py:148
  15.6 1.7 %copy-start.1 = (f32[128,256]{1,0:T(8,128)}, f32[128,256]{1,0:T(8,128)S(1)}, u32[]{:S(2)}) copy-start(f32[128,256]{1,0:T(8,128)S(1)} %get-tuple-element.23) | copy-start | bytes 393220
  15.6 2.0 %copy-start.7 = (s32[128]{0:T(128)S(1)}, s32[128]{0:T(128)}, u32[]{:S(2)}) copy-start(s32[128]{0:T(128)} %param.10) | copy-start | bytes 1540
  15.6 2.0 %copy-start.8 = (s32[128]{0:T(128)S(1)}, s32[128]{0:T(128)}, u32[]{:S(2)}) copy-start(s32[128]{0:T(128)} %param.9) | copy-start | bytes 1540
  15.6 2.4 %copy-start.5 = (f32[128]{0:T(128)}, f32[128]{0:T(128)S(1)}, u32[]{:S(2)}) copy-start(f32[128]{0:T(128)S(1)} %add_rsqrt_fusion.4) | copy-start | bytes 1540
  30.6 13.1 %all-to-all-start.1 = ((bf16[32,32,256]{2,1,0:T(8,128)(2,1)}), bf16[32,32,256]{2,1,0:T(8,128)(2,1)S(1)}, u32[]{:S(2)}, u32[]{:S(2)}) async-start(bf16[32,32,256]{2,1,0:T(8,128)(2,1)} %convolution_convert_fusion), calls=%async_computation.1 | async-start | bytes 1048576 | tf_op jit(solution)/shard_map/all_to_all | solution.py:205
  34.5 9.3 %copy-start.4 = (pred[32,4]{1,0:T(8,128)(4,1)S(1)}, pred[32,4]{1,0:T(8,128)(4,1)}, u32[]{:S(2)}) copy-start(pred[32,4]{1,0:T(8,128)(4,1)} %iota_compare_fusion.1) | copy-start | bytes 388
  34.6 9.7 %copy-start.2 = (f32[128,256]{1,0:T(8,128)S(1)}, f32[128,256]{1,0:T(8,128)}, u32[]{:S(2)}) copy-start(f32[128,256]{1,0:T(8,128)} %copy-done.1) | copy-start | bytes 393220
  34.6 9.7 %copy-start.6 = (f32[128]{0:T(128)S(1)}, f32[128]{0:T(128)}, u32[]{:S(2)}) copy-start(f32[128]{0:T(128)} %copy-done.5) | copy-start | bytes 1540
  34.6 9.6 %collective-permute-start.3 = (bf16[4,32,256]{2,1,0:T(8,128)(2,1)S(1)}, bf16[4,32,256]{2,1,0:T(8,128)(2,1)S(1)}, u32[]{:S(2)}, u32[]{:S(2)}) collective-permute-start(bf16[4,32,256]{2,1,0:T(8,128)(2,1)S(1)} %bitcast.71), channel_id=1, source_target_pairs={{0,3},{1,0},{2,1},{3,2},{4,7},{5,4},{6,5},{7,6},{8,11},{9,8},{10,9... | collective-permute-start | bytes 196616 | tf_op jit(solution)/shard_map/ppermute | solution.py:186
  35.1 9.1 %collective-permute-start.4 = (bf16[4,32,256]{2,1,0:T(8,128)(2,1)S(1)}, bf16[4,32,256]{2,1,0:T(8,128)(2,1)S(1)}, u32[]{:S(2)}, u32[]{:S(2)}) collective-permute-start(bf16[4,32,256]{2,1,0:T(8,128)(2,1)S(1)} %bitcast.70), channel_id=1, source_target_pairs={{0,2},{1,3},{2,0},{3,1},{4,6},{5,7},{6,4},{7,5},{8,10},{9,11},{10,... | collective-permute-start | bytes 196616 | tf_op jit(solution)/shard_map/ppermute | solution.py:186
  36.8 7.4 %collective-permute-start.5 = (bf16[4,32,256]{2,1,0:T(8,128)(2,1)S(1)}, bf16[4,32,256]{2,1,0:T(8,128)(2,1)S(1)}, u32[]{:S(2)}, u32[]{:S(2)}) collective-permute-start(bf16[4,32,256]{2,1,0:T(8,128)(2,1)S(1)} %bitcast.69), channel_id=1, source_target_pairs={{0,1},{1,2},{2,3},{3,0},{4,5},{5,6},{6,7},{7,4},{8,9},{9,10},{10,1... | collective-permute-start | bytes 196616 | tf_op jit(solution)/shard_map/ppermute | solution.py:186

commit v6 on v5

--- a/solution.py
+++ b/solution.py
@@ -43,24 +43,46 @@
     return jnp.broadcast_to(total, (rows // group, group, width)).reshape(rows, width)
 
 
-def softmax_bwd_kernel(group, score_scale, recv, edge_at_ref, s_ref, m_ref, d_ref, g_scr):
+def place_kernel(group, recv, edge_at_ref, m_ref, g_ref):
     block = pl.program_id(0)
-    firsts = s_ref.shape[0] // group
+    firsts = g_ref.shape[0] // group
 
     def place(first, carry):
         row = pl.multiple_of(first * group, group)
         base = (block * firsts + first) * recv
         for second in range(recv):
-            g_scr[pl.ds(row, group), second * group : (second + 1) * group] = m_ref[
+            g_ref[pl.ds(row, group), second * group : (second + 1) * group] = m_ref[
                 edge_at_ref[base + second]
-            ].astype(jnp.float32)
+            ]
         return carry
 
     lax.fori_loop(0, firsts, place, 0)
+
+
+def place_grads(edge_at, blocks, total_rows, width, group):
+    recv = width // group
+    block = 128 if total_rows % 128 == 0 else total_rows
+    return pl.pallas_call(
+        functools.partial(place_kernel, group, recv),
+        out_shape=jax.ShapeDtypeStruct((total_rows, width), blocks.dtype),
+        grid_spec=pltpu.PrefetchScalarGridSpec(
+            num_scalar_prefetch=1,
+            grid=(total_rows // block,),
+            in_specs=[pl.BlockSpec(blocks.shape, lambda b, e: (0, 0, 0))],
+            out_specs=pl.BlockSpec((block, width), lambda b, e: (b, 0)),
+        ),
+        compiler_params=pltpu.CompilerParams(vmem_limit_bytes=32 * 1024 * 1024),
+        cost_estimate=pl.CostEstimate(
+            flops=0, transcendentals=0, bytes_accessed=2 * total_rows * width + 2 * blocks.size
+        ),
+    )(edge_at, blocks)
+
+
+def softmax_bwd_kernel(group, score_scale, s_ref, g_ref, d_ref):
     expo = jnp.exp(s_ref[...])
     rows = expo / lane_group_sum(expo, group)
     cols = expo / row_group_sum(expo, group)
-    grads = g_scr[...]
+    grads = g_ref[...].astype(jnp.float32)
     d_rows = grads * cols
     d_cols = grads * rows
     d_scores = rows * (d_rows - lane_group_sum(d_rows * rows, group)) + cols * (
@@ -69,30 +91,25 @@
     d_ref[...] = (d_scores * score_scale).astype(jnp.bfloat16)
 
 
-def softmax_bwd(scores, edge_at, blocks, group, score_scale):
+def softmax_bwd(scores, grads, group, score_scale):
     total_rows, width = scores.shape
-    recv = width // group
     block = 128 if total_rows % 128 == 0 else total_rows
     return pl.pallas_call(
-        functools.partial(softmax_bwd_kernel, group, score_scale, recv),
+        functools.partial(softmax_bwd_kernel, group, score_scale),
         out_shape=jax.ShapeDtypeStruct((total_rows, width), jnp.bfloat16),
-        grid_spec=pltpu.PrefetchScalarGridSpec(
-            num_scalar_prefetch=1,
-            grid=(total_rows // block,),
-            in_specs=[
-                pl.BlockSpec((block, width), lambda b, e: (b, 0)),
-                pl.BlockSpec(blocks.shape, lambda b, e: (0, 0, 0)),
-            ],
-            out_specs=pl.BlockSpec((block, width), lambda b, e: (b, 0)),
-            scratch_shapes=[pltpu.VMEM((block, width), jnp.float32)],
-        ),
+        grid=(total_rows // block,),
+        in_specs=[
+            pl.BlockSpec((block, width), lambda b: (b, 0)),
+            pl.BlockSpec((block, width), lambda b: (b, 0)),
+        ],
+        out_specs=pl.BlockSpec((block, width), lambda b: (b, 0)),
         compiler_params=pltpu.CompilerParams(vmem_limit_bytes=48 * 1024 * 1024),
         cost_estimate=pl.CostEstimate(
             flops=30 * total_rows * width,
             transcendentals=total_rows * width,
-            bytes_accessed=6 * total_rows * width,
-        ),
-    )(edge_at, scores, blocks)
+            bytes_accessed=8 * total_rows * width,
+        ),
+    )(scores, grads)
 
 
 def local(n_grp, n_sub, tokens, proj_weight, match_grad, edge_first, pair_second_image, send_pick):
@@ -163,6 +180,7 @@
         [match_grad.reshape(edge_count, length, length), jnp.zeros((1, length, length), match_grad.dtype)],
         axis=0,
     )
+    grads = place_grads(edge_at, blocks, group_img * length, recv * length, length)
     pool2 = pool.reshape(group_img * length, feat_width)
     recv2 = received.reshape(recv * length, feat_width)
     score_scale = 1.0 / (feat_width * SOFTMAX_COOLING)
@@ -170,7 +188,7 @@
         lax.dot_general(pool2, recv2, (((1,), (1,)), ((), ())), preferred_element_type=jnp.float32)
         * score_scale
     )
-    d_scaled = softmax_bwd(scores, edge_at, blocks, length, score_scale)
+    d_scaled = softmax_bwd(scores, grads, length, score_scale)
     pool_total = jnp.dot(d_scaled, recv2, preferred_element_type=jnp.float32).reshape(
         group_img, length, feat_width
     )

time: 45.8 us -> 44.5 us (0.972)
  waiting for transfers between devices: 10.6 us -> 6.77 us
  starting transfers between devices: 16.6 us -> 19 us
  Pallas kernels: 5.09 us -> 5.9 us
  other arithmetic: 4.33 us -> 3.74 us
    all_to_all x1, waiting for transfers between devices: 3.88 us -> 1.2 us  [local(): lax.all_to_all(outgoing, 'grp', split_axis=0, concat_axis=0, tiled=True)]
    ppermute x3, starting transfers between devices: 2.4 us -> 3.87 us  [local(): lax.ppermute(pool_b[k * img_count:(k + 1) * img_count], 'sub', shift(n_su...]
    all_to_all x1, waiting for transfers between devices: 6.69 us -> 5.24 us  [local(): lax.all_to_all(slot_b, 'grp', split_axis=0, concat_axis=0, tiled=True)]
    ppermute x3, starting transfers between devices: 6.99 us -> 7.89 us  [local(): lax.ppermute(tokens, 'sub', shift(n_sub, k))]
    pallas_call x1 -> x2, Pallas kernels: 5.09 us -> 5.9 us  [the longest x1 3.29 us: place_grads(): pl.pallas_call(functools.partial(place_kernel, group, recv), out_shape=ja...]
    eq x1, other arithmetic: 1.32 us -> 0.73 us  [local(): order[:, None, None, None]]
  transfers between devices with their start and end apart: 8 -> 8, of which waited for: 2 -> 3; matrix products, arithmetic and copies ran while one was open for 20% -> 19% of each run, Pallas kernels for 0% -> 7%
where the time goes in v6:
time: 44.5 us; the launch traced here: 44.1 us
  starting transfers between devices  19 us (43%)
  waiting for transfers between devices  6.77 us (15%)
  Pallas kernels  5.9 us (13%)
  matrix products  5.19 us (12%)
  other arithmetic  3.74 us (8%)
  local copies, waits for them, and re-layouts  3.22 us (7%)
    ppermute x3, starting transfers between devices, local(): lax.ppermute(tokens, 'sub', shift(n_sub, k))  7.89 us
    all_to_all x1, waiting for transfers between devices, local(): lax.all_to_all(slot_b, 'grp', split_axis=0, concat_axis=0, tiled=True)  5.24 us
    ppermute x3, starting transfers between devices, local(): lax.ppermute(pool_b[k * img_count:(k + 1) * img_count], 'sub', shift(n_su...  3.87 us
    all_to_all x1, starting transfers between devices, local(): lax.all_to_all(outgoing, 'grp', split_axis=0, concat_axis=0, tiled=True)  3.72 us
    all_to_all x1, starting transfers between devices, local(): lax.all_to_all(slot_b, 'grp', split_axis=0, concat_axis=0, tiled=True)  3.49 us
    pallas_call x1, Pallas kernels, place_grads(): pl.pallas_call(functools.partial(place_kernel, group, recv), out_shape=ja...  3.29 us
    pallas_call x1, Pallas kernels, softmax_bwd(): pl.pallas_call(functools.partial(softmax_bwd_kernel, group, score_scale),...  2.6 us
    dot_general x5, matrix products, normalize(): jnp.dot(tokens.reshape(image_count * length, feat_width), proj_weight, pr...  2.21 us
  transfers between devices with their start and end apart: 8, of which 3 were waited for; matrix products, arithmetic and copies ran while one was open for 19% of the time, Pallas kernels for 7%

profile of v6, /device:TPU:0, one launch (start us, length us, event | category | flops | bytes accessed | tf_op | source)
XLA Modules:
  0.0 44.1 jit_solution(15209923646292392398)
XLA Ops:
  0.0 4.1 %collective-permute-start.1 = (bf16[4,32,256]{2,1,0:T(8,128)(2,1)}, bf16[4,32,256]{2,1,0:T(8,128)(2,1)S(1)}, u32[]{:S(2)}, u32[]{:S(2)}) collective-permute-start(bf16[4,32,256]{2,1,0:T(8,128)(2,1)} %param.6), channel_id=1, source_target_pairs={{0,2},{1,3},{2,0},{3,1},{4,6},{5,7},{6,4},{7,5},{8,10},{9,11},{10,... | collective-permute-start | bytes 196616 | tf_op jit(solution)/shard_map/ppermute | solution.py:130
  4.1 1.6 %collective-permute-start = (bf16[4,32,256]{2,1,0:T(8,128)(2,1)}, bf16[4,32,256]{2,1,0:T(8,128)(2,1)S(1)}, u32[]{:S(2)}, u32[]{:S(2)}) collective-permute-start(bf16[4,32,256]{2,1,0:T(8,128)(2,1)} %param.6), channel_id=1, source_target_pairs={{0,1},{1,2},{2,3},{3,0},{4,5},{5,6},{6,7},{7,4},{8,9},{9,10},{10,1... | collective-permute-start | bytes 196616 | tf_op jit(solution)/shard_map/ppermute | solution.py:130
  5.6 2.2 %collective-permute-start.2 = (bf16[4,32,256]{2,1,0:T(8,128)(2,1)}, bf16[4,32,256]{2,1,0:T(8,128)(2,1)S(1)}, u32[]{:S(2)}, u32[]{:S(2)}) collective-permute-start(bf16[4,32,256]{2,1,0:T(8,128)(2,1)} %param.6), channel_id=1, source_target_pairs={{0,3},{1,0},{2,1},{3,2},{4,7},{5,4},{6,5},{7,6},{8,11},{9,8},{10,9... | collective-permute-start | bytes 196616 | tf_op jit(solution)/shard_map/ppermute | solution.py:130
  7.9 0.8 %slice_bitcast_fusion.3 = (bf16[32,256]{1,0:T(8,128)(2,1)S(1)}, bf16[32,256]{1,0:T(8,128)(2,1)S(1)}, bf16[32,256]{1,0:T(8,128)(2,1)S(1)}, bf16[32,256]{1,0:T(8,128)(2,1)S(1)}) fusion(bf16[4,32,256]{2,1,0:T(8,128)(2,1)} %param.6), kind=kLoop, calls=%fused_computation.32 | loop fusion | bytes 131072 | tf_op jit(solution)/shard_map/squeeze | solution.py:152
  8.7 0.7 %broadcast_compare_fusion.2 = (pred[32]{0:T(512)(128)(4,1)S(1)}, pred[32]{0:T(512)(128)(4,1)S(1)}, pred[32]{0:T(512)(128)(4,1)S(1)}) fusion(s32[32]{0:T(128)} %param.11), kind=kLoop, calls=%fused_computation.52 | loop fusion | flops 96 | bytes 224 | tf_op jit(solution)/shard_map/eq | solution.py:152
  9.4 1.0 %select_select_fusion = bf16[32,32,256]{2,1,0:T(8,128)(2,1)} fusion(pred[32]{0:T(512)(128)(4,1)S(1)} %get-tuple-element.15, pred[32]{0:T(512)(128)(4,1)S(1)} %get-tuple-element.14, pred[32]{0:T(512)(128)(4,1)S(1)} %get-tuple-element.13, bf16[32,256]{1,0:T(8,128)(2,1)S(1)} %get-tuple-element.11, bf16[32,256]{1,0:T(8,128)(2,1)S(1)} %get-tuple-element.12, ...), kind=kLoop, calls=%fused_computation.7 | loop fusion | flops 786432 | bytes 589920 | tf_op jit(solution)/shard_map/jit(_where)/select_n | solution.py:152
  10.3 3.7 %all-to-all-start = ((bf16[32,32,256]{2,1,0:T(8,128)(2,1)}), bf16[32,32,256]{2,1,0:T(8,128)(2,1)S(1)}, u32[]{:S(2)}, u32[]{:S(2)}) async-start(bf16[32,32,256]{2,1,0:T(8,128)(2,1)} %select_select_fusion), calls=%async_computation | async-start | bytes 1048576 | tf_op jit(solution)/shard_map/all_to_all | solution.py:165
  14.0 0.7 %iota_compare_fusion.1 = pred[32,4]{1,0:T(8,128)(4,1)S(1)} fusion(s32[32]{0:T(128)} %param.11), kind=kLoop, calls=%fused_computation.28 | loop fusion | flops 128 | bytes 256 | tf_op jit(solution)/shard_map/eq | solution.py:224
  14.8 1.1 %multiply_reduce_fusion.4 = (f32[128]{0:T(128)S(1)}, f32[128,256]{1,0:T(8,128)S(1)}) fusion(bf16[128,256]{1,0:T(8,128)(2,1)} %bitcast.60, bf16[256,256]{1,0:T(8,128)(2,1)S(1)} %copy-done), kind=kOutput, calls=%fused_computation.26 | convolution fusion | flops 16842624 | bytes 328192 | tf_op jit(solution)/shard_map/dot_general | solution.py:18
  16.1 1.5 %copy.12 = bf16[128,32,32]{2,1,0:T(8,128)(2,1)S(1)} copy(bf16[128,32,32]{0,2,1:T(8,128)(2,1)S(1)} %bitcast.59) | data formatting | bytes 524288 | tf_op jit(solution)/shard_map/reshape | solution.py:180
  18.1 3.3 %shard_map.64.g_ref = bf16[512,1024]{1,0:T(8,128)(2,1)S(1)} custom-call(s32[512]{0:T(512)S(1)} %select_reduce_fusion.1.edge_at_ref, bf16[129,32,32]{2,1,0:T(8,128)(2,1)S(1)} %concatenate.7.m_ref), custom_call_target="tpu_custom_call" | custom-call | bytes 1312768 | tf_op jit(solution)/shard_map/pallas_call | solution.py:65
  22.6 1.2 %all-to-all-done = bf16[32,32,256]{2,1,0:T(8,128)(2,1)S(1)} async-done(((bf16[32,32,256]{2,1,0:T(8,128)(2,1)}), bf16[32,32,256]{2,1,0:T(8,128)(2,1)S(1)}, u32[]{:S(2)}, u32[]{:S(2)}) %all-to-all-start) | async-done | bytes 524320 | tf_op jit(solution)/shard_map/all_to_all | solution.py:165
  23.7 0.4 multiply_reduce_fusion
  24.1 0.4 convolution_multiply_fusion.s_ref
  24.6 2.6 %shard_map.65 = bf16[512,1024]{1,0:T(8,128)(2,1)S(1)} custom-call(f32[512,1024]{1,0:T(8,128)S(1)} %convolution_multiply_fusion.s_ref, bf16[512,1024]{1,0:T(8,128)(2,1)S(1)} %shard_map.64.g_ref), custom_call_target="tpu_custom_call" | custom-call | flops 15728640 | bytes 4194304 | tf_op jit(solution)/shard_map/pallas_call | solution.py:97
  27.2 0.5 %copy.13 = bf16[1024,512]{1,0:T(8,128)(2,1)S(1)} copy(bf16[1024,512]{0,1:T(8,128)(2,1)S(1)} %bitcast.54) | data formatting | bytes 2097152 | tf_op jit(solution)/shard_map/dot_general | solution.py:195
  27.7 1.2 %convolution_convert_fusion = bf16[32,32,256]{2,1,0:T(8,128)(2,1)} fusion(bf16[32,32,512]{2,1,0:T(8,128)(2,1)S(1)} %bitcast.55, bf16[512,256,1]{1,0,2:T(8,128)(2,1)S(1)} %bitcast.57), kind=kOutput, calls=%fused_computation.2 | convolution fusion | flops 268697600 | bytes 1835008 | tf_op jit(solution)/shard_map/dot_general | solution.py:195
  29.0 3.5 %all-to-all-start.1 = ((bf16[32,32,256]{2,1,0:T(8,128)(2,1)}), bf16[32,32,256]{2,1,0:T(8,128)(2,1)S(1)}, u32[]{:S(2)}, u32[]{:S(2)}) async-start(bf16[32,32,256]{2,1,0:T(8,128)(2,1)} %convolution_convert_fusion), calls=%async_computation.1 | async-start | bytes 1048576 | tf_op jit(solution)/shard_map/all_to_all | solution.py:223
  32.5 0.5 %convolution_convert_fusion.1 = bf16[512,256]{1,0:T(8,128)(2,1)S(1)} fusion(bf16[512,1024]{1,0:T(8,128)(2,1)S(1)} %shard_map.65, f32[1024,256]{0,1:T(8,128)S(1)} %get-tuple-element.25, f32[1024]{0:T(1024)S(1)} %add_rsqrt_fusion), kind=kOutput, calls=%fused_computation.3 | convolution fusion | flops 269090816 | bytes 2363392 | tf_op jit(solution)/shard_map/dot_general | solution.py:192
  33.1 3.8 %collective-permute-start.3 = (bf16[4,32,256]{2,1,0:T(8,128)(2,1)S(1)}, bf16[4,32,256]{2,1,0:T(8,128)(2,1)S(1)}, u32[]{:S(2)}, u32[]{:S(2)}) collective-permute-start(bf16[4,32,256]{2,1,0:T(8,128)(2,1)S(1)} %bitcast.70), channel_id=1, source_target_pairs={{0,3},{1,0},{2,1},{3,2},{4,7},{5,4},{6,5},{7,6},{8,11},{9,8},{10,9... | collective-permute-start | bytes 196616 | tf_op jit(solution)/shard_map/ppermute | solution.py:204
  36.9 5.2 %all-to-all-done.1 = bf16[32,32,256]{2,1,0:T(8,128)(2,1)S(1)} async-done(((bf16[32,32,256]{2,1,0:T(8,128)(2,1)}), bf16[32,32,256]{2,1,0:T(8,128)(2,1)S(1)}, u32[]{:S(2)}, u32[]{:S(2)}) %all-to-all-start.1) | async-done | bytes 524320 | tf_op jit(solution)/shard_map/all_to_all | solution.py:223
  42.2 0.4 select_reduce_fusion
  42.6 0.3 collective-permute-done.4
  43.3 0.8 %convolution_convert_fusion.2 = bf16[128,256]{1,0:T(8,128)(2,1)} fusion(bf16[128,256]{1,0:T(8,128)(2,1)S(1)} %fusion.5, bf16[256,256]{1,0:T(8,128)(2,1)S(1)} %copy-done), kind=kOutput, calls=%fused_computation.4 | convolution fusion | flops 16809984 | bytes 262144 | tf_op jit(solution)/shard_map/nk,dk->nd/dot_general | solution.py:236
  (42 shorter events, 2.3 us)
Async XLA Ops:
  0.0 14.8 %copy-start = (bf16[256,256]{1,0:T(8,128)(2,1)S(1)}, bf16[256,256]{1,0:T(8,128)(2,1)}, u32[]{:S(2)}) copy-start(bf16[256,256]{1,0:T(8,128)(2,1)} %param.7) | copy-start | bytes 393220
  0.0 15.9 %copy-start.3 = (bf16[128,1024]{1,0:T(8,128)(2,1)S(1)}, bf16[128,1024]{1,0:T(8,128)(2,1)}, u32[]{:S(2)}) copy-start(bf16[128,1024]{1,0:T(8,128)(2,1)} %param.8) | copy-start | bytes 786436
  0.0 21.4 %collective-permute-start.1 = (bf16[4,32,256]{2,1,0:T(8,128)(2,1)}, bf16[4,32,256]{2,1,0:T(8,128)(2,1)S(1)}, u32[]{:S(2)}, u32[]{:S(2)}) collective-permute-start(bf16[4,32,256]{2,1,0:T(8,128)(2,1)} %param.6), channel_id=1, source_target_pairs={{0,2},{1,3},{2,0},{3,1},{4,6},{5,7},{6,4},{7,5},{8,10},{9,11},{10,... | collective-permute-start | bytes 196616 | tf_op jit(solution)/shard_map/ppermute | solution.py:130
  4.1 17.6 %collective-permute-start = (bf16[4,32,256]{2,1,0:T(8,128)(2,1)}, bf16[4,32,256]{2,1,0:T(8,128)(2,1)S(1)}, u32[]{:S(2)}, u32[]{:S(2)}) collective-permute-start(bf16[4,32,256]{2,1,0:T(8,128)(2,1)} %param.6), channel_id=1, source_target_pairs={{0,1},{1,2},{2,3},{3,0},{4,5},{5,6},{6,7},{7,4},{8,9},{9,10},{10,1... | collective-permute-start | bytes 196616 | tf_op jit(solution)/shard_map/ppermute | solution.py:130
  5.6 16.3 %collective-permute-start.2 = (bf16[4,32,256]{2,1,0:T(8,128)(2,1)}, bf16[4,32,256]{2,1,0:T(8,128)(2,1)S(1)}, u32[]{:S(2)}, u32[]{:S(2)}) collective-permute-start(bf16[4,32,256]{2,1,0:T(8,128)(2,1)} %param.6), channel_id=1, source_target_pairs={{0,3},{1,0},{2,1},{3,2},{4,7},{5,4},{6,5},{7,6},{8,11},{9,8},{10,9... | collective-permute-start | bytes 196616 | tf_op jit(solution)/shard_map/ppermute | solution.py:130
  10.3 13.4 %all-to-all-start = ((bf16[32,32,256]{2,1,0:T(8,128)(2,1)}), bf16[32,32,256]{2,1,0:T(8,128)(2,1)S(1)}, u32[]{:S(2)}, u32[]{:S(2)}) async-start(bf16[32,32,256]{2,1,0:T(8,128)(2,1)} %select_select_fusion), calls=%async_computation | async-start | bytes 1048576 | tf_op jit(solution)/shard_map/all_to_all | solution.py:165
  15.9 5.5 %copy-start.1 = (f32[128,256]{1,0:T(8,128)}, f32[128,256]{1,0:T(8,128)S(1)}, u32[]{:S(2)}) copy-start(f32[128,256]{1,0:T(8,128)S(1)} %get-tuple-element.23) | copy-start | bytes 393220
  15.9 2.0 %copy-start.4 = (s32[128]{0:T(128)S(1)}, s32[128]{0:T(128)}, u32[]{:S(2)}) copy-start(s32[128]{0:T(128)} %param.10) | copy-start | bytes 1540
  15.9 2.0 %copy-start.5 = (s32[128]{0:T(128)S(1)}, s32[128]{0:T(128)}, u32[]{:S(2)}) copy-start(s32[128]{0:T(128)} %param.9) | copy-start | bytes 1540
  29.0 13.1 %all-to-all-start.1 = ((bf16[32,32,256]{2,1,0:T(8,128)(2,1)}), bf16[32,32,256]{2,1,0:T(8,128)(2,1)S(1)}, u32[]{:S(2)}, u32[]{:S(2)}) async-start(bf16[32,32,256]{2,1,0:T(8,128)(2,1)} %convolution_convert_fusion), calls=%async_computation.1 | async-start | bytes 1048576 | tf_op jit(solution)/shard_map/all_to_all | solution.py:223
  32.9 10.0 %copy-start.2 = (f32[128,256]{1,0:T(8,128)S(1)}, f32[128,256]{1,0:T(8,128)}, u32[]{:S(2)}) copy-start(f32[128,256]{1,0:T(8,128)} %copy-done.1) | copy-start | bytes 393220
  33.0 9.6 %collective-permute-start.5 = (bf16[4,32,256]{2,1,0:T(8,128)(2,1)S(1)}, bf16[4,32,256]{2,1,0:T(8,128)(2,1)S(1)}, u32[]{:S(2)}, u32[]{:S(2)}) collective-permute-start(bf16[4,32,256]{2,1,0:T(8,128)(2,1)S(1)} %bitcast.71), channel_id=1, source_target_pairs={{0,1},{1,2},{2,3},{3,0},{4,5},{5,6},{6,7},{7,4},{8,9},{9,10},{10,1... | collective-permute-start | bytes 196616 | tf_op jit(solution)/shard_map/ppermute | solution.py:204
  33.1 9.6 %collective-permute-start.3 = (bf16[4,32,256]{2,1,0:T(8,128)(2,1)S(1)}, bf16[4,32,256]{2,1,0:T(8,128)(2,1)S(1)}, u32[]{:S(2)}, u32[]{:S(2)}) collective-permute-start(bf16[4,32,256]{2,1,0:T(8,128)(2,1)S(1)} %bitcast.70), channel_id=1, source_target_pairs={{0,3},{1,0},{2,1},{3,2},{4,7},{5,4},{6,5},{7,6},{8,11},{9,8},{10,9... | collective-permute-start | bytes 196616 | tf_op jit(solution)/shard_map/ppermute | solution.py:204
  36.9 6.1 %collective-permute-start.4 = (bf16[4,32,256]{2,1,0:T(8,128)(2,1)S(1)}, bf16[4,32,256]{2,1,0:T(8,128)(2,1)S(1)}, u32[]{:S(2)}, u32[]{:S(2)}) collective-permute-start(bf16[4,32,256]{2,1,0:T(8,128)(2,1)S(1)} %bitcast.69), channel_id=1, source_target_pairs={{0,2},{1,3},{2,0},{3,1},{4,6},{5,7},{6,4},{7,5},{8,10},{9,11},{10,... | collective-permute-start | bytes 196616 | tf_op jit(solution)/shard_map/ppermute | solution.py:204

commit v7 on v6

--- a/solution.py
+++ b/solution.py
@@ -10,7 +10,6 @@
 EPSILON = 1e-05
 SOFTMAX_COOLING = 0.1
 SUB_MODE = "perm"
-GRP_MODE = "a2a"
 
 
 def normalize(tokens, proj_weight):
@@ -143,24 +142,25 @@
         first_at = edge_first
 
     picks = send_pick.reshape(n_grp, slots)
-    if GRP_MODE == "perm":
-        order = picks[(grp_at + jnp.arange(n_grp, dtype=jnp.int32)) % n_grp].reshape(recv)
-    else:
-        order = send_pick
-    outgoing = jnp.broadcast_to(tokens[img_count - 1], (recv, length, feat_width))
-    for image in range(img_count - 2, -1, -1):
-        outgoing = jnp.where(order[:, None, None] == image, tokens[image], outgoing)
-    if GRP_MODE == "perm":
-        received = jnp.concatenate(
-            [outgoing[:slots]]
-            + [
-                lax.ppermute(outgoing[k * slots : (k + 1) * slots], "grp", shift(n_grp, k))
-                for k in range(1, n_grp)
-            ],
-            axis=0,
-        )
-        second_at = ((grp_at - pair_second_image // slots) % n_grp) * slots + pair_second_image % slots
-    else:
+    whole = slots == img_count
+    if whole:
+        pick_rows = jnp.pad(
+            picks.astype(tokens.dtype)[:, None, :], ((0, 0), (0, 15), (0, feat_width - slots))
+        )
+        outgoing = jnp.concatenate(
+            [jnp.broadcast_to(tokens.reshape(1, img_count * length, feat_width), (n_grp, img_count * length, feat_width)), pick_rows],
+            axis=1,
+        )
+        arrived = lax.all_to_all(outgoing, "grp", split_axis=0, concat_axis=0, tiled=True)
+        received = normalize(
+            arrived[:, : img_count * length].reshape(n_grp * img_count, length, feat_width), proj_weight
+        )[2]
+        got_picks = arrived[:, img_count * length, :slots].astype(jnp.int32).reshape(recv)
+        second_at = (pair_second_image // slots) * img_count + jnp.take(got_picks, pair_second_image)
+    else:
+        outgoing = jnp.broadcast_to(tokens[img_count - 1], (recv, length, feat_width))
+        for image in range(img_count - 2, -1, -1):
+            outgoing = jnp.where(send_pick[:, None, None] == image, tokens[image], outgoing)
         received = normalize(
             lax.all_to_all(outgoing, "grp", split_axis=0, concat_axis=0, tiled=True), proj_weight
         )[2]
@@ -210,21 +210,12 @@
     else:
         owned = lax.psum_scatter(pool_b, "sub", scatter_dimension=0, tiled=True).astype(jnp.float32)
 
-    if GRP_MODE == "perm":
-        returned = jnp.concatenate(
-            [slot_b[:slots]]
-            + [
-                lax.ppermute(slot_b[k * slots : (k + 1) * slots], "grp", shift(n_grp, -k))
-                for k in range(1, n_grp)
-            ],
-            axis=0,
-        )
-    else:
-        returned = lax.all_to_all(slot_b, "grp", split_axis=0, concat_axis=0, tiled=True)
-    slot_images = order[:, None, None, None] == jnp.arange(img_count, dtype=jnp.int32)[None, :, None, None]
-    incoming_gradient = owned + jnp.sum(
-        jnp.where(slot_images, returned.astype(jnp.float32)[:, None], 0.0), axis=0
-    )
+    returned = lax.all_to_all(slot_b, "grp", split_axis=0, concat_axis=0, tiled=True).astype(jnp.float32)
+    if whole:
+        incoming_gradient = owned + jnp.sum(returned.reshape(n_grp, img_count, length, feat_width), axis=0)
+    else:
+        slot_images = send_pick[:, None, None, None] == jnp.arange(img_count, dtype=jnp.int32)[None, :, None, None]
+        incoming_gradient = owned + jnp.sum(jnp.where(slot_images, returned[:, None], 0.0), axis=0)
     incoming_gradient = incoming_gradient.reshape(img_count * length, feat_width)
     feature_grad = (
         inv_rms

time: 44.5 us -> 48.9 us (1.099)
  waiting for transfers between devices: 6.77 us -> 13.1 us
  local copies, waits for them, and re-layouts: 3.22 us -> 4.73 us
  starting transfers between devices: 19 us -> 17.5 us
  other arithmetic: 3.74 us -> 2.53 us
  matrix products: 5.19 us -> 4.37 us
    all_to_all x1, waiting for transfers between devices: 1.2 us -> 6.93 us  [local(): lax.all_to_all(outgoing, 'grp', split_axis=0, concat_axis=0, tiled=True)]
    ppermute x3, starting transfers between devices: 7.89 us -> 6.09 us  [local(): lax.ppermute(tokens, 'sub', shift(n_sub, k))]
    eq x2 -> x0, other arithmetic: 1.39 us -> none  [the longest x1 0.73 us: local(): order[:, None, None, None]]
    gather x0 -> x1, local copies, waits for them, and re-layouts: none -> 1.23 us  [local(): jnp.take(got_picks, pair_second_image)]
    select_n x1, other arithmetic: 0.96 us -> 0.01 us  [local(): jnp.take(got_picks, pair_second_image)]
    ppermute x3, waiting for transfers between devices: 0.33 us -> 1.25 us  [local(): lax.ppermute(pool_b[k * img_count:(k + 1) * img_count], 'sub', shift(n_su...]
    broadcast_in_dim x0 -> x1, local copies, waits for them, and re-layouts: none -> 0.88 us  [local(): jnp.broadcast_to(tokens.reshape(1, img_count * length, feat_width), (n_gr...]
    concatenate x0 -> x1, other arithmetic: none -> 0.85 us  [local(): jnp.concatenate([jnp.broadcast_to(tokens.reshape(1, img_count * length, f...]
  transfers between devices with their start and end apart: 8 -> 8, of which waited for: 3 -> 3; matrix products, arithmetic and copies ran while one was open for 19% -> 13% of each run, Pallas kernels for 7% -> 0%
where the time goes in v7:
time: 48.9 us; the launch traced here: 48.5 us
  starting transfers between devices  17.5 us (36%)
  waiting for transfers between devices  13.1 us (27%)
  Pallas kernels  5.9 us (12%)
  local copies, waits for them, and re-layouts  4.73 us (10%)
  matrix products  4.37 us (9%)
  other arithmetic  2.53 us (5%)
    all_to_all x1, waiting for transfers between devices, local(): lax.all_to_all(outgoing, 'grp', split_axis=0, concat_axis=0, tiled=True)  6.93 us
    ppermute x3, starting transfers between devices, local(): lax.ppermute(tokens, 'sub', shift(n_sub, k))  6.09 us
    all_to_all x1, waiting for transfers between devices, local(): lax.all_to_all(slot_b, 'grp', split_axis=0, concat_axis=0, tiled=True)  4.9 us
    ppermute x3, starting transfers between devices, local(): lax.ppermute(pool_b[k * img_count:(k + 1) * img_count], 'sub', shift(n_su...  4.21 us
    all_to_all x1, starting transfers between devices, local(): lax.all_to_all(outgoing, 'grp', split_axis=0, concat_axis=0, tiled=True)  3.72 us
    all_to_all x1, starting transfers between devices, local(): lax.all_to_all(slot_b, 'grp', split_axis=0, concat_axis=0, tiled=True)  3.49 us
    pallas_call x1, Pallas kernels, place_grads(): pl.pallas_call(functools.partial(place_kernel, group, recv), out_shape=ja...  3.29 us
    pallas_call x1, Pallas kernels, softmax_bwd(): pl.pallas_call(functools.partial(softmax_bwd_kernel, group, score_scale),...  2.6 us
  transfers between devices with their start and end apart: 8, of which 3 were waited for; matrix products, arithmetic and copies ran while one was open for 13% of the time, Pallas kernels for 0%

profile of v7, /device:TPU:0, one launch (start us, length us, event | category | flops | bytes accessed | tf_op | source)
XLA Modules:
  0.0 48.5 jit_solution(17258116880530923851)
XLA Ops:
  0.0 3.1 %collective-permute-start = (bf16[4,32,256]{2,1,0:T(8,128)(2,1)}, bf16[4,32,256]{2,1,0:T(8,128)(2,1)S(1)}, u32[]{:S(2)}, u32[]{:S(2)}) collective-permute-start(bf16[4,32,256]{2,1,0:T(8,128)(2,1)} %param.6), channel_id=1, source_target_pairs={{0,1},{1,2},{2,3},{3,0},{4,5},{5,6},{6,7},{7,4},{8,9},{9,10},{10,1... | collective-permute-start | bytes 196616 | tf_op jit(solution)/shard_map/ppermute | solution.py:129
  3.1 2.1 %collective-permute-start.2 = (bf16[4,32,256]{2,1,0:T(8,128)(2,1)}, bf16[4,32,256]{2,1,0:T(8,128)(2,1)S(1)}, u32[]{:S(2)}, u32[]{:S(2)}) collective-permute-start(bf16[4,32,256]{2,1,0:T(8,128)(2,1)} %param.6), channel_id=1, source_target_pairs={{0,3},{1,0},{2,1},{3,2},{4,7},{5,4},{6,5},{7,6},{8,11},{9,8},{10,9... | collective-permute-start | bytes 196616 | tf_op jit(solution)/shard_map/ppermute | solution.py:129
  5.1 1.0 %collective-permute-start.1 = (bf16[4,32,256]{2,1,0:T(8,128)(2,1)}, bf16[4,32,256]{2,1,0:T(8,128)(2,1)S(1)}, u32[]{:S(2)}, u32[]{:S(2)}) collective-permute-start(bf16[4,32,256]{2,1,0:T(8,128)(2,1)} %param.6), channel_id=1, source_target_pairs={{0,2},{1,3},{2,0},{3,1},{4,6},{5,7},{6,4},{7,5},{8,10},{9,11},{10,... | collective-permute-start | bytes 196616 | tf_op jit(solution)/shard_map/ppermute | solution.py:129
  6.1 0.7 %convert_element_type.70 = bf16[32]{0:T(256)(128)(2,1)S(1)} convert(s32[32]{0:T(128)} %param.11) | non-fusion elementwise | flops 32 | bytes 192 | tf_op jit(solution)/shard_map/convert_element_type | solution.py:148
  6.8 0.9 %broadcast_in_dim.18 = bf16[8,128,256]{2,1,0:T(8,128)(2,1)S(1)} broadcast(bf16[128,256]{1,0:T(8,128)(2,1)} %bitcast.55), dimensions={1,2} | broadcast | bytes 589824 | tf_op jit(solution)/shard_map/broadcast_in_dim | solution.py:151
  7.8 0.9 %fusion.1 = bf16[8,144,256]{2,1,0:T(8,128)(2,1)} fusion(bf16[8,1,4]{2,1,0:T(2,128)(2,1)S(1)} %convert_element_type.86, bf16[8,128,256]{2,1,0:T(8,128)(2,1)S(1)} %broadcast_in_dim.18), kind=kLoop, calls=%fused_computation.10 | loop fusion | flops 1769472 | bytes 1114176 | tf_op jit(solution)/shard_map/concatenate | solution.py:150
  8.6 3.7 %all-to-all-start = ((bf16[8,144,256]{2,1,0:T(8,128)(2,1)}), bf16[8,144,256]{2,1,0:T(8,128)(2,1)S(1)}, u32[]{:S(2)}, u32[]{:S(2)}) async-start(bf16[8,144,256]{2,1,0:T(8,128)(2,1)} %fusion.1), calls=%async_computation | async-start | bytes 1179648 | tf_op jit(solution)/shard_map/all_to_all | solution.py:154
  12.8 1.4 %copy.14 = bf16[128,32,32]{2,1,0:T(8,128)(2,1)S(1)} copy(bf16[128,32,32]{0,2,1:T(8,128)(2,1)S(1)} %bitcast.54) | data formatting | bytes 524288 | tf_op jit(solution)/shard_map/reshape | solution.py:180
  15.8 6.9 %all-to-all-done = bf16[8,144,256]{2,1,0:T(8,128)(2,1)S(1)} async-done(((bf16[8,144,256]{2,1,0:T(8,128)(2,1)}), bf16[8,144,256]{2,1,0:T(8,128)(2,1)S(1)}, u32[]{:S(2)}, u32[]{:S(2)}) %all-to-all-start) | async-done | bytes 589856 | tf_op jit(solution)/shard_map/all_to_all | solution.py:154
  22.9 1.2 %gather_fusion = s32[128]{0:T(128)S(1)} fusion(s32[32]{0:T(128)S(1)} %reshape.134, s32[1024]{0:T(1024)S(1)} %pad_clamp_fusion), kind=kCustom, calls=%fused_computation | custom fusion | bytes 1536 | tf_op jit(solution)/shard_map/jit(_take)/gather | solution.py:159
  24.3 0.4 multiply_reduce_fusion
  24.7 3.3 %shard_map.64.g_ref = bf16[512,1024]{1,0:T(8,128)(2,1)S(1)} custom-call(s32[512]{0:T(512)S(1)} %select_reduce_fusion.edge_at_ref, bf16[129,32,32]{2,1,0:T(8,128)(2,1)S(1)} %concatenate.11.m_ref), custom_call_target="tpu_custom_call" | custom-call | bytes 1312768 | tf_op jit(solution)/shard_map/pallas_call | solution.py:64
  28.0 0.4 convolution_multiply_fusion.s_ref
  28.4 2.6 %shard_map.65 = bf16[512,1024]{1,0:T(8,128)(2,1)S(1)} custom-call(f32[512,1024]{1,0:T(8,128)S(1)} %convolution_multiply_fusion.s_ref, bf16[512,1024]{1,0:T(8,128)(2,1)S(1)} %shard_map.64.g_ref), custom_call_target="tpu_custom_call" | custom-call | flops 15728640 | bytes 4194304 | tf_op jit(solution)/shard_map/pallas_call | solution.py:96
  31.1 0.5 %copy.15 = bf16[1024,512]{1,0:T(8,128)(2,1)S(1)} copy(bf16[1024,512]{0,1:T(8,128)(2,1)S(1)} %bitcast.48) | data formatting | bytes 2097152 | tf_op jit(solution)/shard_map/dot_general | solution.py:195
  31.6 1.2 %convolution_convert_fusion = bf16[32,32,256]{2,1,0:T(8,128)(2,1)} fusion(bf16[32,32,512]{2,1,0:T(8,128)(2,1)S(1)} %bitcast.49, bf16[512,256,1]{1,0,2:T(8,128)(2,1)S(1)} %bitcast.51), kind=kOutput, calls=%fused_computation.2 | convolution fusion | flops 268697600 | bytes 1835008 | tf_op jit(solution)/shard_map/dot_general | solution.py:195
  32.8 3.5 %all-to-all-start.1 = ((bf16[32,32,256]{2,1,0:T(8,128)(2,1)}), bf16[32,32,256]{2,1,0:T(8,128)(2,1)S(1)}, u32[]{:S(2)}, u32[]{:S(2)}) async-start(bf16[32,32,256]{2,1,0:T(8,128)(2,1)} %convolution_convert_fusion), calls=%async_computation.1 | async-start | bytes 1048576 | tf_op jit(solution)/shard_map/all_to_all | solution.py:213
  36.3 0.5 %convolution_convert_fusion.1 = bf16[512,256]{1,0:T(8,128)(2,1)S(1)} fusion(bf16[512,1024]{1,0:T(8,128)(2,1)S(1)} %shard_map.65, f32[1024,256]{0,1:T(8,128)S(1)} %get-tuple-element.18, f32[1024]{0:T(1024)S(1)} %add_rsqrt_fusion), kind=kOutput, calls=%fused_computation.3 | convolution fusion | flops 269090816 | bytes 2363392 | tf_op jit(solution)/shard_map/dot_general | solution.py:192
  36.9 1.6 %collective-permute-start.5 = (bf16[4,32,256]{2,1,0:T(8,128)(2,1)S(1)}, bf16[4,32,256]{2,1,0:T(8,128)(2,1)S(1)}, u32[]{:S(2)}, u32[]{:S(2)}) collective-permute-start(bf16[4,32,256]{2,1,0:T(8,128)(2,1)S(1)} %bitcast.67), channel_id=1, source_target_pairs={{0,1},{1,2},{2,3},{3,0},{4,5},{5,6},{6,7},{7,4},{8,9},{9,10},{10,1... | collective-permute-start | bytes 196616 | tf_op jit(solution)/shard_map/ppermute | solution.py:204
  38.5 2.2 %collective-permute-start.3 = (bf16[4,32,256]{2,1,0:T(8,128)(2,1)S(1)}, bf16[4,32,256]{2,1,0:T(8,128)(2,1)S(1)}, u32[]{:S(2)}, u32[]{:S(2)}) collective-permute-start(bf16[4,32,256]{2,1,0:T(8,128)(2,1)S(1)} %bitcast.66), channel_id=1, source_target_pairs={{0,3},{1,0},{2,1},{3,2},{4,7},{5,4},{6,5},{7,6},{8,11},{9,8},{10,9... | collective-permute-start | bytes 196616 | tf_op jit(solution)/shard_map/ppermute | solution.py:204
  40.7 0.3 collective-permute-start.4
  41.1 4.9 %all-to-all-done.1 = bf16[32,32,256]{2,1,0:T(8,128)(2,1)S(1)} async-done(((bf16[32,32,256]{2,1,0:T(8,128)(2,1)}), bf16[32,32,256]{2,1,0:T(8,128)(2,1)S(1)}, u32[]{:S(2)}, u32[]{:S(2)}) %all-to-all-start.1) | async-done | bytes 524320 | tf_op jit(solution)/shard_map/all_to_all | solution.py:213
  46.1 1.2 %collective-permute-done.4 = bf16[4,32,256]{2,1,0:T(8,128)(2,1)S(1)} collective-permute-done((bf16[4,32,256]{2,1,0:T(8,128)(2,1)S(1)}, bf16[4,32,256]{2,1,0:T(8,128)(2,1)S(1)}, u32[]{:S(2)}, u32[]{:S(2)}) %collective-permute-start.4) | collective-permute-done | bytes 65568 | tf_op jit(solution)/shard_map/ppermute | solution.py:204
  47.7 0.8 %convolution_convert_fusion.2 = bf16[128,256]{1,0:T(8,128)(2,1)} fusion(bf16[128,256]{1,0:T(8,128)(2,1)S(1)} %fusion.7, bf16[256,256]{1,0:T(8,128)(2,1)S(1)} %copy-done), kind=kOutput, calls=%fused_computation.6 | convolution fusion | flops 16809984 | bytes 262144 | tf_op jit(solution)/shard_map/nk,dk->nd/dot_general | solution.py:227
  (49 shorter events, 2.7 us)
Async XLA Ops:
  0.0 12.4 %copy-start = (bf16[256,256]{1,0:T(8,128)(2,1)S(1)}, bf16[256,256]{1,0:T(8,128)(2,1)}, u32[]{:S(2)}) copy-start(bf16[256,256]{1,0:T(8,128)(2,1)} %param.7) | copy-start | bytes 393220
  0.0 14.6 %collective-permute-start = (bf16[4,32,256]{2,1,0:T(8,128)(2,1)}, bf16[4,32,256]{2,1,0:T(8,128)(2,1)S(1)}, u32[]{:S(2)}, u32[]{:S(2)}) collective-permute-start(bf16[4,32,256]{2,1,0:T(8,128)(2,1)} %param.6), channel_id=1, source_target_pairs={{0,1},{1,2},{2,3},{3,0},{4,5},{5,6},{6,7},{7,4},{8,9},{9,10},{10,1... | collective-permute-start | bytes 196616 | tf_op jit(solution)/shard_map/ppermute | solution.py:129
  3.1 11.9 %collective-permute-start.2 = (bf16[4,32,256]{2,1,0:T(8,128)(2,1)}, bf16[4,32,256]{2,1,0:T(8,128)(2,1)S(1)}, u32[]{:S(2)}, u32[]{:S(2)}) collective-permute-start(bf16[4,32,256]{2,1,0:T(8,128)(2,1)} %param.6), channel_id=1, source_target_pairs={{0,3},{1,0},{2,1},{3,2},{4,7},{5,4},{6,5},{7,6},{8,11},{9,8},{10,9... | collective-permute-start | bytes 196616 | tf_op jit(solution)/shard_map/ppermute | solution.py:129
  5.1 10.1 %collective-permute-start.1 = (bf16[4,32,256]{2,1,0:T(8,128)(2,1)}, bf16[4,32,256]{2,1,0:T(8,128)(2,1)S(1)}, u32[]{:S(2)}, u32[]{:S(2)}) collective-permute-start(bf16[4,32,256]{2,1,0:T(8,128)(2,1)} %param.6), channel_id=1, source_target_pairs={{0,2},{1,3},{2,0},{3,1},{4,6},{5,7},{6,4},{7,5},{8,10},{9,11},{10,... | collective-permute-start | bytes 196616 | tf_op jit(solution)/shard_map/ppermute | solution.py:129
  7.7 4.6 %copy-start.6 = (s32[128]{0:T(128)S(1)}, s32[128]{0:T(128)}, u32[]{:S(2)}) copy-start(s32[128]{0:T(128)} %param.10) | copy-start | bytes 1540
  7.7 4.6 %copy-start.3 = (bf16[4,32,256]{2,1,0:T(8,128)(2,1)S(1)}, bf16[4,32,256]{2,1,0:T(8,128)(2,1)}, u32[]{:S(2)}) copy-start(bf16[4,32,256]{2,1,0:T(8,128)(2,1)} %param.6) | copy-start | bytes 196612
  7.7 4.9 %copy-start.4 = (bf16[128,1024]{1,0:T(8,128)(2,1)S(1)}, bf16[128,1024]{1,0:T(8,128)(2,1)}, u32[]{:S(2)}) copy-start(bf16[128,1024]{1,0:T(8,128)(2,1)} %param.8) | copy-start | bytes 786436
  8.6 14.1 %all-to-all-start = ((bf16[8,144,256]{2,1,0:T(8,128)(2,1)}), bf16[8,144,256]{2,1,0:T(8,128)(2,1)S(1)}, u32[]{:S(2)}, u32[]{:S(2)}) async-start(bf16[8,144,256]{2,1,0:T(8,128)(2,1)} %fusion.1), calls=%async_computation | async-start | bytes 1179648 | tf_op jit(solution)/shard_map/all_to_all | solution.py:154
  12.6 1.7 %copy-start.1 = (f32[128,256]{1,0:T(8,128)}, f32[128,256]{1,0:T(8,128)S(1)}, u32[]{:S(2)}) copy-start(f32[128,256]{1,0:T(8,128)S(1)} %get-tuple-element.16) | copy-start | bytes 393220
  14.9 9.2 %copy-start.5 = (s32[128]{0:T(128)S(1)}, s32[128]{0:T(128)}, u32[]{:S(2)}) copy-start(s32[128]{0:T(128)} %param.9) | copy-start | bytes 1540
  32.8 13.1 %all-to-all-start.1 = ((bf16[32,32,256]{2,1,0:T(8,128)(2,1)}), bf16[32,32,256]{2,1,0:T(8,128)(2,1)S(1)}, u32[]{:S(2)}, u32[]{:S(2)}) async-start(bf16[32,32,256]{2,1,0:T(8,128)(2,1)} %convolution_convert_fusion), calls=%async_computation.1 | async-start | bytes 1048576 | tf_op jit(solution)/shard_map/all_to_all | solution.py:213
  36.8 10.5 %copy-start.2 = (f32[128,256]{1,0:T(8,128)S(1)}, f32[128,256]{1,0:T(8,128)}, u32[]{:S(2)}) copy-start(f32[128,256]{1,0:T(8,128)} %copy-done.1) | copy-start | bytes 393220
  36.9 9.2 %collective-permute-start.5 = (bf16[4,32,256]{2,1,0:T(8,128)(2,1)S(1)}, bf16[4,32,256]{2,1,0:T(8,128)(2,1)S(1)}, u32[]{:S(2)}, u32[]{:S(2)}) collective-permute-start(bf16[4,32,256]{2,1,0:T(8,128)(2,1)S(1)} %bitcast.67), channel_id=1, source_target_pairs={{0,1},{1,2},{2,3},{3,0},{4,5},{5,6},{6,7},{7,4},{8,9},{9,10},{10,1... | collective-permute-start | bytes 196616 | tf_op jit(solution)/shard_map/ppermute | solution.py:204
  38.5 7.6 %collective-permute-start.3 = (bf16[4,32,256]{2,1,0:T(8,128)(2,1)S(1)}, bf16[4,32,256]{2,1,0:T(8,128)(2,1)S(1)}, u32[]{:S(2)}, u32[]{:S(2)}) collective-permute-start(bf16[4,32,256]{2,1,0:T(8,128)(2,1)S(1)} %bitcast.66), channel_id=1, source_target_pairs={{0,3},{1,0},{2,1},{3,2},{4,7},{5,4},{6,5},{7,6},{8,11},{9,8},{10,9... | collective-permute-start | bytes 196616 | tf_op jit(solution)/shard_map/ppermute | solution.py:204
  40.7 6.6 %collective-permute-start.4 = (bf16[4,32,256]{2,1,0:T(8,128)(2,1)S(1)}, bf16[4,32,256]{2,1,0:T(8,128)(2,1)S(1)}, u32[]{:S(2)}, u32[]{:S(2)}) collective-permute-start(bf16[4,32,256]{2,1,0:T(8,128)(2,1)S(1)} %bitcast.65), channel_id=1, source_target_pairs={{0,2},{1,3},{2,0},{3,1},{4,6},{5,7},{6,4},{7,5},{8,10},{9,11},{10,... | collective-permute-start | bytes 196616 | tf_op jit(solution)/shard_map/ppermute | solution.py:204

commit v8 on v6

--- a/solution.py
+++ b/solution.py
@@ -78,8 +78,17 @@
     )(edge_at, blocks)
 
 
-def softmax_bwd_kernel(group, score_scale, s_ref, g_ref, d_ref):
-    expo = jnp.exp(s_ref[...])
+def softmax_bwd_kernel(group, score_scale, p_ref, r_ref, g_ref, pool_ref, slot_ref, slot_acc):
+    step = pl.program_id(0)
+    first_feats = p_ref[...]
+    second_feats = r_ref[...]
+    scores = (
+        lax.dot_general(
+            first_feats, second_feats, (((1,), (1,)), ((), ())), preferred_element_type=jnp.float32
+        )
+        * score_scale
+    )
+    expo = jnp.exp(scores)
     rows = expo / lane_group_sum(expo, group)
     cols = expo / row_group_sum(expo, group)
     grads = g_ref[...].astype(jnp.float32)
@@ -88,28 +97,55 @@
     d_scores = rows * (d_rows - lane_group_sum(d_rows * rows, group)) + cols * (
         d_cols - row_group_sum(d_cols * cols, group)
     )
-    d_ref[...] = (d_scores * score_scale).astype(jnp.bfloat16)
-
-
-def softmax_bwd(scores, grads, group, score_scale):
-    total_rows, width = scores.shape
+    d_scaled = d_scores * score_scale
+    pool_ref[...] = jnp.dot(
+        d_scaled.astype(jnp.bfloat16), second_feats, preferred_element_type=jnp.float32
+    ).astype(pool_ref.dtype)
+    slot_step = jnp.dot(
+        d_scaled.T.astype(jnp.bfloat16), first_feats, preferred_element_type=jnp.float32
+    )
+
+    @pl.when(step == 0)
+    def _():
+        slot_acc[...] = slot_step
+
+    @pl.when(step > 0)
+    def _():
+        slot_acc[...] += slot_step
+
+    @pl.when(step == pl.num_programs(0) - 1)
+    def _():
+        slot_ref[...] = slot_acc[...].astype(slot_ref.dtype)
+
+
+def softmax_bwd(pool2, recv2, grads, group, score_scale):
+    total_rows, width = grads.shape
+    feat_width = pool2.shape[1]
     block = 128 if total_rows % 128 == 0 else total_rows
     return pl.pallas_call(
         functools.partial(softmax_bwd_kernel, group, score_scale),
-        out_shape=jax.ShapeDtypeStruct((total_rows, width), jnp.bfloat16),
+        out_shape=(
+            jax.ShapeDtypeStruct((total_rows, feat_width), jnp.bfloat16),
+            jax.ShapeDtypeStruct((width, feat_width), jnp.bfloat16),
+        ),
         grid=(total_rows // block,),
         in_specs=[
-            pl.BlockSpec((block, width), lambda b: (b, 0)),
+            pl.BlockSpec((block, feat_width), lambda b: (b, 0)),
+            pl.BlockSpec((width, feat_width), lambda b: (0, 0)),
             pl.BlockSpec((block, width), lambda b: (b, 0)),
         ],
-        out_specs=pl.BlockSpec((block, width), lambda b: (b, 0)),
+        out_specs=(
+            pl.BlockSpec((block, feat_width), lambda b: (b, 0)),
+            pl.BlockSpec((width, feat_width), lambda b: (0, 0)),
+        ),
+        scratch_shapes=[pltpu.VMEM((width, feat_width), jnp.float32)],
         compiler_params=pltpu.CompilerParams(vmem_limit_bytes=48 * 1024 * 1024),
         cost_estimate=pl.CostEstimate(
-            flops=30 * total_rows * width,
+            flops=30 * total_rows * width + 6 * total_rows * width * feat_width,
             transcendentals=total_rows * width,
-            bytes_accessed=8 * total_rows * width,
-        ),
-    )(scores, grads)
+            bytes_accessed=2 * total_rows * width + 2 * (total_rows + width) * feat_width,
+        ),
+    )(pool2, recv2, grads)
 
 
 def local(n_grp, n_sub, tokens, proj_weight, match_grad, edge_first, pair_second_image, send_pick):
@@ -184,19 +220,9 @@
     pool2 = pool.reshape(group_img * length, feat_width)
     recv2 = received.reshape(recv * length, feat_width)
     score_scale = 1.0 / (feat_width * SOFTMAX_COOLING)
-    scores = (
-        lax.dot_general(pool2, recv2, (((1,), (1,)), ((), ())), preferred_element_type=jnp.float32)
-        * score_scale
-    )
-    d_scaled = softmax_bwd(scores, grads, length, score_scale)
-    pool_total = jnp.dot(d_scaled, recv2, preferred_element_type=jnp.float32).reshape(
-        group_img, length, feat_width
-    )
-    slot_total = lax.dot_general(
-        d_scaled, pool2, (((0,), (0,)), ((), ())), preferred_element_type=jnp.float32
-    ).reshape(recv, length, feat_width)
-    pool_b = pool_total.astype(jnp.bfloat16)
-    slot_b = slot_total.astype(jnp.bfloat16)
+    pool_b, slot_b = softmax_bwd(pool2, recv2, grads, length, score_scale)
+    pool_b = pool_b.reshape(group_img, length, feat_width)
+    slot_b = slot_b.reshape(recv, length, feat_width)
 
     if SUB_MODE == "perm":
         owned = pool_b[:img_count].astype(jnp.float32)

time: 44.5 us -> 45.6 us (1.025)
  Pallas kernels: 5.9 us -> 9.34 us
  matrix products: 5.19 us -> 2.22 us
  waiting for transfers between devices: 6.77 us -> 9.48 us
  starting transfers between devices: 19 us -> 16.7 us
  local copies, waits for them, and re-layouts: 3.22 us -> 3.88 us
    pallas_call x1, Pallas kernels: 2.6 us -> 6.05 us  [softmax_bwd(): pl.pallas_call(functools.partial(softmax_bwd_kernel, group, score_scale),...]
    dot_general x3 -> x0, matrix products: 2.15 us -> none  [the longest x1 1.22 us: local(): lax.dot_general(d_scaled, pool2, (((0,), (0,)), ((), ())), preferred_elem...]
    all_to_all x1, waiting for transfers between devices: 5.24 us -> 7.13 us  [local(): lax.all_to_all(slot_b, 'grp', split_axis=0, concat_axis=0, tiled=True)]
    ppermute x3, starting transfers between devices: 3.87 us -> 2.41 us  [local(): lax.ppermute(pool_b[k * img_count:(k + 1) * img_count], 'sub', shift(n_su...]
    all_to_all x1, waiting for transfers between devices: 1.2 us -> 2.34 us  [local(): lax.all_to_all(outgoing, 'grp', split_axis=0, concat_axis=0, tiled=True)]
    unnamed x13 -> x17, local copies, waits for them, and re-layouts: 0.2 us -> 1.08 us
    ppermute x3, starting transfers between devices: 7.89 us -> 7.05 us  [local(): lax.ppermute(tokens, 'sub', shift(n_sub, k))]
    dot_general x5, matrix products: 2.21 us -> 1.38 us  [normalize(): jnp.dot(tokens.reshape(image_count * length, feat_width), proj_weight, pr...]
  transfers between devices with their start and end apart: 8 -> 8, of which waited for: 3 -> 2; matrix products, arithmetic and copies ran while one was open for 19% -> 14% of each run, Pallas kernels for 7% -> 7%
where the time goes in v8:
time: 45.6 us; the launch traced here: 45.2 us
  starting transfers between devices  16.7 us (37%)
  waiting for transfers between devices  9.48 us (21%)
  Pallas kernels  9.34 us (20%)
  local copies, waits for them, and re-layouts  3.88 us (9%)
  other arithmetic  3.29 us (7%)
  matrix products  2.22 us (5%)
    all_to_all x1, waiting for transfers between devices, local(): lax.all_to_all(slot_b, 'grp', split_axis=0, concat_axis=0, tiled=True)  7.13 us
    ppermute x3, starting transfers between devices, local(): lax.ppermute(tokens, 'sub', shift(n_sub, k))  7.05 us
    pallas_call x1, Pallas kernels, softmax_bwd(): pl.pallas_call(functools.partial(softmax_bwd_kernel, group, score_scale),...  6.05 us
    all_to_all x1, starting transfers between devices, local(): lax.all_to_all(outgoing, 'grp', split_axis=0, concat_axis=0, tiled=True)  3.72 us
    all_to_all x1, starting transfers between devices, local(): lax.all_to_all(slot_b, 'grp', split_axis=0, concat_axis=0, tiled=True)  3.49 us
    pallas_call x1, Pallas kernels, place_grads(): pl.pallas_call(functools.partial(place_kernel, group, recv), out_shape=ja...  3.29 us
    ppermute x3, starting transfers between devices, local(): lax.ppermute(pool_b[k * img_count:(k + 1) * img_count], 'sub', shift(n_su...  2.41 us
    all_to_all x1, waiting for transfers between devices, local(): lax.all_to_all(outgoing, 'grp', split_axis=0, concat_axis=0, tiled=True)  2.34 us
  transfers between devices with their start and end apart: 8, of which 2 were waited for; matrix products, arithmetic and copies ran while one was open for 14% of the time, Pallas kernels for 7%

profile of v8, /device:TPU:0, one launch (start us, length us, event | category | flops | bytes accessed | tf_op | source)
XLA Modules:
  0.0 45.2 jit_solution(15210171951893531121)
XLA Ops:
  0.0 3.1 %collective-permute-start = (bf16[4,32,256]{2,1,0:T(8,128)(2,1)}, bf16[4,32,256]{2,1,0:T(8,128)(2,1)S(1)}, u32[]{:S(2)}, u32[]{:S(2)}) collective-permute-start(bf16[4,32,256]{2,1,0:T(8,128)(2,1)} %param.6), channel_id=1, source_target_pairs={{0,1},{1,2},{2,3},{3,0},{4,5},{5,6},{6,7},{7,4},{8,9},{9,10},{10,1... | collective-permute-start | bytes 196616 | tf_op jit(solution)/shard_map/ppermute | solution.py:166
  3.1 2.6 %collective-permute-start.1 = (bf16[4,32,256]{2,1,0:T(8,128)(2,1)}, bf16[4,32,256]{2,1,0:T(8,128)(2,1)S(1)}, u32[]{:S(2)}, u32[]{:S(2)}) collective-permute-start(bf16[4,32,256]{2,1,0:T(8,128)(2,1)} %param.6), channel_id=1, source_target_pairs={{0,2},{1,3},{2,0},{3,1},{4,6},{5,7},{6,4},{7,5},{8,10},{9,11},{10,... | collective-permute-start | bytes 196616 | tf_op jit(solution)/shard_map/ppermute | solution.py:166
  5.7 1.3 %collective-permute-start.2 = (bf16[4,32,256]{2,1,0:T(8,128)(2,1)}, bf16[4,32,256]{2,1,0:T(8,128)(2,1)S(1)}, u32[]{:S(2)}, u32[]{:S(2)}) collective-permute-start(bf16[4,32,256]{2,1,0:T(8,128)(2,1)} %param.6), channel_id=1, source_target_pairs={{0,3},{1,0},{2,1},{3,2},{4,7},{5,4},{6,5},{7,6},{8,11},{9,8},{10,9... | collective-permute-start | bytes 196616 | tf_op jit(solution)/shard_map/ppermute | solution.py:166
  7.1 0.8 %slice_bitcast_fusion.3 = (bf16[32,256]{1,0:T(8,128)(2,1)S(1)}, bf16[32,256]{1,0:T(8,128)(2,1)S(1)}, bf16[32,256]{1,0:T(8,128)(2,1)S(1)}, bf16[32,256]{1,0:T(8,128)(2,1)S(1)}) fusion(bf16[4,32,256]{2,1,0:T(8,128)(2,1)} %param.6), kind=kLoop, calls=%fused_computation.29 | loop fusion | bytes 131072 | tf_op jit(solution)/shard_map/squeeze | solution.py:188
  7.8 0.7 %broadcast_compare_fusion.2 = (pred[32]{0:T(512)(128)(4,1)S(1)}, pred[32]{0:T(512)(128)(4,1)S(1)}, pred[32]{0:T(512)(128)(4,1)S(1)}) fusion(s32[32]{0:T(128)} %param.11), kind=kLoop, calls=%fused_computation.49 | loop fusion | flops 96 | bytes 224 | tf_op jit(solution)/shard_map/eq | solution.py:188
  8.5 1.0 %select_select_fusion = bf16[32,32,256]{2,1,0:T(8,128)(2,1)} fusion(pred[32]{0:T(512)(128)(4,1)S(1)} %get-tuple-element.19, pred[32]{0:T(512)(128)(4,1)S(1)} %get-tuple-element.18, pred[32]{0:T(512)(128)(4,1)S(1)} %get-tuple-element.17, bf16[32,256]{1,0:T(8,128)(2,1)S(1)} %get-tuple-element.15, bf16[32,256]{1,0:T(8,128)(2,1)S(1)} %get-tuple-element.16, ...), kind=kLoop, calls=%fused_computation.4 | loop fusion | flops 786432 | bytes 589920 | tf_op jit(solution)/shard_map/jit(_where)/select_n | solution.py:188
  9.5 3.7 %all-to-all-start = ((bf16[32,32,256]{2,1,0:T(8,128)(2,1)}), bf16[32,32,256]{2,1,0:T(8,128)(2,1)S(1)}, u32[]{:S(2)}, u32[]{:S(2)}) async-start(bf16[32,32,256]{2,1,0:T(8,128)(2,1)} %select_select_fusion), calls=%async_computation | async-start | bytes 1048576 | tf_op jit(solution)/shard_map/all_to_all | solution.py:201
  13.2 0.3 multiply_reduce_fusion.4
  13.7 1.5 %copy.13 = bf16[128,32,32]{2,1,0:T(8,128)(2,1)S(1)} copy(bf16[128,32,32]{0,2,1:T(8,128)(2,1)S(1)} %bitcast.49) | data formatting | bytes 524288 | tf_op jit(solution)/shard_map/reshape | solution.py:216
  15.5 0.4 copy-done.6
  16.1 3.3 %shard_map.64.g_ref = bf16[512,1024]{1,0:T(8,128)(2,1)S(1)} custom-call(s32[512]{0:T(512)S(1)} %select_reduce_fusion.1.edge_at_ref, bf16[129,32,32]{2,1,0:T(8,128)(2,1)S(1)} %concatenate.7.m_ref), custom_call_target="tpu_custom_call" | custom-call | bytes 1312768 | tf_op jit(solution)/shard_map/pallas_call | solution.py:65
  19.7 0.3 multiply_reduce_fusion.2
  20.0 0.3 multiply_reduce_fusion.1
  20.6 2.3 %all-to-all-done = bf16[32,32,256]{2,1,0:T(8,128)(2,1)S(1)} async-done(((bf16[32,32,256]{2,1,0:T(8,128)(2,1)}), bf16[32,32,256]{2,1,0:T(8,128)(2,1)S(1)}, u32[]{:S(2)}, u32[]{:S(2)}) %all-to-all-start) | async-done | bytes 524320 | tf_op jit(solution)/shard_map/all_to_all | solution.py:201
  22.9 0.4 multiply_reduce_fusion
  23.3 0.3 copy.11
  23.8 6.0 %shard_map.65 = (bf16[512,256]{1,0:T(8,128)(2,1)S(1)}, bf16[1024,256]{1,0:T(8,128)(2,1)}) custom-call(bf16[512,256]{1,0:T(8,128)(2,1)S(1)} %bitcast.47, bf16[1024,256]{1,0:T(8,128)(2,1)S(1)} %multiply_convert_fusion.r_ref, bf16[512,1024]{1,0:T(8,128)(2,1)S(1)} %shard_map.64.g_ref), custom_call_target="tpu_custom_call" | custom-call | flops 821035008 | bytes 1835008 | tf_op jit(solution)/shard_map/pallas_call | solution.py:125
  29.9 3.5 %all-to-all-start.1 = ((bf16[32,32,256]{2,1,0:T(8,128)(2,1)}), bf16[32,32,256]{2,1,0:T(8,128)(2,1)S(1)}, u32[]{:S(2)}, u32[]{:S(2)}) async-start(bf16[32,32,256]{2,1,0:T(8,128)(2,1)} %bitcast.19), calls=%async_computation.1 | async-start | bytes 1048576 | tf_op jit(solution)/shard_map/all_to_all | solution.py:249
  33.5 0.5 %collective-permute-start.3 = (bf16[4,32,256]{2,1,0:T(8,128)(2,1)S(1)}, bf16[4,32,256]{2,1,0:T(8,128)(2,1)S(1)}, u32[]{:S(2)}, u32[]{:S(2)}) collective-permute-start(bf16[4,32,256]{2,1,0:T(8,128)(2,1)S(1)} %bitcast.61), channel_id=1, source_target_pairs={{0,3},{1,0},{2,1},{3,2},{4,7},{5,4},{6,5},{7,6},{8,11},{9,8},{10,9... | collective-permute-start | bytes 196616 | tf_op jit(solution)/shard_map/ppermute | solution.py:230
  34.0 1.7 %collective-permute-start.4 = (bf16[4,32,256]{2,1,0:T(8,128)(2,1)S(1)}, bf16[4,32,256]{2,1,0:T(8,128)(2,1)S(1)}, u32[]{:S(2)}, u32[]{:S(2)}) collective-permute-start(bf16[4,32,256]{2,1,0:T(8,128)(2,1)S(1)} %bitcast.60), channel_id=1, source_target_pairs={{0,2},{1,3},{2,0},{3,1},{4,6},{5,7},{6,4},{7,5},{8,10},{9,11},{10,... | collective-permute-start | bytes 196616 | tf_op jit(solution)/shard_map/ppermute | solution.py:230
  35.9 7.1 %all-to-all-done.1 = bf16[32,32,256]{2,1,0:T(8,128)(2,1)S(1)} async-done(((bf16[32,32,256]{2,1,0:T(8,128)(2,1)}), bf16[32,32,256]{2,1,0:T(8,128)(2,1)S(1)}, u32[]{:S(2)}, u32[]{:S(2)}) %all-to-all-start.1) | async-done | bytes 524320 | tf_op jit(solution)/shard_map/all_to_all | solution.py:249
  43.2 0.4 select_reduce_fusion
  43.6 0.5 %copy-done.2 = f32[128,256]{1,0:T(8,128)S(1)} copy-done((f32[128,256]{1,0:T(8,128)S(1)}, f32[128,256]{1,0:T(8,128)}, u32[]{:S(2)}) %copy-start.2) | copy-done | bytes 131096
  44.4 0.8 %convolution_convert_fusion = bf16[128,256]{1,0:T(8,128)(2,1)} fusion(bf16[128,256]{1,0:T(8,128)(2,1)S(1)} %fusion.5, bf16[256,256]{1,0:T(8,128)(2,1)S(1)} %copy-done), kind=kOutput, calls=%fused_computation.1 | convolution fusion | flops 16809984 | bytes 262144 | tf_op jit(solution)/shard_map/nk,dk->nd/dot_general | solution.py:262
  (44 shorter events, 2.2 us)
Async XLA Ops:
  0.0 13.2 %copy-start = (bf16[256,256]{1,0:T(8,128)(2,1)S(1)}, bf16[256,256]{1,0:T(8,128)(2,1)}, u32[]{:S(2)}) copy-start(bf16[256,256]{1,0:T(8,128)(2,1)} %param.7) | copy-start | bytes 393220
  0.0 13.2 %copy-start.3 = (bf16[4,32,256]{2,1,0:T(8,128)(2,1)S(1)}, bf16[4,32,256]{2,1,0:T(8,128)(2,1)}, u32[]{:S(2)}) copy-start(bf16[4,32,256]{2,1,0:T(8,128)(2,1)} %param.6) | copy-start | bytes 196612
  0.0 13.5 %copy-start.4 = (bf16[128,1024]{1,0:T(8,128)(2,1)S(1)}, bf16[128,1024]{1,0:T(8,128)(2,1)}, u32[]{:S(2)}) copy-start(bf16[128,1024]{1,0:T(8,128)(2,1)} %param.8) | copy-start | bytes 786436
  0.0 19.4 %collective-permute-start = (bf16[4,32,256]{2,1,0:T(8,128)(2,1)}, bf16[4,32,256]{2,1,0:T(8,128)(2,1)S(1)}, u32[]{:S(2)}, u32[]{:S(2)}) collective-permute-start(bf16[4,32,256]{2,1,0:T(8,128)(2,1)} %param.6), channel_id=1, source_target_pairs={{0,1},{1,2},{2,3},{3,0},{4,5},{5,6},{6,7},{7,4},{8,9},{9,10},{10,1... | collective-permute-start | bytes 196616 | tf_op jit(solution)/shard_map/ppermute | solution.py:166
  3.1 16.6 %collective-permute-start.1 = (bf16[4,32,256]{2,1,0:T(8,128)(2,1)}, bf16[4,32,256]{2,1,0:T(8,128)(2,1)S(1)}, u32[]{:S(2)}, u32[]{:S(2)}) collective-permute-start(bf16[4,32,256]{2,1,0:T(8,128)(2,1)} %param.6), channel_id=1, source_target_pairs={{0,2},{1,3},{2,0},{3,1},{4,6},{5,7},{6,4},{7,5},{8,10},{9,11},{10,... | collective-permute-start | bytes 196616 | tf_op jit(solution)/shard_map/ppermute | solution.py:166
  5.7 14.3 %collective-permute-start.2 = (bf16[4,32,256]{2,1,0:T(8,128)(2,1)}, bf16[4,32,256]{2,1,0:T(8,128)(2,1)S(1)}, u32[]{:S(2)}, u32[]{:S(2)}) collective-permute-start(bf16[4,32,256]{2,1,0:T(8,128)(2,1)} %param.6), channel_id=1, source_target_pairs={{0,3},{1,0},{2,1},{3,2},{4,7},{5,4},{6,5},{7,6},{8,11},{9,8},{10,9... | collective-permute-start | bytes 196616 | tf_op jit(solution)/shard_map/ppermute | solution.py:166
  9.5 13.4 %all-to-all-start = ((bf16[32,32,256]{2,1,0:T(8,128)(2,1)}), bf16[32,32,256]{2,1,0:T(8,128)(2,1)S(1)}, u32[]{:S(2)}, u32[]{:S(2)}) async-start(bf16[32,32,256]{2,1,0:T(8,128)(2,1)} %select_select_fusion), calls=%async_computation | async-start | bytes 1048576 | tf_op jit(solution)/shard_map/all_to_all | solution.py:201
  13.5 2.0 %copy-start.1 = (f32[128,256]{1,0:T(8,128)}, f32[128,256]{1,0:T(8,128)S(1)}, u32[]{:S(2)}) copy-start(f32[128,256]{1,0:T(8,128)S(1)} %get-tuple-element.27) | copy-start | bytes 393220
  15.2 0.7 %copy-start.6 = (s32[128]{0:T(128)S(1)}, s32[128]{0:T(128)}, u32[]{:S(2)}) copy-start(s32[128]{0:T(128)} %param.10) | copy-start | bytes 1540
  15.2 0.7 %copy-start.7 = (s32[128]{0:T(128)S(1)}, s32[128]{0:T(128)}, u32[]{:S(2)}) copy-start(s32[128]{0:T(128)} %param.9) | copy-start | bytes 1540
  23.8 9.6 %copy-start.5 = (s32[32]{0:T(128)S(1)}, s32[32]{0:T(128)}, u32[]{:S(2)}) copy-start(s32[32]{0:T(128)} %param.11) | copy-start | bytes 388
  29.9 13.1 %all-to-all-start.1 = ((bf16[32,32,256]{2,1,0:T(8,128)(2,1)}), bf16[32,32,256]{2,1,0:T(8,128)(2,1)S(1)}, u32[]{:S(2)}, u32[]{:S(2)}) async-start(bf16[32,32,256]{2,1,0:T(8,128)(2,1)} %bitcast.19), calls=%async_computation.1 | async-start | bytes 1048576 | tf_op jit(solution)/shard_map/all_to_all | solution.py:249
  33.5 10.0 %collective-permute-start.3 = (bf16[4,32,256]{2,1,0:T(8,128)(2,1)S(1)}, bf16[4,32,256]{2,1,0:T(8,128)(2,1)S(1)}, u32[]{:S(2)}, u32[]{:S(2)}) collective-permute-start(bf16[4,32,256]{2,1,0:T(8,128)(2,1)S(1)} %bitcast.61), channel_id=1, source_target_pairs={{0,3},{1,0},{2,1},{3,2},{4,7},{5,4},{6,5},{7,6},{8,11},{9,8},{10,9... | collective-permute-start | bytes 196616 | tf_op jit(solution)/shard_map/ppermute | solution.py:230
  34.0 9.5 %collective-permute-start.4 = (bf16[4,32,256]{2,1,0:T(8,128)(2,1)S(1)}, bf16[4,32,256]{2,1,0:T(8,128)(2,1)S(1)}, u32[]{:S(2)}, u32[]{:S(2)}) collective-permute-start(bf16[4,32,256]{2,1,0:T(8,128)(2,1)S(1)} %bitcast.60), channel_id=1, source_target_pairs={{0,2},{1,3},{2,0},{3,1},{4,6},{5,7},{6,4},{7,5},{8,10},{9,11},{10,... | collective-permute-start | bytes 196616 | tf_op jit(solution)/shard_map/ppermute | solution.py:230
  35.7 7.9 %collective-permute-start.5 = (bf16[4,32,256]{2,1,0:T(8,128)(2,1)S(1)}, bf16[4,32,256]{2,1,0:T(8,128)(2,1)S(1)}, u32[]{:S(2)}, u32[]{:S(2)}) collective-permute-start(bf16[4,32,256]{2,1,0:T(8,128)(2,1)S(1)} %bitcast.59), channel_id=1, source_target_pairs={{0,1},{1,2},{2,3},{3,0},{4,5},{5,6},{6,7},{7,4},{8,9},{9,10},{10,1... | collective-permute-start | bytes 196616 | tf_op jit(solution)/shard_map/ppermute | solution.py:230
  43.2 0.9 %copy-start.2 = (f32[128,256]{1,0:T(8,128)S(1)}, f32[128,256]{1,0:T(8,128)}, u32[]{:S(2)}) copy-start(f32[128,256]{1,0:T(8,128)} %copy-done.1) | copy-start | bytes 393220

commit v9 on v6

--- a/solution.py
+++ b/solution.py
@@ -78,7 +78,7 @@
     )(edge_at, blocks)
 
 
-def softmax_bwd_kernel(group, score_scale, s_ref, g_ref, d_ref):
+def softmax_bwd_kernel(group, score_scale, s_ref, g_ref, d_ref, dt_ref):
     expo = jnp.exp(s_ref[...])
     rows = expo / lane_group_sum(expo, group)
     cols = expo / row_group_sum(expo, group)
@@ -88,7 +88,9 @@
     d_scores = rows * (d_rows - lane_group_sum(d_rows * rows, group)) + cols * (
         d_cols - row_group_sum(d_cols * cols, group)
     )
-    d_ref[...] = (d_scores * score_scale).astype(jnp.bfloat16)
+    d_scaled = d_scores * score_scale
+    d_ref[...] = d_scaled.astype(jnp.bfloat16)
+    dt_ref[...] = d_scaled.T.astype(jnp.bfloat16)
 
 
 def softmax_bwd(scores, grads, group, score_scale):
@@ -96,13 +98,19 @@
     block = 128 if total_rows % 128 == 0 else total_rows
     return pl.pallas_call(
         functools.partial(softmax_bwd_kernel, group, score_scale),
-        out_shape=jax.ShapeDtypeStruct((total_rows, width), jnp.bfloat16),
+        out_shape=(
+            jax.ShapeDtypeStruct((total_rows, width), jnp.bfloat16),
+            jax.ShapeDtypeStruct((width, total_rows), jnp.bfloat16),
+        ),
         grid=(total_rows // block,),
         in_specs=[
             pl.BlockSpec((block, width), lambda b: (b, 0)),
             pl.BlockSpec((block, width), lambda b: (b, 0)),
         ],
-        out_specs=pl.BlockSpec((block, width), lambda b: (b, 0)),
+        out_specs=(
+            pl.BlockSpec((block, width), lambda b: (b, 0)),
+            pl.BlockSpec((width, block), lambda b: (0, b)),
+        ),
         compiler_params=pltpu.CompilerParams(vmem_limit_bytes=48 * 1024 * 1024),
         cost_estimate=pl.CostEstimate(
             flops=30 * total_rows * width,
@@ -188,13 +196,13 @@
         lax.dot_general(pool2, recv2, (((1,), (1,)), ((), ())), preferred_element_type=jnp.float32)
         * score_scale
     )
-    d_scaled = softmax_bwd(scores, grads, length, score_scale)
+    d_scaled, d_scaled_t = softmax_bwd(scores, grads, length, score_scale)
     pool_total = jnp.dot(d_scaled, recv2, preferred_element_type=jnp.float32).reshape(
         group_img, length, feat_width
     )
-    slot_total = lax.dot_general(
-        d_scaled, pool2, (((0,), (0,)), ((), ())), preferred_element_type=jnp.float32
-    ).reshape(recv, length, feat_width)
+    slot_total = jnp.dot(d_scaled_t, pool2, preferred_element_type=jnp.float32).reshape(
+        recv, length, feat_width
+    )
     pool_b = pool_total.astype(jnp.bfloat16)
     slot_b = slot_total.astype(jnp.bfloat16)
 

time: 44.5 us -> 43.2 us (0.971)
  starting transfers between devices: 19 us -> 16.6 us
  waiting for transfers between devices: 6.77 us -> 7.92 us
  local copies, waits for them, and re-layouts: 3.22 us -> 2.67 us
    all_to_all x1, waiting for transfers between devices: 5.24 us -> 6.71 us  [local(): lax.all_to_all(slot_b, 'grp', split_axis=0, concat_axis=0, tiled=True)]
    ppermute x3, starting transfers between devices: 3.87 us -> 2.42 us  [local(): lax.ppermute(pool_b[k * img_count:(k + 1) * img_count], 'sub', shift(n_su...]
    ppermute x3, starting transfers between devices: 7.89 us -> 6.99 us  [local(): lax.ppermute(tokens, 'sub', shift(n_sub, k))]
    dot_general x1 -> x0, local copies, waits for them, and re-layouts: 0.54 us -> none  [local(): lax.dot_general(d_scaled, pool2, (((0,), (0,)), ((), ())), preferred_elem...]
  transfers between devices with their start and end apart: 8 -> 8, of which waited for: 3 -> 2; matrix products, arithmetic and copies ran while one was open for 19% -> 20% of each run, Pallas kernels for 7% -> 8%
where the time goes in v9:
time: 43.2 us; the launch traced here: 42.8 us
  starting transfers between devices  16.6 us (38%)
  waiting for transfers between devices  7.92 us (18%)
  Pallas kernels  6.33 us (15%)
  matrix products  5.18 us (12%)
  other arithmetic  3.72 us (9%)
  local copies, waits for them, and re-layouts  2.67 us (6%)
    ppermute x3, starting transfers between devices, local(): lax.ppermute(tokens, 'sub', shift(n_sub, k))  6.99 us
    all_to_all x1, waiting for transfers between devices, local(): lax.all_to_all(slot_b, 'grp', split_axis=0, concat_axis=0, tiled=True)  6.71 us
    all_to_all x1, starting transfers between devices, local(): lax.all_to_all(outgoing, 'grp', split_axis=0, concat_axis=0, tiled=True)  3.72 us
    all_to_all x1, starting transfers between devices, local(): lax.all_to_all(slot_b, 'grp', split_axis=0, concat_axis=0, tiled=True)  3.49 us
    pallas_call x1, Pallas kernels, place_grads(): pl.pallas_call(functools.partial(place_kernel, group, recv), out_shape=ja...  3.29 us
    pallas_call x1, Pallas kernels, softmax_bwd(): pl.pallas_call(functools.partial(softmax_bwd_kernel, group, score_scale),...  3.04 us
    ppermute x3, starting transfers between devices, local(): lax.ppermute(pool_b[k * img_count:(k + 1) * img_count], 'sub', shift(n_su...  2.42 us
    dot_general x5, matrix products, normalize(): jnp.dot(tokens.reshape(image_count * length, feat_width), proj_weight, pr...  2.21 us
  transfers between devices with their start and end apart: 8, of which 2 were waited for; matrix products, arithmetic and copies ran while one was open for 20% of the time, Pallas kernels for 8%

profile of v9, /device:TPU:0, one launch (start us, length us, event | category | flops | bytes accessed | tf_op | source)
XLA Modules:
  0.0 42.8 jit_solution(7965412478642520485)
XLA Ops:
  0.0 3.1 %collective-permute-start = (bf16[4,32,256]{2,1,0:T(8,128)(2,1)}, bf16[4,32,256]{2,1,0:T(8,128)(2,1)S(1)}, u32[]{:S(2)}, u32[]{:S(2)}) collective-permute-start(bf16[4,32,256]{2,1,0:T(8,128)(2,1)} %param.6), channel_id=1, source_target_pairs={{0,1},{1,2},{2,3},{3,0},{4,5},{5,6},{6,7},{7,4},{8,9},{9,10},{10,1... | collective-permute-start | bytes 196616 | tf_op jit(solution)/shard_map/ppermute | solution.py:138
  3.1 2.6 %collective-permute-start.1 = (bf16[4,32,256]{2,1,0:T(8,128)(2,1)}, bf16[4,32,256]{2,1,0:T(8,128)(2,1)S(1)}, u32[]{:S(2)}, u32[]{:S(2)}) collective-permute-start(bf16[4,32,256]{2,1,0:T(8,128)(2,1)} %param.6), channel_id=1, source_target_pairs={{0,2},{1,3},{2,0},{3,1},{4,6},{5,7},{6,4},{7,5},{8,10},{9,11},{10,... | collective-permute-start | bytes 196616 | tf_op jit(solution)/shard_map/ppermute | solution.py:138
  5.6 1.3 %collective-permute-start.2 = (bf16[4,32,256]{2,1,0:T(8,128)(2,1)}, bf16[4,32,256]{2,1,0:T(8,128)(2,1)S(1)}, u32[]{:S(2)}, u32[]{:S(2)}) collective-permute-start(bf16[4,32,256]{2,1,0:T(8,128)(2,1)} %param.6), channel_id=1, source_target_pairs={{0,3},{1,0},{2,1},{3,2},{4,7},{5,4},{6,5},{7,6},{8,11},{9,8},{10,9... | collective-permute-start | bytes 196616 | tf_op jit(solution)/shard_map/ppermute | solution.py:138
  7.0 0.8 %slice_bitcast_fusion.3 = (bf16[32,256]{1,0:T(8,128)(2,1)S(1)}, bf16[32,256]{1,0:T(8,128)(2,1)S(1)}, bf16[32,256]{1,0:T(8,128)(2,1)S(1)}, bf16[32,256]{1,0:T(8,128)(2,1)S(1)}) fusion(bf16[4,32,256]{2,1,0:T(8,128)(2,1)} %param.6), kind=kLoop, calls=%fused_computation.32 | loop fusion | bytes 131072 | tf_op jit(solution)/shard_map/squeeze | solution.py:160
  7.8 0.7 %broadcast_compare_fusion.2 = (pred[32]{0:T(512)(128)(4,1)S(1)}, pred[32]{0:T(512)(128)(4,1)S(1)}, pred[32]{0:T(512)(128)(4,1)S(1)}) fusion(s32[32]{0:T(128)} %param.11), kind=kLoop, calls=%fused_computation.52 | loop fusion | flops 96 | bytes 224 | tf_op jit(solution)/shard_map/eq | solution.py:160
  8.5 1.0 %select_select_fusion = bf16[32,32,256]{2,1,0:T(8,128)(2,1)} fusion(pred[32]{0:T(512)(128)(4,1)S(1)} %get-tuple-element.19, pred[32]{0:T(512)(128)(4,1)S(1)} %get-tuple-element.18, pred[32]{0:T(512)(128)(4,1)S(1)} %get-tuple-element.17, bf16[32,256]{1,0:T(8,128)(2,1)S(1)} %get-tuple-element.15, bf16[32,256]{1,0:T(8,128)(2,1)S(1)} %get-tuple-element.16, ...), kind=kLoop, calls=%fused_computation.7 | loop fusion | flops 786432 | bytes 589920 | tf_op jit(solution)/shard_map/jit(_where)/select_n | solution.py:160
  9.4 3.7 %all-to-all-start = ((bf16[32,32,256]{2,1,0:T(8,128)(2,1)}), bf16[32,32,256]{2,1,0:T(8,128)(2,1)S(1)}, u32[]{:S(2)}, u32[]{:S(2)}) async-start(bf16[32,32,256]{2,1,0:T(8,128)(2,1)} %select_select_fusion), calls=%async_computation | async-start | bytes 1048576 | tf_op jit(solution)/shard_map/all_to_all | solution.py:173
  13.1 0.7 %iota_compare_fusion.1 = pred[32,4]{1,0:T(8,128)(4,1)S(1)} fusion(s32[32]{0:T(128)} %param.11), kind=kLoop, calls=%fused_computation.28 | loop fusion | flops 128 | bytes 256 | tf_op jit(solution)/shard_map/eq | solution.py:232
  13.9 1.1 %multiply_reduce_fusion.4 = (f32[128]{0:T(128)S(1)}, f32[128,256]{1,0:T(8,128)S(1)}) fusion(bf16[128,256]{1,0:T(8,128)(2,1)} %bitcast.58, bf16[256,256]{1,0:T(8,128)(2,1)S(1)} %copy-done), kind=kOutput, calls=%fused_computation.26 | convolution fusion | flops 16842624 | bytes 328192 | tf_op jit(solution)/shard_map/dot_general | solution.py:18
  15.2 1.5 %copy.10 = bf16[128,32,32]{2,1,0:T(8,128)(2,1)S(1)} copy(bf16[128,32,32]{0,2,1:T(8,128)(2,1)S(1)} %bitcast.57) | data formatting | bytes 524288 | tf_op jit(solution)/shard_map/reshape | solution.py:188
  17.2 3.3 %shard_map.64.g_ref = bf16[512,1024]{1,0:T(8,128)(2,1)S(1)} custom-call(s32[512]{0:T(512)S(1)} %select_reduce_fusion.1.edge_at_ref, bf16[129,32,32]{2,1,0:T(8,128)(2,1)S(1)} %concatenate.7.m_ref), custom_call_target="tpu_custom_call" | custom-call | bytes 1312768 | tf_op jit(solution)/shard_map/pallas_call | solution.py:65
  20.8 0.3 multiply_reduce_fusion.2
  21.6 1.2 %all-to-all-done = bf16[32,32,256]{2,1,0:T(8,128)(2,1)S(1)} async-done(((bf16[32,32,256]{2,1,0:T(8,128)(2,1)}), bf16[32,32,256]{2,1,0:T(8,128)(2,1)S(1)}, u32[]{:S(2)}, u32[]{:S(2)}) %all-to-all-start) | async-done | bytes 524320 | tf_op jit(solution)/shard_map/all_to_all | solution.py:173
  22.8 0.4 multiply_reduce_fusion
  23.2 0.4 %convolution_multiply_fusion.s_ref = f32[512,1024]{1,0:T(8,128)S(1)} fusion(bf16[512,256]{1,0:T(8,128)(2,1)S(1)} %bitcast.54, f32[1024,256]{0,1:T(8,128)S(1)} %get-tuple-element.29, f32[1024]{0:T(1024)S(1)} %add_rsqrt_fusion), kind=kOutput, calls=%fused_computation.1 | convolution fusion | flops 269484032 | bytes 3411968 | tf_op jit(solution)/shard_map/dot_general | solution.py:196
  23.7 3.0 %shard_map.65 = (bf16[512,1024]{1,0:T(8,128)(2,1)S(1)}, bf16[1024,512]{1,0:T(8,128)(2,1)S(1)}) custom-call(f32[512,1024]{1,0:T(8,128)S(1)} %convolution_multiply_fusion.s_ref, bf16[512,1024]{1,0:T(8,128)(2,1)S(1)} %shard_map.64.g_ref), custom_call_target="tpu_custom_call" | custom-call | flops 15728640 | bytes 4194304 | tf_op jit(solution)/shard_map/pallas_call | solution.py:99
  26.7 1.2 %convolution_convert_fusion = bf16[32,32,256]{2,1,0:T(8,128)(2,1)} fusion(bf16[32,32,512]{2,1,0:T(8,128)(2,1)S(1)} %bitcast.53, bf16[512,256,1]{1,0,2:T(8,128)(2,1)S(1)} %bitcast.55), kind=kOutput, calls=%fused_computation.2 | convolution fusion | flops 268697600 | bytes 1835008 | tf_op jit(solution)/shard_map/dot_general | solution.py:203
  27.9 3.5 %all-to-all-start.1 = ((bf16[32,32,256]{2,1,0:T(8,128)(2,1)}), bf16[32,32,256]{2,1,0:T(8,128)(2,1)S(1)}, u32[]{:S(2)}, u32[]{:S(2)}) async-start(bf16[32,32,256]{2,1,0:T(8,128)(2,1)} %convolution_convert_fusion), calls=%async_computation.1 | async-start | bytes 1048576 | tf_op jit(solution)/shard_map/all_to_all | solution.py:231
  31.4 0.5 %convolution_convert_fusion.1 = bf16[512,256]{1,0:T(8,128)(2,1)S(1)} fusion(bf16[512,1024]{1,0:T(8,128)(2,1)S(1)} %get-tuple-element.7, f32[1024,256]{0,1:T(8,128)S(1)} %get-tuple-element.29, f32[1024]{0:T(1024)S(1)} %add_rsqrt_fusion), kind=kOutput, calls=%fused_computation.3 | convolution fusion | flops 269090816 | bytes 2363392 | tf_op jit(solution)/shard_map/dot_general | solution.py:200
  31.9 0.5 %collective-permute-start.3 = (bf16[4,32,256]{2,1,0:T(8,128)(2,1)S(1)}, bf16[4,32,256]{2,1,0:T(8,128)(2,1)S(1)}, u32[]{:S(2)}, u32[]{:S(2)}) collective-permute-start(bf16[4,32,256]{2,1,0:T(8,128)(2,1)S(1)} %bitcast.69), channel_id=1, source_target_pairs={{0,3},{1,0},{2,1},{3,2},{4,7},{5,4},{6,5},{7,6},{8,11},{9,8},{10,9... | collective-permute-start | bytes 196616 | tf_op jit(solution)/shard_map/ppermute | solution.py:212
  32.5 1.7 %collective-permute-start.4 = (bf16[4,32,256]{2,1,0:T(8,128)(2,1)S(1)}, bf16[4,32,256]{2,1,0:T(8,128)(2,1)S(1)}, u32[]{:S(2)}, u32[]{:S(2)}) collective-permute-start(bf16[4,32,256]{2,1,0:T(8,128)(2,1)S(1)} %bitcast.68), channel_id=1, source_target_pairs={{0,2},{1,3},{2,0},{3,1},{4,6},{5,7},{6,4},{7,5},{8,10},{9,11},{10,... | collective-permute-start | bytes 196616 | tf_op jit(solution)/shard_map/ppermute | solution.py:212
  34.4 6.7 %all-to-all-done.1 = bf16[32,32,256]{2,1,0:T(8,128)(2,1)S(1)} async-done(((bf16[32,32,256]{2,1,0:T(8,128)(2,1)}), bf16[32,32,256]{2,1,0:T(8,128)(2,1)S(1)}, u32[]{:S(2)}, u32[]{:S(2)}) %all-to-all-start.1) | async-done | bytes 524320 | tf_op jit(solution)/shard_map/all_to_all | solution.py:231
  41.2 0.4 select_reduce_fusion
  42.0 0.8 %convolution_convert_fusion.2 = bf16[128,256]{1,0:T(8,128)(2,1)} fusion(bf16[128,256]{1,0:T(8,128)(2,1)S(1)} %fusion.5, bf16[256,256]{1,0:T(8,128)(2,1)S(1)} %copy-done), kind=kOutput, calls=%fused_computation.4 | convolution fusion | flops 16809984 | bytes 262144 | tf_op jit(solution)/shard_map/nk,dk->nd/dot_general | solution.py:244
  (41 shorter events, 2.2 us)
Async XLA Ops:
  0.0 13.9 %copy-start = (bf16[256,256]{1,0:T(8,128)(2,1)S(1)}, bf16[256,256]{1,0:T(8,128)(2,1)}, u32[]{:S(2)}) copy-start(bf16[256,256]{1,0:T(8,128)(2,1)} %param.7) | copy-start | bytes 393220
  0.0 15.0 %copy-start.3 = (bf16[128,1024]{1,0:T(8,128)(2,1)S(1)}, bf16[128,1024]{1,0:T(8,128)(2,1)}, u32[]{:S(2)}) copy-start(bf16[128,1024]{1,0:T(8,128)(2,1)} %param.8) | copy-start | bytes 786436
  0.0 20.5 %collective-permute-start = (bf16[4,32,256]{2,1,0:T(8,128)(2,1)}, bf16[4,32,256]{2,1,0:T(8,128)(2,1)S(1)}, u32[]{:S(2)}, u32[]{:S(2)}) collective-permute-start(bf16[4,32,256]{2,1,0:T(8,128)(2,1)} %param.6), channel_id=1, source_target_pairs={{0,1},{1,2},{2,3},{3,0},{4,5},{5,6},{6,7},{7,4},{8,9},{9,10},{10,1... | collective-permute-start | bytes 196616 | tf_op jit(solution)/shard_map/ppermute | solution.py:138
  3.1 17.7 %collective-permute-start.1 = (bf16[4,32,256]{2,1,0:T(8,128)(2,1)}, bf16[4,32,256]{2,1,0:T(8,128)(2,1)S(1)}, u32[]{:S(2)}, u32[]{:S(2)}) collective-permute-start(bf16[4,32,256]{2,1,0:T(8,128)(2,1)} %param.6), channel_id=1, source_target_pairs={{0,2},{1,3},{2,0},{3,1},{4,6},{5,7},{6,4},{7,5},{8,10},{9,11},{10,... | collective-permute-start | bytes 196616 | tf_op jit(solution)/shard_map/ppermute | solution.py:138
  5.6 15.4 %collective-permute-start.2 = (bf16[4,32,256]{2,1,0:T(8,128)(2,1)}, bf16[4,32,256]{2,1,0:T(8,128)(2,1)S(1)}, u32[]{:S(2)}, u32[]{:S(2)}) collective-permute-start(bf16[4,32,256]{2,1,0:T(8,128)(2,1)} %param.6), channel_id=1, source_target_pairs={{0,3},{1,0},{2,1},{3,2},{4,7},{5,4},{6,5},{7,6},{8,11},{9,8},{10,9... | collective-permute-start | bytes 196616 | tf_op jit(solution)/shard_map/ppermute | solution.py:138
  9.4 13.4 %all-to-all-start = ((bf16[32,32,256]{2,1,0:T(8,128)(2,1)}), bf16[32,32,256]{2,1,0:T(8,128)(2,1)S(1)}, u32[]{:S(2)}, u32[]{:S(2)}) async-start(bf16[32,32,256]{2,1,0:T(8,128)(2,1)} %select_select_fusion), calls=%async_computation | async-start | bytes 1048576 | tf_op jit(solution)/shard_map/all_to_all | solution.py:173
  15.0 5.5 %copy-start.1 = (f32[128,256]{1,0:T(8,128)}, f32[128,256]{1,0:T(8,128)S(1)}, u32[]{:S(2)}) copy-start(f32[128,256]{1,0:T(8,128)S(1)} %get-tuple-element.27) | copy-start | bytes 393220
  15.0 2.0 %copy-start.4 = (s32[128]{0:T(128)S(1)}, s32[128]{0:T(128)}, u32[]{:S(2)}) copy-start(s32[128]{0:T(128)} %param.10) | copy-start | bytes 1540
  15.0 2.0 %copy-start.5 = (s32[128]{0:T(128)S(1)}, s32[128]{0:T(128)}, u32[]{:S(2)}) copy-start(s32[128]{0:T(128)} %param.9) | copy-start | bytes 1540
  27.9 13.1 %all-to-all-start.1 = ((bf16[32,32,256]{2,1,0:T(8,128)(2,1)}), bf16[32,32,256]{2,1,0:T(8,128)(2,1)S(1)}, u32[]{:S(2)}, u32[]{:S(2)}) async-start(bf16[32,32,256]{2,1,0:T(8,128)(2,1)} %convolution_convert_fusion), calls=%async_computation.1 | async-start | bytes 1048576 | tf_op jit(solution)/shard_map/all_to_all | solution.py:231
  31.9 9.7 %copy-start.2 = (f32[128,256]{1,0:T(8,128)S(1)}, f32[128,256]{1,0:T(8,128)}, u32[]{:S(2)}) copy-start(f32[128,256]{1,0:T(8,128)} %copy-done.1) | copy-start | bytes 393220
  31.9 9.6 %collective-permute-start.3 = (bf16[4,32,256]{2,1,0:T(8,128)(2,1)S(1)}, bf16[4,32,256]{2,1,0:T(8,128)(2,1)S(1)}, u32[]{:S(2)}, u32[]{:S(2)}) collective-permute-start(bf16[4,32,256]{2,1,0:T(8,128)(2,1)S(1)} %bitcast.69), channel_id=1, source_target_pairs={{0,3},{1,0},{2,1},{3,2},{4,7},{5,4},{6,5},{7,6},{8,11},{9,8},{10,9... | collective-permute-start | bytes 196616 | tf_op jit(solution)/shard_map/ppermute | solution.py:212
  32.5 9.1 %collective-permute-start.4 = (bf16[4,32,256]{2,1,0:T(8,128)(2,1)S(1)}, bf16[4,32,256]{2,1,0:T(8,128)(2,1)S(1)}, u32[]{:S(2)}, u32[]{:S(2)}) collective-permute-start(bf16[4,32,256]{2,1,0:T(8,128)(2,1)S(1)} %bitcast.68), channel_id=1, source_target_pairs={{0,2},{1,3},{2,0},{3,1},{4,6},{5,7},{6,4},{7,5},{8,10},{9,11},{10,... | collective-permute-start | bytes 196616 | tf_op jit(solution)/shard_map/ppermute | solution.py:212
  34.1 7.4 %collective-permute-start.5 = (bf16[4,32,256]{2,1,0:T(8,128)(2,1)S(1)}, bf16[4,32,256]{2,1,0:T(8,128)(2,1)S(1)}, u32[]{:S(2)}, u32[]{:S(2)}) collective-permute-start(bf16[4,32,256]{2,1,0:T(8,128)(2,1)S(1)} %bitcast.67), channel_id=1, source_target_pairs={{0,1},{1,2},{2,3},{3,0},{4,5},{5,6},{6,7},{7,4},{8,9},{9,10},{10,1... | collective-permute-start | bytes 196616 | tf_op jit(solution)/shard_map/ppermute | solution.py:212

commit v10 on v9

--- a/solution.py
+++ b/solution.py
@@ -27,6 +27,10 @@
 
 def shift(count, step):
     return [(i, (i + step) % count) for i in range(count)]
+
+
+def partner(count, step):
+    return [(i, i ^ step) for i in range(count)]
 
 
 def lane_group_sum(x, group):
@@ -131,16 +135,27 @@
 
     normed, inv_rms, normed_b = normalize(tokens, proj_weight)
 
+    paired = n_sub & (n_sub - 1) == 0
+
+    def sub_to(k):
+        return partner(n_sub, k) if paired else shift(n_sub, k)
+
+    def sub_back(k):
+        return partner(n_sub, k) if paired else shift(n_sub, -k)
+
     if SUB_MODE == "perm":
         pool = jnp.concatenate(
             [normed_b]
             + [
-                normalize(lax.ppermute(tokens, "sub", shift(n_sub, k)), proj_weight)[2]
+                normalize(lax.ppermute(tokens, "sub", sub_to(k)), proj_weight)[2]
                 for k in range(1, n_sub)
             ],
             axis=0,
         )
-        first_at = ((sub_at - edge_first // img_count) % n_sub) * img_count + edge_first % img_count
+        if paired:
+            first_at = ((edge_first // img_count) ^ sub_at) * img_count + edge_first % img_count
+        else:
+            first_at = ((sub_at - edge_first // img_count) % n_sub) * img_count + edge_first % img_count
     elif SUB_MODE == "gather":
         pool = lax.all_gather(normed_b, "sub", axis=0, tiled=True)
         first_at = edge_first
@@ -210,7 +225,7 @@
         owned = pool_b[:img_count].astype(jnp.float32)
         for k in range(1, n_sub):
             owned = owned + lax.ppermute(
-                pool_b[k * img_count : (k + 1) * img_count], "sub", shift(n_sub, -k)
+                pool_b[k * img_count : (k + 1) * img_count], "sub", sub_back(k)
             ).astype(jnp.float32)
     elif SUB_MODE == "a2a":
         back = lax.all_to_all(pool_b, "sub", split_axis=0, concat_axis=0, tiled=True).astype(jnp.float32)

time: 43.2 us -> 42.7 us (0.988)
  waiting for transfers between devices: 7.92 us -> 6.55 us
  starting transfers between devices: 16.6 us -> 17.5 us
    all_to_all x1, waiting for transfers between devices: 6.71 us -> 4.67 us  [local(): lax.all_to_all(slot_b, 'grp', split_axis=0, concat_axis=0, tiled=True)]
    ppermute x6, starting transfers between devices: 9.41 us -> 10.1 us  [the longest x3 5.64 us: local(): lax.ppermute(tokens, 'sub', sub_to(k))]
    ppermute x6, waiting for transfers between devices: 0.02 us -> 0.68 us  [the longest x3 0.67 us: local(): lax.ppermute(pool_b[k * img_count:(k + 1) * img_count], 'sub', sub_back(k))]
  transfers between devices with their start and end apart: 8 -> 8, of which waited for: 2 -> 3; matrix products, arithmetic and copies ran while one was open for 20% -> 20% of each run, Pallas kernels for 8% -> 8%
where the time goes in v10:
time: 42.7 us; the launch traced here: 42.3 us
  starting transfers between devices  17.5 us (41%)
  waiting for transfers between devices  6.55 us (15%)
  Pallas kernels  6.33 us (15%)
  matrix products  5.19 us (12%)
  other arithmetic  3.71 us (9%)
  local copies, waits for them, and re-layouts  2.67 us (6%)
    ppermute x3, starting transfers between devices, local(): lax.ppermute(tokens, 'sub', sub_to(k))  5.64 us
    all_to_all x1, waiting for transfers between devices, local(): lax.all_to_all(slot_b, 'grp', split_axis=0, concat_axis=0, tiled=True)  4.67 us
    ppermute x3, starting transfers between devices, local(): lax.ppermute(pool_b[k * img_count:(k + 1) * img_count], 'sub', sub_back(k))  4.45 us
    all_to_all x1, starting transfers between devices, local(): lax.all_to_all(outgoing, 'grp', split_axis=0, concat_axis=0, tiled=True)  3.95 us
    all_to_all x1, starting transfers between devices, local(): lax.all_to_all(slot_b, 'grp', split_axis=0, concat_axis=0, tiled=True)  3.49 us
    pallas_call x1, Pallas kernels, place_grads(): pl.pallas_call(functools.partial(place_kernel, group, recv), out_shape=ja...  3.29 us
    pallas_call x1, Pallas kernels, softmax_bwd(): pl.pallas_call(functools.partial(softmax_bwd_kernel, group, score_scale),...  3.04 us
    dot_general x5, matrix products, normalize(): jnp.dot(tokens.reshape(image_count * length, feat_width), proj_weight, pr...  2.22 us
  transfers between devices with their start and end apart: 8, of which 3 were waited for; matrix products, arithmetic and copies ran while one was open for 20% of the time, Pallas kernels for 8%

profile of v10, /device:TPU:0, one launch (start us, length us, event | category | flops | bytes accessed | tf_op | source)
XLA Modules:
  0.0 42.3 jit_solution(11265073226733959211)
XLA Ops:
  0.0 3.1 %collective-permute-start = (bf16[4,32,256]{2,1,0:T(8,128)(2,1)}, bf16[4,32,256]{2,1,0:T(8,128)(2,1)S(1)}, u32[]{:S(2)}, u32[]{:S(2)}) collective-permute-start(bf16[4,32,256]{2,1,0:T(8,128)(2,1)} %param.6), channel_id=1, source_target_pairs={{0,1},{1,0},{2,3},{3,2},{4,5},{5,4},{6,7},{7,6},{8,9},{9,8},{10,11... | collective-permute-start | bytes 196616 | tf_op jit(solution)/shard_map/ppermute | solution.py:150
  3.1 2.6 %collective-permute-start.1 = (bf16[4,32,256]{2,1,0:T(8,128)(2,1)}, bf16[4,32,256]{2,1,0:T(8,128)(2,1)S(1)}, u32[]{:S(2)}, u32[]{:S(2)}) collective-permute-start(bf16[4,32,256]{2,1,0:T(8,128)(2,1)} %param.6), channel_id=1, source_target_pairs={{0,2},{1,3},{2,0},{3,1},{4,6},{5,7},{6,4},{7,5},{8,10},{9,11},{10,... | collective-permute-start | bytes 196616 | tf_op jit(solution)/shard_map/ppermute | solution.py:150
  5.7 0.8 %slice_bitcast_fusion.3 = (bf16[32,256]{1,0:T(8,128)(2,1)S(1)}, bf16[32,256]{1,0:T(8,128)(2,1)S(1)}, bf16[32,256]{1,0:T(8,128)(2,1)S(1)}, bf16[32,256]{1,0:T(8,128)(2,1)S(1)}) fusion(bf16[4,32,256]{2,1,0:T(8,128)(2,1)} %param.6), kind=kLoop, calls=%fused_computation.32 | loop fusion | bytes 131072 | tf_op jit(solution)/shard_map/squeeze | solution.py:175
  6.4 0.7 %broadcast_compare_fusion.2 = (pred[32]{0:T(512)(128)(4,1)S(1)}, pred[32]{0:T(512)(128)(4,1)S(1)}, pred[32]{0:T(512)(128)(4,1)S(1)}) fusion(s32[32]{0:T(128)} %param.11), kind=kLoop, calls=%fused_computation.47 | loop fusion | flops 96 | bytes 224 | tf_op jit(solution)/shard_map/eq | solution.py:175
  7.1 1.0 %select_select_fusion = bf16[32,32,256]{2,1,0:T(8,128)(2,1)} fusion(pred[32]{0:T(512)(128)(4,1)S(1)} %get-tuple-element.19, pred[32]{0:T(512)(128)(4,1)S(1)} %get-tuple-element.18, pred[32]{0:T(512)(128)(4,1)S(1)} %get-tuple-element.17, bf16[32,256]{1,0:T(8,128)(2,1)S(1)} %get-tuple-element.15, bf16[32,256]{1,0:T(8,128)(2,1)S(1)} %get-tuple-element.16, ...), kind=kLoop, calls=%fused_computation.7 | loop fusion | flops 786432 | bytes 589920 | tf_op jit(solution)/shard_map/jit(_where)/select_n | solution.py:175
  8.1 3.9 %all-to-all-start = ((bf16[32,32,256]{2,1,0:T(8,128)(2,1)}), bf16[32,32,256]{2,1,0:T(8,128)(2,1)S(1)}, u32[]{:S(2)}, u32[]{:S(2)}) async-start(bf16[32,32,256]{2,1,0:T(8,128)(2,1)} %select_select_fusion), calls=%async_computation | async-start | bytes 1048576 | tf_op jit(solution)/shard_map/all_to_all | solution.py:188
  12.0 0.7 %iota_compare_fusion.1 = pred[32,4]{1,0:T(8,128)(4,1)S(1)} fusion(s32[32]{0:T(128)} %param.11), kind=kLoop, calls=%fused_computation.28 | loop fusion | flops 128 | bytes 256 | tf_op jit(solution)/shard_map/eq | solution.py:247
  12.7 1.1 %multiply_reduce_fusion.4 = (f32[128]{0:T(128)S(1)}, f32[128,256]{1,0:T(8,128)S(1)}) fusion(bf16[128,256]{1,0:T(8,128)(2,1)} %bitcast.58, bf16[256,256]{1,0:T(8,128)(2,1)S(1)} %copy-done), kind=kOutput, calls=%fused_computation.26 | convolution fusion | flops 16842624 | bytes 328192 | tf_op jit(solution)/shard_map/dot_general | solution.py:18
  14.1 1.5 %copy.10 = bf16[128,32,32]{2,1,0:T(8,128)(2,1)S(1)} copy(bf16[128,32,32]{0,2,1:T(8,128)(2,1)S(1)} %bitcast.57) | data formatting | bytes 524288 | tf_op jit(solution)/shard_map/reshape | solution.py:203
  16.0 3.3 %shard_map.64.g_ref = bf16[512,1024]{1,0:T(8,128)(2,1)S(1)} custom-call(s32[512]{0:T(512)S(1)} %select_reduce_fusion.1.edge_at_ref, bf16[129,32,32]{2,1,0:T(8,128)(2,1)S(1)} %concatenate.7.m_ref), custom_call_target="tpu_custom_call" | custom-call | bytes 1312768 | tf_op jit(solution)/shard_map/pallas_call | solution.py:69
  19.3 0.3 multiply_reduce_fusion.3
  20.5 1.2 %all-to-all-done = bf16[32,32,256]{2,1,0:T(8,128)(2,1)S(1)} async-done(((bf16[32,32,256]{2,1,0:T(8,128)(2,1)}), bf16[32,32,256]{2,1,0:T(8,128)(2,1)S(1)}, u32[]{:S(2)}, u32[]{:S(2)}) %all-to-all-start) | async-done | bytes 524320 | tf_op jit(solution)/shard_map/all_to_all | solution.py:188
  21.7 0.4 multiply_reduce_fusion
  22.1 0.4 %convolution_multiply_fusion.s_ref = f32[512,1024]{1,0:T(8,128)S(1)} fusion(bf16[512,256]{1,0:T(8,128)(2,1)S(1)} %bitcast.54, f32[1024,256]{0,1:T(8,128)S(1)} %get-tuple-element.29, f32[1024]{0:T(1024)S(1)} %add_rsqrt_fusion), kind=kOutput, calls=%fused_computation.1 | convolution fusion | flops 269484032 | bytes 3411968 | tf_op jit(solution)/shard_map/dot_general | solution.py:211
  22.5 3.0 %shard_map.65 = (bf16[512,1024]{1,0:T(8,128)(2,1)S(1)}, bf16[1024,512]{1,0:T(8,128)(2,1)S(1)}) custom-call(f32[512,1024]{1,0:T(8,128)S(1)} %convolution_multiply_fusion.s_ref, bf16[512,1024]{1,0:T(8,128)(2,1)S(1)} %shard_map.64.g_ref), custom_call_target="tpu_custom_call" | custom-call | flops 15728640 | bytes 4194304 | tf_op jit(solution)/shard_map/pallas_call | solution.py:103
  25.6 1.2 %convolution_convert_fusion = bf16[32,32,256]{2,1,0:T(8,128)(2,1)} fusion(bf16[32,32,512]{2,1,0:T(8,128)(2,1)S(1)} %bitcast.53, bf16[512,256,1]{1,0,2:T(8,128)(2,1)S(1)} %bitcast.55), kind=kOutput, calls=%fused_computation.2 | convolution fusion | flops 268697600 | bytes 1835008 | tf_op jit(solution)/shard_map/dot_general | solution.py:218
  26.8 3.5 %all-to-all-start.1 = ((bf16[32,32,256]{2,1,0:T(8,128)(2,1)}), bf16[32,32,256]{2,1,0:T(8,128)(2,1)S(1)}, u32[]{:S(2)}, u32[]{:S(2)}) async-start(bf16[32,32,256]{2,1,0:T(8,128)(2,1)} %convolution_convert_fusion), calls=%async_computation.1 | async-start | bytes 1048576 | tf_op jit(solution)/shard_map/all_to_all | solution.py:246
  30.3 0.5 %convolution_convert_fusion.1 = bf16[512,256]{1,0:T(8,128)(2,1)S(1)} fusion(bf16[512,1024]{1,0:T(8,128)(2,1)S(1)} %get-tuple-element.7, f32[1024,256]{0,1:T(8,128)S(1)} %get-tuple-element.29, f32[1024]{0:T(1024)S(1)} %add_rsqrt_fusion), kind=kOutput, calls=%fused_computation.3 | convolution fusion | flops 269090816 | bytes 2363392 | tf_op jit(solution)/shard_map/dot_general | solution.py:215
  30.8 0.8 %collective-permute-start.3 = (bf16[4,32,256]{2,1,0:T(8,128)(2,1)S(1)}, bf16[4,32,256]{2,1,0:T(8,128)(2,1)S(1)}, u32[]{:S(2)}, u32[]{:S(2)}) collective-permute-start(bf16[4,32,256]{2,1,0:T(8,128)(2,1)S(1)} %bitcast.69), channel_id=1, source_target_pairs={{0,1},{1,0},{2,3},{3,2},{4,5},{5,4},{6,7},{7,6},{8,9},{9,8},{10,11... | collective-permute-start | bytes 196616 | tf_op jit(solution)/shard_map/ppermute | solution.py:227
  31.6 3.5 %collective-permute-start.4 = (bf16[4,32,256]{2,1,0:T(8,128)(2,1)S(1)}, bf16[4,32,256]{2,1,0:T(8,128)(2,1)S(1)}, u32[]{:S(2)}, u32[]{:S(2)}) collective-permute-start(bf16[4,32,256]{2,1,0:T(8,128)(2,1)S(1)} %bitcast.68), channel_id=1, source_target_pairs={{0,2},{1,3},{2,0},{3,1},{4,6},{5,7},{6,4},{7,5},{8,10},{9,11},{10,... | collective-permute-start | bytes 196616 | tf_op jit(solution)/shard_map/ppermute | solution.py:227
  35.3 4.7 %all-to-all-done.1 = bf16[32,32,256]{2,1,0:T(8,128)(2,1)S(1)} async-done(((bf16[32,32,256]{2,1,0:T(8,128)(2,1)}), bf16[32,32,256]{2,1,0:T(8,128)(2,1)S(1)}, u32[]{:S(2)}, u32[]{:S(2)}) %all-to-all-start.1) | async-done | bytes 524320 | tf_op jit(solution)/shard_map/all_to_all | solution.py:246
  40.1 0.4 select_reduce_fusion
  40.4 0.7 %collective-permute-done.5 = bf16[4,32,256]{2,1,0:T(8,128)(2,1)S(1)} collective-permute-done((bf16[4,32,256]{2,1,0:T(8,128)(2,1)S(1)}, bf16[4,32,256]{2,1,0:T(8,128)(2,1)S(1)}, u32[]{:S(2)}, u32[]{:S(2)}) %collective-permute-start.5) | collective-permute-done | bytes 65568 | tf_op jit(solution)/shard_map/ppermute | solution.py:227
  41.5 0.8 %convolution_convert_fusion.2 = bf16[128,256]{1,0:T(8,128)(2,1)} fusion(bf16[128,256]{1,0:T(8,128)(2,1)S(1)} %fusion.5, bf16[256,256]{1,0:T(8,128)(2,1)S(1)} %copy-done), kind=kOutput, calls=%fused_computation.4 | convolution fusion | flops 16809984 | bytes 262144 | tf_op jit(solution)/shard_map/nk,dk->nd/dot_general | solution.py:259
  (41 shorter events, 2.2 us)
Async XLA Ops:
  0.0 12.7 %copy-start = (bf16[256,256]{1,0:T(8,128)(2,1)S(1)}, bf16[256,256]{1,0:T(8,128)(2,1)}, u32[]{:S(2)}) copy-start(bf16[256,256]{1,0:T(8,128)(2,1)} %param.7) | copy-start | bytes 393220
  0.0 13.9 %copy-start.3 = (bf16[128,1024]{1,0:T(8,128)(2,1)S(1)}, bf16[128,1024]{1,0:T(8,128)(2,1)}, u32[]{:S(2)}) copy-start(bf16[128,1024]{1,0:T(8,128)(2,1)} %param.8) | copy-start | bytes 786436
  0.0 19.3 %collective-permute-start = (bf16[4,32,256]{2,1,0:T(8,128)(2,1)}, bf16[4,32,256]{2,1,0:T(8,128)(2,1)S(1)}, u32[]{:S(2)}, u32[]{:S(2)}) collective-permute-start(bf16[4,32,256]{2,1,0:T(8,128)(2,1)} %param.6), channel_id=1, source_target_pairs={{0,1},{1,0},{2,3},{3,2},{4,5},{5,4},{6,7},{7,6},{8,9},{9,8},{10,11... | collective-permute-start | bytes 196616 | tf_op jit(solution)/shard_map/ppermute | solution.py:150
  3.1 16.6 %collective-permute-start.1 = (bf16[4,32,256]{2,1,0:T(8,128)(2,1)}, bf16[4,32,256]{2,1,0:T(8,128)(2,1)S(1)}, u32[]{:S(2)}, u32[]{:S(2)}) collective-permute-start(bf16[4,32,256]{2,1,0:T(8,128)(2,1)} %param.6), channel_id=1, source_target_pairs={{0,2},{1,3},{2,0},{3,1},{4,6},{5,7},{6,4},{7,5},{8,10},{9,11},{10,... | collective-permute-start | bytes 196616 | tf_op jit(solution)/shard_map/ppermute | solution.py:150
  5.6 14.3 %collective-permute-start.2 = (bf16[4,32,256]{2,1,0:T(8,128)(2,1)}, bf16[4,32,256]{2,1,0:T(8,128)(2,1)S(1)}, u32[]{:S(2)}, u32[]{:S(2)}) collective-permute-start(bf16[4,32,256]{2,1,0:T(8,128)(2,1)} %param.6), channel_id=1, source_target_pairs={{0,3},{1,2},{2,1},{3,0},{4,7},{5,6},{6,5},{7,4},{8,11},{9,10},{10,... | collective-permute-start | bytes 196616 | tf_op jit(solution)/shard_map/ppermute | solution.py:150
  8.1 13.7 %all-to-all-start = ((bf16[32,32,256]{2,1,0:T(8,128)(2,1)}), bf16[32,32,256]{2,1,0:T(8,128)(2,1)S(1)}, u32[]{:S(2)}, u32[]{:S(2)}) async-start(bf16[32,32,256]{2,1,0:T(8,128)(2,1)} %select_select_fusion), calls=%async_computation | async-start | bytes 1048576 | tf_op jit(solution)/shard_map/all_to_all | solution.py:188
  13.8 5.5 %copy-start.1 = (f32[128,256]{1,0:T(8,128)}, f32[128,256]{1,0:T(8,128)S(1)}, u32[]{:S(2)}) copy-start(f32[128,256]{1,0:T(8,128)S(1)} %get-tuple-element.27) | copy-start | bytes 393220
  13.8 2.0 %copy-start.4 = (s32[128]{0:T(128)S(1)}, s32[128]{0:T(128)}, u32[]{:S(2)}) copy-start(s32[128]{0:T(128)} %param.10) | copy-start | bytes 1540
  13.9 2.0 %copy-start.5 = (s32[128]{0:T(128)S(1)}, s32[128]{0:T(128)}, u32[]{:S(2)}) copy-start(s32[128]{0:T(128)} %param.9) | copy-start | bytes 1540
  26.8 13.1 %all-to-all-start.1 = ((bf16[32,32,256]{2,1,0:T(8,128)(2,1)}), bf16[32,32,256]{2,1,0:T(8,128)(2,1)S(1)}, u32[]{:S(2)}, u32[]{:S(2)}) async-start(bf16[32,32,256]{2,1,0:T(8,128)(2,1)} %convolution_convert_fusion), calls=%async_computation.1 | async-start | bytes 1048576 | tf_op jit(solution)/shard_map/all_to_all | solution.py:246
  30.8 10.4 %copy-start.2 = (f32[128,256]{1,0:T(8,128)S(1)}, f32[128,256]{1,0:T(8,128)}, u32[]{:S(2)}) copy-start(f32[128,256]{1,0:T(8,128)} %copy-done.1) | copy-start | bytes 393220
  30.8 9.6 %collective-permute-start.3 = (bf16[4,32,256]{2,1,0:T(8,128)(2,1)S(1)}, bf16[4,32,256]{2,1,0:T(8,128)(2,1)S(1)}, u32[]{:S(2)}, u32[]{:S(2)}) collective-permute-start(bf16[4,32,256]{2,1,0:T(8,128)(2,1)S(1)} %bitcast.69), channel_id=1, source_target_pairs={{0,1},{1,0},{2,3},{3,2},{4,5},{5,4},{6,7},{7,6},{8,9},{9,8},{10,11... | collective-permute-start | bytes 196616 | tf_op jit(solution)/shard_map/ppermute | solution.py:227
  31.6 8.9 %collective-permute-start.4 = (bf16[4,32,256]{2,1,0:T(8,128)(2,1)S(1)}, bf16[4,32,256]{2,1,0:T(8,128)(2,1)S(1)}, u32[]{:S(2)}, u32[]{:S(2)}) collective-permute-start(bf16[4,32,256]{2,1,0:T(8,128)(2,1)S(1)} %bitcast.68), channel_id=1, source_target_pairs={{0,2},{1,3},{2,0},{3,1},{4,6},{5,7},{6,4},{7,5},{8,10},{9,11},{10,... | collective-permute-start | bytes 196616 | tf_op jit(solution)/shard_map/ppermute | solution.py:227
  35.0 6.1 %collective-permute-start.5 = (bf16[4,32,256]{2,1,0:T(8,128)(2,1)S(1)}, bf16[4,32,256]{2,1,0:T(8,128)(2,1)S(1)}, u32[]{:S(2)}, u32[]{:S(2)}) collective-permute-start(bf16[4,32,256]{2,1,0:T(8,128)(2,1)S(1)} %bitcast.67), channel_id=1, source_target_pairs={{0,3},{1,2},{2,1},{3,0},{4,7},{5,6},{6,5},{7,4},{8,11},{9,10},{10,... | collective-permute-start | bytes 196616 | tf_op jit(solution)/shard_map/ppermute | solution.py:227

commit v11 on v10

--- a/solution.py
+++ b/solution.py
@@ -170,9 +170,10 @@
         order = picks[(grp_at + jnp.arange(n_grp, dtype=jnp.int32)) % n_grp].reshape(recv)
     else:
         order = send_pick
-    outgoing = jnp.broadcast_to(tokens[img_count - 1], (recv, length, feat_width))
-    for image in range(img_count - 2, -1, -1):
-        outgoing = jnp.where(order[:, None, None] == image, tokens[image], outgoing)
+    chosen = order[:, None, None, None] == jnp.arange(img_count, dtype=jnp.int32)[None, :, None, None]
+    outgoing = jnp.sum(
+        jnp.where(chosen, tokens[None], jnp.zeros((), tokens.dtype)), axis=1
+    ).astype(tokens.dtype)
     if GRP_MODE == "perm":
         received = jnp.concatenate(
             [outgoing[:slots]]

time: 42.7 us -> 42.4 us (level)
  local copies, waits for them, and re-layouts: 2.67 us -> 1.88 us
  other arithmetic: 3.71 us -> 4.15 us
    reduce_sum x0 -> x1, other arithmetic: none -> 2.06 us  [local(): jnp.sum(jnp.where(chosen, tokens[None], jnp.zeros((), tokens.dtype)), axi...]
    select_n x1 -> x0, other arithmetic: 0.96 us -> none  [local(): outgoing = jnp.where(order[:, None, None] == image, tokens[image], outgoing)]
    squeeze x1 -> x0, local copies, waits for them, and re-layouts: 0.79 us -> none  [local(): outgoing = jnp.where(order[:, None, None] == image, tokens[image], outgoing)]
    all_to_all x1, waiting for transfers between devices: 1.19 us -> 1.92 us  [local(): lax.all_to_all(outgoing, 'grp', split_axis=0, concat_axis=0, tiled=True)]
    ppermute x3, waiting for transfers between devices: 0.67 us -> 0.01 us  [local(): lax.ppermute(pool_b[k * img_count:(k + 1) * img_count], 'sub', sub_back(k))]
    eq x1 -> x0, other arithmetic: 0.66 us -> none  [local(): outgoing = jnp.where(order[:, None, None] == image, tokens[image], outgoing)]
  transfers between devices with their start and end apart: 8 -> 8, of which waited for: 3 -> 2; matrix products, arithmetic and copies ran while one was open for 20% -> 19% of each run, Pallas kernels for 8% -> 8%
where the time goes in v11:
time: 42.4 us; the launch traced here: 42 us
  starting transfers between devices  17.5 us (41%)
  waiting for transfers between devices  6.6 us (16%)
  Pallas kernels  6.33 us (15%)
  matrix products  5.2 us (12%)
  other arithmetic  4.15 us (10%)
  local copies, waits for them, and re-layouts  1.88 us (4%)
    ppermute x3, starting transfers between devices, local(): lax.ppermute(tokens, 'sub', sub_to(k))  5.64 us
    all_to_all x1, waiting for transfers between devices, local(): lax.all_to_all(slot_b, 'grp', split_axis=0, concat_axis=0, tiled=True)  4.66 us
    ppermute x3, starting transfers between devices, local(): lax.ppermute(pool_b[k * img_count:(k + 1) * img_count], 'sub', sub_back(k))  4.45 us
    all_to_all x1, starting transfers between devices, local(): lax.all_to_all(outgoing, 'grp', split_axis=0, concat_axis=0, tiled=True)  3.94 us
    all_to_all x1, starting transfers between devices, local(): lax.all_to_all(slot_b, 'grp', split_axis=0, concat_axis=0, tiled=True)  3.49 us
    pallas_call x1, Pallas kernels, place_grads(): pl.pallas_call(functools.partial(place_kernel, group, recv), out_shape=ja...  3.29 us
    pallas_call x1, Pallas kernels, softmax_bwd(): pl.pallas_call(functools.partial(softmax_bwd_kernel, group, score_scale),...  3.04 us
    dot_general x5, matrix products, normalize(): jnp.dot(tokens.reshape(image_count * length, feat_width), proj_weight, pr...  2.22 us
  transfers between devices with their start and end apart: 8, of which 2 were waited for; matrix products, arithmetic and copies ran while one was open for 19% of the time, Pallas kernels for 8%

profile of v11, /device:TPU:0, one launch (start us, length us, event | category | flops | bytes accessed | tf_op | source)
XLA Modules:
  0.0 42.0 jit_solution(7654552599011082062)
XLA Ops:
  0.0 4.1 %collective-permute-start.1 = (bf16[4,32,256]{2,1,0:T(8,128)(2,1)}, bf16[4,32,256]{2,1,0:T(8,128)(2,1)S(1)}, u32[]{:S(2)}, u32[]{:S(2)}) collective-permute-start(bf16[4,32,256]{2,1,0:T(8,128)(2,1)} %param.6), channel_id=1, source_target_pairs={{0,2},{1,3},{2,0},{3,1},{4,6},{5,7},{6,4},{7,5},{8,10},{9,11},{10,... | collective-permute-start | bytes 196616 | tf_op jit(solution)/shard_map/ppermute | solution.py:150
  4.1 1.6 %collective-permute-start = (bf16[4,32,256]{2,1,0:T(8,128)(2,1)}, bf16[4,32,256]{2,1,0:T(8,128)(2,1)S(1)}, u32[]{:S(2)}, u32[]{:S(2)}) collective-permute-start(bf16[4,32,256]{2,1,0:T(8,128)(2,1)} %param.6), channel_id=1, source_target_pairs={{0,1},{1,0},{2,3},{3,2},{4,5},{5,4},{6,7},{7,6},{8,9},{9,8},{10,11... | collective-permute-start | bytes 196616 | tf_op jit(solution)/shard_map/ppermute | solution.py:150
  5.7 0.7 %iota_compare_fusion.1 = pred[32,4]{1,0:T(8,128)(4,1)S(1)} fusion(s32[32]{0:T(128)} %param.11), kind=kLoop, calls=%fused_computation.28 | loop fusion | flops 128 | bytes 256 | tf_op jit(solution)/shard_map/eq | solution.py:173
  6.4 2.1 %select_reduce_fusion.1 = bf16[32,32,256]{2,1,0:T(8,128)(2,1)} fusion(pred[32,4]{1,0:T(8,128)(4,1)S(1)} %iota_compare_fusion.1, bf16[4,32,256]{2,1,0:T(8,128)(2,1)} %param.6), kind=kLoop, calls=%fused_computation.1 | loop fusion | flops 1835008 | bytes 589952 | tf_op jit(solution)/shard_map/reduce_sum | solution.py:174
  8.4 3.9 %all-to-all-start = ((bf16[32,32,256]{2,1,0:T(8,128)(2,1)}), bf16[32,32,256]{2,1,0:T(8,128)(2,1)S(1)}, u32[]{:S(2)}, u32[]{:S(2)}) async-start(bf16[32,32,256]{2,1,0:T(8,128)(2,1)} %select_reduce_fusion.1), calls=%async_computation | async-start | bytes 1048576 | tf_op jit(solution)/shard_map/all_to_all | solution.py:189
  12.4 1.1 %multiply_reduce_fusion.4 = (f32[128]{0:T(128)S(1)}, f32[128,256]{1,0:T(8,128)S(1)}) fusion(bf16[128,256]{1,0:T(8,128)(2,1)} %bitcast.50, bf16[256,256]{1,0:T(8,128)(2,1)S(1)} %copy-done), kind=kOutput, calls=%fused_computation.26 | convolution fusion | flops 16842624 | bytes 328192 | tf_op jit(solution)/shard_map/dot_general | solution.py:18
  13.7 1.5 %copy.10 = bf16[128,32,32]{2,1,0:T(8,128)(2,1)S(1)} copy(bf16[128,32,32]{0,2,1:T(8,128)(2,1)S(1)} %bitcast.49) | data formatting | bytes 524288 | tf_op jit(solution)/shard_map/reshape | solution.py:204
  15.3 0.2 concatenate.7.m_ref
  15.7 3.3 %shard_map.64.g_ref = bf16[512,1024]{1,0:T(8,128)(2,1)S(1)} custom-call(s32[512]{0:T(512)S(1)} %select_reduce_fusion.2.edge_at_ref, bf16[129,32,32]{2,1,0:T(8,128)(2,1)S(1)} %concatenate.7.m_ref), custom_call_target="tpu_custom_call" | custom-call | bytes 1312768 | tf_op jit(solution)/shard_map/pallas_call | solution.py:69
  19.0 0.3 multiply_reduce_fusion.2
  19.3 0.3 multiply_reduce_fusion.3
  19.6 0.3 multiply_reduce_fusion.1
  20.2 1.9 %all-to-all-done = bf16[32,32,256]{2,1,0:T(8,128)(2,1)S(1)} async-done(((bf16[32,32,256]{2,1,0:T(8,128)(2,1)}), bf16[32,32,256]{2,1,0:T(8,128)(2,1)S(1)}, u32[]{:S(2)}, u32[]{:S(2)}) %all-to-all-start) | async-done | bytes 524320 | tf_op jit(solution)/shard_map/all_to_all | solution.py:189
  22.1 0.4 multiply_reduce_fusion
  22.5 0.4 %convolution_multiply_fusion.s_ref = f32[512,1024]{1,0:T(8,128)S(1)} fusion(bf16[512,256]{1,0:T(8,128)(2,1)S(1)} %bitcast.46, f32[1024,256]{0,1:T(8,128)S(1)} %get-tuple-element.22, f32[1024]{0:T(1024)S(1)} %add_rsqrt_fusion), kind=kOutput, calls=%fused_computation.2 | convolution fusion | flops 269484032 | bytes 3411968 | tf_op jit(solution)/shard_map/dot_general | solution.py:212
  22.9 3.0 %shard_map.65 = (bf16[512,1024]{1,0:T(8,128)(2,1)S(1)}, bf16[1024,512]{1,0:T(8,128)(2,1)S(1)}) custom-call(f32[512,1024]{1,0:T(8,128)S(1)} %convolution_multiply_fusion.s_ref, bf16[512,1024]{1,0:T(8,128)(2,1)S(1)} %shard_map.64.g_ref), custom_call_target="tpu_custom_call" | custom-call | flops 15728640 | bytes 4194304 | tf_op jit(solution)/shard_map/pallas_call | solution.py:103
  26.0 1.2 %convolution_convert_fusion = bf16[32,32,256]{2,1,0:T(8,128)(2,1)} fusion(bf16[32,32,512]{2,1,0:T(8,128)(2,1)S(1)} %bitcast.45, bf16[512,256,1]{1,0,2:T(8,128)(2,1)S(1)} %bitcast.47), kind=kOutput, calls=%fused_computation.3 | convolution fusion | flops 268697600 | bytes 1835008 | tf_op jit(solution)/shard_map/dot_general | solution.py:219
  27.2 3.5 %all-to-all-start.1 = ((bf16[32,32,256]{2,1,0:T(8,128)(2,1)}), bf16[32,32,256]{2,1,0:T(8,128)(2,1)S(1)}, u32[]{:S(2)}, u32[]{:S(2)}) async-start(bf16[32,32,256]{2,1,0:T(8,128)(2,1)} %convolution_convert_fusion), calls=%async_computation.1 | async-start | bytes 1048576 | tf_op jit(solution)/shard_map/all_to_all | solution.py:247
  30.7 0.5 %convolution_convert_fusion.1 = bf16[512,256]{1,0:T(8,128)(2,1)S(1)} fusion(bf16[512,1024]{1,0:T(8,128)(2,1)S(1)} %get-tuple-element.7, f32[1024,256]{0,1:T(8,128)S(1)} %get-tuple-element.22, f32[1024]{0:T(1024)S(1)} %add_rsqrt_fusion), kind=kOutput, calls=%fused_computation.4 | convolution fusion | flops 269090816 | bytes 2363392 | tf_op jit(solution)/shard_map/dot_general | solution.py:216
  31.2 3.6 %collective-permute-start.5 = (bf16[4,32,256]{2,1,0:T(8,128)(2,1)S(1)}, bf16[4,32,256]{2,1,0:T(8,128)(2,1)S(1)}, u32[]{:S(2)}, u32[]{:S(2)}) collective-permute-start(bf16[4,32,256]{2,1,0:T(8,128)(2,1)S(1)} %bitcast.61), channel_id=1, source_target_pairs={{0,3},{1,2},{2,1},{3,0},{4,7},{5,6},{6,5},{7,4},{8,11},{9,10},{10,... | collective-permute-start | bytes 196616 | tf_op jit(solution)/shard_map/ppermute | solution.py:228
  34.9 0.8 %collective-permute-start.4 = (bf16[4,32,256]{2,1,0:T(8,128)(2,1)S(1)}, bf16[4,32,256]{2,1,0:T(8,128)(2,1)S(1)}, u32[]{:S(2)}, u32[]{:S(2)}) collective-permute-start(bf16[4,32,256]{2,1,0:T(8,128)(2,1)S(1)} %bitcast.59), channel_id=1, source_target_pairs={{0,2},{1,3},{2,0},{3,1},{4,6},{5,7},{6,4},{7,5},{8,10},{9,11},{10,... | collective-permute-start | bytes 196616 | tf_op jit(solution)/shard_map/ppermute | solution.py:228
  35.7 4.7 %all-to-all-done.1 = bf16[32,32,256]{2,1,0:T(8,128)(2,1)S(1)} async-done(((bf16[32,32,256]{2,1,0:T(8,128)(2,1)}), bf16[32,32,256]{2,1,0:T(8,128)(2,1)S(1)}, u32[]{:S(2)}, u32[]{:S(2)}) %all-to-all-start.1) | async-done | bytes 524320 | tf_op jit(solution)/shard_map/all_to_all | solution.py:247
  40.5 0.4 select_reduce_fusion
  41.2 0.8 %convolution_convert_fusion.2 = bf16[128,256]{1,0:T(8,128)(2,1)} fusion(bf16[128,256]{1,0:T(8,128)(2,1)S(1)} %fusion.5, bf16[256,256]{1,0:T(8,128)(2,1)S(1)} %copy-done), kind=kOutput, calls=%fused_computation.5 | convolution fusion | flops 16809984 | bytes 262144 | tf_op jit(solution)/shard_map/nk,dk->nd/dot_general | solution.py:260
  (39 shorter events, 1.2 us)
Async XLA Ops:
  0.0 12.4 %copy-start = (bf16[256,256]{1,0:T(8,128)(2,1)S(1)}, bf16[256,256]{1,0:T(8,128)(2,1)}, u32[]{:S(2)}) copy-start(bf16[256,256]{1,0:T(8,128)(2,1)} %param.7) | copy-start | bytes 393220
  0.0 13.5 %copy-start.3 = (bf16[128,1024]{1,0:T(8,128)(2,1)S(1)}, bf16[128,1024]{1,0:T(8,128)(2,1)}, u32[]{:S(2)}) copy-start(bf16[128,1024]{1,0:T(8,128)(2,1)} %param.8) | copy-start | bytes 786436
  0.0 19.0 %collective-permute-start.1 = (bf16[4,32,256]{2,1,0:T(8,128)(2,1)}, bf16[4,32,256]{2,1,0:T(8,128)(2,1)S(1)}, u32[]{:S(2)}, u32[]{:S(2)}) collective-permute-start(bf16[4,32,256]{2,1,0:T(8,128)(2,1)} %param.6), channel_id=1, source_target_pairs={{0,2},{1,3},{2,0},{3,1},{4,6},{5,7},{6,4},{7,5},{8,10},{9,11},{10,... | collective-permute-start | bytes 196616 | tf_op jit(solution)/shard_map/ppermute | solution.py:150
  4.1 15.2 %collective-permute-start = (bf16[4,32,256]{2,1,0:T(8,128)(2,1)}, bf16[4,32,256]{2,1,0:T(8,128)(2,1)S(1)}, u32[]{:S(2)}, u32[]{:S(2)}) collective-permute-start(bf16[4,32,256]{2,1,0:T(8,128)(2,1)} %param.6), channel_id=1, source_target_pairs={{0,1},{1,0},{2,3},{3,2},{4,5},{5,4},{6,7},{7,6},{8,9},{9,8},{10,11... | collective-permute-start | bytes 196616 | tf_op jit(solution)/shard_map/ppermute | solution.py:150
  5.6 13.9 %collective-permute-start.2 = (bf16[4,32,256]{2,1,0:T(8,128)(2,1)}, bf16[4,32,256]{2,1,0:T(8,128)(2,1)S(1)}, u32[]{:S(2)}, u32[]{:S(2)}) collective-permute-start(bf16[4,32,256]{2,1,0:T(8,128)(2,1)} %param.6), channel_id=1, source_target_pairs={{0,3},{1,2},{2,1},{3,0},{4,7},{5,6},{6,5},{7,4},{8,11},{9,10},{10,... | collective-permute-start | bytes 196616 | tf_op jit(solution)/shard_map/ppermute | solution.py:150
  8.4 13.7 %all-to-all-start = ((bf16[32,32,256]{2,1,0:T(8,128)(2,1)}), bf16[32,32,256]{2,1,0:T(8,128)(2,1)S(1)}, u32[]{:S(2)}, u32[]{:S(2)}) async-start(bf16[32,32,256]{2,1,0:T(8,128)(2,1)} %select_reduce_fusion.1), calls=%async_computation | async-start | bytes 1048576 | tf_op jit(solution)/shard_map/all_to_all | solution.py:189
  13.5 5.5 %copy-start.1 = (f32[128,256]{1,0:T(8,128)}, f32[128,256]{1,0:T(8,128)S(1)}, u32[]{:S(2)}) copy-start(f32[128,256]{1,0:T(8,128)S(1)} %get-tuple-element.20) | copy-start | bytes 393220
  13.5 2.0 %copy-start.4 = (s32[128]{0:T(128)S(1)}, s32[128]{0:T(128)}, u32[]{:S(2)}) copy-start(s32[128]{0:T(128)} %param.10) | copy-start | bytes 1540
  13.5 2.0 %copy-start.5 = (s32[128]{0:T(128)S(1)}, s32[128]{0:T(128)}, u32[]{:S(2)}) copy-start(s32[128]{0:T(128)} %param.9) | copy-start | bytes 1540
  27.2 13.1 %all-to-all-start.1 = ((bf16[32,32,256]{2,1,0:T(8,128)(2,1)}), bf16[32,32,256]{2,1,0:T(8,128)(2,1)S(1)}, u32[]{:S(2)}, u32[]{:S(2)}) async-start(bf16[32,32,256]{2,1,0:T(8,128)(2,1)} %convolution_convert_fusion), calls=%async_computation.1 | async-start | bytes 1048576 | tf_op jit(solution)/shard_map/all_to_all | solution.py:247
  31.2 9.7 %copy-start.2 = (f32[128,256]{1,0:T(8,128)S(1)}, f32[128,256]{1,0:T(8,128)}, u32[]{:S(2)}) copy-start(f32[128,256]{1,0:T(8,128)} %copy-done.1) | copy-start | bytes 393220
  31.2 9.6 %collective-permute-start.5 = (bf16[4,32,256]{2,1,0:T(8,128)(2,1)S(1)}, bf16[4,32,256]{2,1,0:T(8,128)(2,1)S(1)}, u32[]{:S(2)}, u32[]{:S(2)}) collective-permute-start(bf16[4,32,256]{2,1,0:T(8,128)(2,1)S(1)} %bitcast.61), channel_id=1, source_target_pairs={{0,3},{1,2},{2,1},{3,0},{4,7},{5,6},{6,5},{7,4},{8,11},{9,10},{10,... | collective-permute-start | bytes 196616 | tf_op jit(solution)/shard_map/ppermute | solution.py:228
  34.9 6.0 %collective-permute-start.3 = (bf16[4,32,256]{2,1,0:T(8,128)(2,1)S(1)}, bf16[4,32,256]{2,1,0:T(8,128)(2,1)S(1)}, u32[]{:S(2)}, u32[]{:S(2)}) collective-permute-start(bf16[4,32,256]{2,1,0:T(8,128)(2,1)S(1)} %bitcast.60), channel_id=1, source_target_pairs={{0,1},{1,0},{2,3},{3,2},{4,5},{5,4},{6,7},{7,6},{8,9},{9,8},{10,11... | collective-permute-start | bytes 196616 | tf_op jit(solution)/shard_map/ppermute | solution.py:228
  34.9 6.0 %collective-permute-start.4 = (bf16[4,32,256]{2,1,0:T(8,128)(2,1)S(1)}, bf16[4,32,256]{2,1,0:T(8,128)(2,1)S(1)}, u32[]{:S(2)}, u32[]{:S(2)}) collective-permute-start(bf16[4,32,256]{2,1,0:T(8,128)(2,1)S(1)} %bitcast.59), channel_id=1, source_target_pairs={{0,2},{1,3},{2,0},{3,1},{4,6},{5,7},{6,4},{7,5},{8,10},{9,11},{10,... | collective-permute-start | bytes 196616 | tf_op jit(solution)/shard_map/ppermute | solution.py:228
